TPU v7x, 32 devices: a whole 2x2x4 slice. The times are simulated.
32 devices in a mesh: groups: 2 (over x), blk: 16 (over z, y, core).
Axes of the slice: x: 2, y: 2, z: 4, core: 2. Of those that a mesh axis runs over, the one named last changes fastest.
Arguments:
- contacts: float32 [512, 6144], P(('groups', 'blk')), parts along dimension 0, may hold values from 0.1 to 10
- widths: int32 [12288], P('groups'), parts along dimension 0, may hold values from 0 to 3
- masked_bins: int32 [768], P('groups'), parts along dimension 0, may hold values from 0 to 6143, as said below
- row_start: int32 [2], P('groups'), parts along dimension 0, may hold values from 0 to 5888
Outputs:
- correlation: float32 [512, 256], P(('groups', 'blk')), parts along dimension 0
There are 2 independent parts, one for each index of `groups`. A program takes and returns all parts, laid end to end along the dimension named above; each array names one. Nothing has to cross between parts.
Inputs may be any that keep to these rules, and one draw needn't show every extreme that they name: `masked_bins`: distinct bins.
All inputs are finite; a program needn't handle non-finite values.
Results may differ from a plain program's by a relative error of at most 0.00083.
Values may be sent and summed in bfloat16 or wider, within the bound.
No kernel may reach another device: no remote copies, remote signals or barrier semaphores. Data moves between devices by JAX's collectives and lax.ppermute only.
A program may use at most 64 MiB of HBM per device.

v0:
```python
import jax
import jax.numpy as jnp
from jax import lax
from jax.sharding import PartitionSpec as P

WMAX = 3


def with_halo(cells, sides, width):
    for axis, dim in sides:
        count = lax.axis_size(axis)
        ends = count - 1
        head = lax.slice_in_dim(cells, 0, width, axis=dim)
        tail = lax.slice_in_dim(cells, cells.shape[dim] - width, cells.shape[dim], axis=dim)
        cells = jnp.concatenate(
            [
                lax.ppermute(tail, axis, [(i, (i + 1) % count) for i in range(ends)]),
                cells,
                lax.ppermute(head, axis, [((i + 1) % count, i) for i in range(ends)]),
            ],
            axis=dim,
        )
    return cells


def smooth(padded, radius_map):
    rows_here = padded.shape[0] - 2 * WMAX
    col_count = padded.shape[1] - 2 * WMAX
    row_sums = padded[WMAX : WMAX + rows_here]
    smoothed = jnp.zeros((rows_here, col_count), jnp.float32)
    for radius in range(WMAX + 1):
        if radius > 0:
            row_sums = (
                row_sums
                + padded[WMAX - radius : WMAX - radius + rows_here]
                + padded[WMAX + radius : WMAX + radius + rows_here]
            )
        box_sums = row_sums[:, WMAX : WMAX + col_count]
        for offset in range(1, radius + 1):
            box_sums = (
                box_sums
                + row_sums[:, WMAX - offset : WMAX - offset + col_count]
                + row_sums[:, WMAX + offset : WMAX + offset + col_count]
            )
        smoothed = smoothed + jnp.where(
            radius_map == radius, box_sums / float((2 * radius + 1) ** 2), 0.0
        )
    return smoothed


def pair_counts(first_bin, nrows, col_count):
    distance = jnp.arange(col_count, dtype=jnp.int32)
    upper_pairs = jnp.clip(col_count - distance - first_bin, 0, nrows)
    lower_pairs = jnp.clip(first_bin + nrows - distance, 0, nrows)
    pair_total = jnp.where(distance == 0, nrows, upper_pairs + lower_pairs)
    return jnp.maximum(pair_total, 1).astype(jnp.float32)


def mirrored_table(table):
    return jnp.concatenate([table[1:][::-1], table])


def skewed_map(table, window_first, rows_here, col_count):
    span = col_count + rows_here - 1
    window = lax.dynamic_slice_in_dim(mirrored_table(table), window_first, span)
    tiled = jnp.tile(window, rows_here + 1)[: rows_here * (span + 1)]
    shifted = tiled.reshape(rows_here, span + 1)[:, :col_count]
    return shifted[::-1]


def diagonal_totals(smoothed, window_first):
    rows_here = smoothed.shape[0]
    col_count = smoothed.shape[1]
    span = col_count + rows_here - 1
    flipped = jnp.pad(smoothed[::-1], ((0, 0), (0, rows_here)))
    flat = flipped.reshape(rows_here * (col_count + rows_here))[: rows_here * span]
    offsets = jnp.sum(flat.reshape(rows_here, span), axis=0)
    spread = lax.dynamic_update_slice_in_dim(
        jnp.zeros((2 * col_count - 1,), jnp.float32), offsets, window_first, 0
    )
    lower = jnp.concatenate([jnp.zeros((1,), jnp.float32), spread[: col_count - 1][::-1]])
    return spread[col_count - 1 :] + lower


def normalize(smoothed, expected_map, kept_rows, kept_cols):
    ratio = smoothed / expected_map
    kept_total = jnp.sum(kept_cols)
    row_mean = jnp.sum(ratio * kept_cols[None, :], axis=1, keepdims=True) / kept_total
    centred = (ratio - row_mean) * kept_cols[None, :]
    variance = jnp.sum(centred * centred, axis=1, keepdims=True) / kept_total
    zscores = (centred * lax.rsqrt(variance + 1e-05) * kept_rows[:, None]).astype(jnp.bfloat16)
    return (zscores, kept_total)


def cross_block(left, right):
    return lax.dot_general(
        left, right, (((1,), (1,)), ((), ())), preferred_element_type=jnp.float32
    )


def shards(contacts, widths, masked_bins, row_start):
    blocks = lax.axis_size("blk")
    position = lax.axis_index("blk")
    rows_here = contacts.shape[0]
    col_count = contacts.shape[1]
    nbins = rows_here * blocks
    first_row = position * rows_here
    first_bin = row_start[0]
    window_first = col_count - 1 - (first_bin + first_row + rows_here - 1)
    radius_map = skewed_map(widths, window_first, rows_here, col_count)
    padded_rows = with_halo(contacts, (("blk", 0),), WMAX)
    padded = jnp.pad(padded_rows, ((0, 0), (WMAX, WMAX)))
    smoothed = smooth(padded, radius_map)
    local_total = diagonal_totals(smoothed, window_first)
    denominator = pair_counts(first_bin, nbins, col_count)
    expected = lax.psum(local_total, "blk") / denominator
    expected_map = skewed_map(expected, window_first, rows_here, col_count)
    kept_bins = jnp.ones((col_count,), jnp.float32).at[masked_bins].set(0.0)
    kept_rows = lax.dynamic_slice_in_dim(kept_bins, first_bin + first_row, rows_here)
    zscores, kept_total = normalize(smoothed, expected_map, kept_rows, kept_bins)
    return cross_block(zscores, lax.all_gather(zscores, "blk", axis=0, tiled=True)) / kept_total


def solution(mesh):
    return jax.shard_map(
        shards,
        mesh=mesh,
        in_specs=(P(("groups", "blk"), None), P("groups"), P("groups"), P("groups")),
        out_specs=P(("groups", "blk"), None),
        check_vma=False,
    )
```

profile of v0, /device:TPU:0, one launch (start us, length us, event | category | flops | bytes accessed | tf_op | source)
XLA Modules:
  0.0 145.9 jit_solution(1816043342483909816)
XLA Ops:
  6.5 0.0 copy-start
  6.5 0.0 all-gather.2.cloned.1.call-start
  6.5 1.1 fusion.14
  7.6 2.4 %collective-permute-start = (f32[3,6144]{1,0:T(4,128)S(1)}, f32[3,6144]{1,0:T(4,128)S(1)}, u32[]{:S(2)}, u32[]{:S(2)}) collective-permute-start(f32[3,6144]{1,0:T(4,128)S(1)} %get-tuple-element.10), channel_id=1, source_target_pairs={{0,1},{1,2},{2,3},{3,4},{4,5},{5,6},{6,7},{7,8},{8,9},{9,10},{10,1... | collective-permute-start | bytes 221192 | tf_op jit(solution)/shard_map/ppermute | solution.py:17
  10.1 1.3 collective-permute-start.1
  12.0 0.7 compare_select_fusion
  12.7 2.9 %scatter_custom_fusion = f32[6144]{0:T(1024)S(1)} fusion(s32[384]{0:T(512)S(1)} %compare_select_fusion, f32[384]{0:T(512)S(1)} %broadcast.30, f32[]{:T(128)} %constant.14.clone.1), kind=kCustom, calls=%fused_computation.47 | custom fusion | bytes 24580 | tf_op jit(solution)/shard_map/scatter | solution.py:118
  15.7 0.7 reduce_sum.38
  16.3 0.1 dynamic_slice.11
  16.4 0.8 slice.102
  17.2 0.1 reverse
  17.3 0.1 slice.234
  17.4 0.8 fusion.11
  18.3 0.2 tile.9
  18.5 0.2 reshape.28
  18.8 0.8 rev.19
  19.6 0.0 collective-permute-done
  19.6 0.0 collective-permute-done.1
  19.6 0.0 copy-done
  19.6 0.3 select_maximum_fusion
  20.0 0.2 slice_add_fusion
  20.2 1.5 %fusion.3 = f32[16,6144]{1,0:T(8,128)S(1)} fusion(f32[16,6150]{1,0:T(8,128)S(1)} %get-tuple-element.7, f32[16,6150]{1,0:T(8,128)S(1)} %get-tuple-element.8, f32[16,6150]{1,0:T(8,128)S(1)} %get-tuple-element.9, f32[16,6144]{1,0:T(8,128)S(1)} %copy-done, s32[16,6144]{1,0:T(8,128)S(1)} %rev.19), kind=kLoop, calls=%fused_computation.16 | loop fusion | flops 2555904 | bytes 7077888 | tf_op jit(solution)/shard_map/add | solution.py:45
  21.7 0.8 rev.20
  22.5 0.3 reshape.29
  22.8 0.3 reshape.30
  23.1 0.1 reduce_sum.36
  23.2 0.5 dynamic_update_slice.3
  23.7 0.1 reverse.1
  23.7 0.1 slice.235
  23.8 0.1 slice_add_fusion.18
  23.9 63.8 %psum.7 = f32[6144]{0:T(1024)S(1)} all-reduce(f32[6144]{0:T(1024)S(1)} %slice_add_fusion.18), channel_id=1, replica_groups=mesh['groups'=2,'blk'=16] {'blk'}, use_global_device_ids=true, to_apply=%region_1.2 | all-reduce | flops 6144 | bytes 49152 | tf_op jit(solution)/shard_map/psum | solution.py:116
  87.7 0.1 slice.162
  87.8 0.1 reverse.2
  87.9 0.1 slice.236
  88.0 0.1 fusion.10
  88.1 0.2 tile.21
  88.4 0.2 reshape.31
  88.7 0.8 rev.23
  89.5 0.2 multiply_reduce_fusion.1
  89.7 0.6 broadcast_divide_fusion
  90.3 0.3 multiply_reduce_fusion
  90.6 0.6 add_rsqrt_fusion
  91.2 0.8 multiply_convert_fusion
  92.0 0.0 all-gather.2.cloned.1.call-update
  92.0 42.8 %all-gather.2.cloned.1.call-done = bf16[256,6144]{1,0:T(8,128)(2,1)} async-done(((bf16[16,6144]{1,0:T(8,128)(2,1)}), bf16[256,6144]{1,0:T(8,128)(2,1)}) %all-gather.2.cloned.1.call-update) | async-done | bytes 3145744 | tf_op jit(solution)/shard_map/all_gather | solution.py:121
  134.8 4.2 %convolution_divide_fusion = f32[16,256]{1,0:T(8,128)} fusion(bf16[16,6144]{1,0:T(8,128)(2,1)} %multiply_convert_fusion, bf16[256,6144]{1,0:T(8,128)(2,1)} %all-gather.2.cloned.1.call-done, f32[]{:T(128)} %reduce_sum.38), kind=kOutput, calls=%fused_computation.1 | convolution fusion | flops 50335744 | bytes 3358724 | tf_op jit(solution)/shard_map/dot_general | solution.py:96
  (11 shorter events, 0.3 us)
Async XLA Ops:
  6.5 13.1 %copy-start = (f32[16,6144]{1,0:T(8,128)S(1)}, f32[16,6144]{1,0:T(8,128)}, u32[]{:S(2)}) copy-start(f32[16,6144]{1,0:T(8,128)} %param.4) | copy-start | bytes 1179652
  6.5 128.3 %all-gather.2.cloned.1.call-start = ((), (), s32[]{:S(2)}) async-start(), calls=%async_computation | async-start | bytes 3342336 | tf_op jit(solution)/shard_map/all_gather | solution.py:121
  7.6 11.9 %collective-permute-start = (f32[3,6144]{1,0:T(4,128)S(1)}, f32[3,6144]{1,0:T(4,128)S(1)}, u32[]{:S(2)}, u32[]{:S(2)}) collective-permute-start(f32[3,6144]{1,0:T(4,128)S(1)} %get-tuple-element.10), channel_id=1, source_target_pairs={{0,1},{1,2},{2,3},{3,4},{4,5},{5,6},{6,7},{7,8},{8,9},{9,10},{10,1... | collective-permute-start | bytes 221192 | tf_op jit(solution)/shard_map/ppermute | solution.py:17
  10.1 9.5 %collective-permute-start.1 = (f32[3,6144]{1,0:T(4,128)S(1)}, f32[3,6144]{1,0:T(4,128)S(1)}, u32[]{:S(2)}, u32[]{:S(2)}) collective-permute-start(f32[3,6144]{1,0:T(4,128)S(1)} %get-tuple-element.11), channel_id=1, source_target_pairs={{1,0},{2,1},{3,2},{4,3},{5,4},{6,5},{7,6},{8,7},{9,8},{10,9},{11,1... | collective-permute-start | bytes 221192 | tf_op jit(solution)/shard_map/ppermute | solution.py:19
Sparse Core Ops, SparseCore 0:
  92.2 42.6 all-gather.1
where the time goes:
time: 146 us
  blocking collectives  63.8 us (44%)
  waiting for transfers between devices  42.8 us (29%)
  between operations  14.3 us (10%)
  local copies, waits for them, and re-layouts  10 us (7%)
  other arithmetic  7.07 us (5%)
  matrix products  4.17 us (3%)
  starting transfers between devices  3.7 us (3%)
    psum x1, blocking collectives, shards(): expected = lax.psum(local_total, 'blk') / denominator  63.8 us
    all_gather x1, waiting for transfers between devices, shards(): lax.all_gather(zscores, 'blk', axis=0, tiled=True)  42.8 us
    dot_general x1, matrix products, cross_block(): lax.dot_general(left, right, (((1,), (1,)), ((), ())), preferred_element_...  4.17 us
    scatter x1, local copies, waits for them, and re-layouts, shards(): kept_bins = jnp.ones((col_count,), jnp.float32).at[masked_bins].set(0.0)  2.95 us
  transfers between devices with their start and end apart: 3, of which 1 were waited for; matrix products, arithmetic and copies ran while one was open for 5% of the time, Pallas kernels for 0%

commit v1 on v0

--- a/solution.py
+++ b/solution.py
@@ -98,6 +98,26 @@
     )
 
 
+def tree_sum(values, axis):
+    count = lax.axis_size(axis)
+    if count & (count - 1):
+        return lax.psum(values, axis)
+    step = 1
+    while step < count:
+        values = values + lax.ppermute(values, axis, [(i, i ^ step) for i in range(count)])
+        step *= 2
+    return values
+
+
+def gram_rows(zscores, axis):
+    blocks = lax.axis_size(axis)
+    rows_here = zscores.shape[0]
+    columns = lax.all_to_all(zscores, axis, 1, 0, tiled=True)
+    partial = cross_block(columns, columns)
+    pieces = lax.all_to_all(partial, axis, 0, 0, tiled=True)
+    return jnp.sum(pieces.reshape(blocks, rows_here, pieces.shape[1]), axis=0)
+
+
 def shards(contacts, widths, masked_bins, row_start):
     blocks = lax.axis_size("blk")
     position = lax.axis_index("blk")
@@ -113,12 +133,12 @@
     smoothed = smooth(padded, radius_map)
     local_total = diagonal_totals(smoothed, window_first)
     denominator = pair_counts(first_bin, nbins, col_count)
-    expected = lax.psum(local_total, "blk") / denominator
+    expected = tree_sum(local_total, "blk") / denominator
     expected_map = skewed_map(expected, window_first, rows_here, col_count)
     kept_bins = jnp.ones((col_count,), jnp.float32).at[masked_bins].set(0.0)
     kept_rows = lax.dynamic_slice_in_dim(kept_bins, first_bin + first_row, rows_here)
     zscores, kept_total = normalize(smoothed, expected_map, kept_rows, kept_bins)
-    return cross_block(zscores, lax.all_gather(zscores, "blk", axis=0, tiled=True)) / kept_total
+    return gram_rows(zscores, "blk") / kept_total
 
 
 def solution(mesh):

time: 146 us -> 62.9 us (0.43)
  blocking collectives: 63.8 us -> 25.6 us
  waiting for transfers between devices: 42.8 us -> 6.51 us
  between operations: 14.3 us -> 0.96 us
  starting transfers between devices: 3.7 us -> 13.6 us
  matrix products: 4.17 us -> 0.25 us
    psum x1 -> x0, blocking collectives: 63.8 us -> none  [shards(): expected = lax.psum(local_total, 'blk') / denominator]
    all_gather x1 -> x0, waiting for transfers between devices: 42.8 us -> none  [shards(): lax.all_gather(zscores, 'blk', axis=0, tiled=True)]
    all_to_all x0 -> x2, blocking collectives: none -> 25.6 us  [the longest x1 12.9 us: gram_rows(): columns = lax.all_to_all(zscores, axis, 1, 0, tiled=True)]
    ppermute x0 -> x4, starting transfers between devices: none -> 9.95 us  [tree_sum(): lax.ppermute(values, axis, [(i, i ^ step) for i in range(count)])]
    ppermute x0 -> x4, waiting for transfers between devices: none -> 4.91 us  [tree_sum(): lax.ppermute(values, axis, [(i, i ^ step) for i in range(count)])]
    dot_general x1, matrix products: 4.17 us -> 0.25 us  [cross_block(): lax.dot_general(left, right, (((1,), (1,)), ((), ())), preferred_element_...]
    ppermute x1, waiting for transfers between devices: 0.01 us -> 1.6 us  [with_halo(): lax.ppermute(head, axis, [((i + 1) % count, i) for i in range(ends)])]
  transfers between devices with their start and end apart: 3 -> 6, of which waited for: 1 -> 4; matrix products, arithmetic and copies ran while one was open for 5% -> 9% of each run, Pallas kernels for 0% -> 0%
where the time goes in v1:
time: 62.9 us; the launch traced here: 62.6 us
  blocking collectives  25.6 us (41%)
  starting transfers between devices  13.6 us (22%)
  local copies, waits for them, and re-layouts  9.23 us (15%)
  waiting for transfers between devices  6.51 us (10%)
  other arithmetic  6.45 us (10%)
  between operations  0.96 us (2%)
    all_to_all x1, blocking collectives, gram_rows(): columns = lax.all_to_all(zscores, axis, 1, 0, tiled=True)  12.9 us
    all_to_all x1, blocking collectives, gram_rows(): pieces = lax.all_to_all(partial, axis, 0, 0, tiled=True)  12.6 us
    ppermute x4, starting transfers between devices, tree_sum(): lax.ppermute(values, axis, [(i, i ^ step) for i in range(count)])  9.95 us
    ppermute x4, waiting for transfers between devices, tree_sum(): lax.ppermute(values, axis, [(i, i ^ step) for i in range(count)])  4.91 us
    scatter x1, local copies, waits for them, and re-layouts, shards(): kept_bins = jnp.ones((col_count,), jnp.float32).at[masked_bins].set(0.0)  2.95 us
    ppermute x1, starting transfers between devices, with_halo(): lax.ppermute(tail, axis, [(i, (i + 1) % count) for i in range(ends)])  2.4 us
    ppermute x1, waiting for transfers between devices, with_halo(): lax.ppermute(head, axis, [((i + 1) % count, i) for i in range(ends)])  1.6 us
    rev x2, local copies, waits for them, and re-layouts, skewed_map(): return shifted[::-1]  1.54 us
  transfers between devices with their start and end apart: 6, of which 4 were waited for; matrix products, arithmetic and copies ran while one was open for 9% of the time, Pallas kernels for 0%

profile of v1, /device:TPU:0, one launch (start us, length us, event | category | flops | bytes accessed | tf_op | source)
XLA Modules:
  0.0 62.6 jit_solution(8830150444654447309)
XLA Ops:
  0.0 1.1 %fusion.16 = (f32[3,6144]{1,0:T(4,128)S(1)}, f32[3,6144]{1,0:T(4,128)S(1)}) fusion(f32[16,6144]{1,0:T(8,128)} %param.4), kind=kLoop, calls=%fused_computation.55 | loop fusion | bytes 294912 | tf_op jit(solution)/shard_map/slice | solution.py:14
  1.1 2.4 %collective-permute-start = (f32[3,6144]{1,0:T(4,128)S(1)}, f32[3,6144]{1,0:T(4,128)S(1)}, u32[]{:S(2)}, u32[]{:S(2)}) collective-permute-start(f32[3,6144]{1,0:T(4,128)S(1)} %get-tuple-element.10), channel_id=1, source_target_pairs={{0,1},{1,2},{2,3},{3,4},{4,5},{5,6},{6,7},{7,8},{8,9},{9,10},{10,1... | collective-permute-start | bytes 221192 | tf_op jit(solution)/shard_map/ppermute | solution.py:17
  3.5 1.3 %collective-permute-start.1 = (f32[3,6144]{1,0:T(4,128)S(1)}, f32[3,6144]{1,0:T(4,128)S(1)}, u32[]{:S(2)}, u32[]{:S(2)}) collective-permute-start(f32[3,6144]{1,0:T(4,128)S(1)} %get-tuple-element.11), channel_id=1, source_target_pairs={{1,0},{2,1},{3,2},{4,3},{5,4},{6,5},{7,6},{8,7},{9,8},{10,9},{11,1... | collective-permute-start | bytes 221192 | tf_op jit(solution)/shard_map/ppermute | solution.py:19
  5.4 0.1 slice.102
  5.5 0.1 reverse
  5.6 0.1 slice.234
  5.7 0.1 fusion.13
  5.8 0.2 tile.9
  6.1 0.2 reshape.37
  6.4 0.8 %rev.19 = s32[16,6144]{1,0:T(8,128)S(1)} reverse(s32[16,6144]{1,0:T(8,128)S(1)} %slice.136), dimensions={0} | reverse | bytes 786432 | tf_op jit(solution)/shard_map/rev | solution.py:68
  7.2 1.6 %collective-permute-done.1 = f32[3,6144]{1,0:T(4,128)S(1)} collective-permute-done((f32[3,6144]{1,0:T(4,128)S(1)}, f32[3,6144]{1,0:T(4,128)S(1)}, u32[]{:S(2)}, u32[]{:S(2)}) %collective-permute-start.1) | collective-permute-done | bytes 73760 | tf_op jit(solution)/shard_map/ppermute | solution.py:19
  8.8 0.3 select_maximum_fusion
  9.1 0.2 slice_add_fusion
  9.4 1.5 %fusion.3 = f32[16,6144]{1,0:T(8,128)S(1)} fusion(f32[16,6150]{1,0:T(8,128)S(1)} %get-tuple-element.7, f32[16,6150]{1,0:T(8,128)S(1)} %get-tuple-element.8, f32[16,6150]{1,0:T(8,128)S(1)} %get-tuple-element.9, f32[16,6144]{1,0:T(8,128)S(1)} %copy-done, s32[16,6144]{1,0:T(8,128)S(1)} %rev.19), kind=kLoop, calls=%fused_computation.15 | loop fusion | flops 2555904 | bytes 7077888 | tf_op jit(solution)/shard_map/add | solution.py:45
  10.9 0.8 %rev.20 = f32[16,6144]{1,0:T(8,128)S(1)} reverse(f32[16,6144]{1,0:T(8,128)S(1)} %fusion.3), dimensions={0} | reverse | bytes 786432 | tf_op jit(solution)/shard_map/rev | solution.py:75
  11.7 0.3 reshape.38
  12.0 0.3 reshape.39
  12.3 0.1 reduce_sum.45
  12.3 0.5 dynamic_update_slice.3
  12.8 0.1 reverse.1
  12.9 0.1 slice.235
  13.0 0.1 slice_add_fusion.18
  13.1 3.3 %collective-permute-start.2 = (f32[6144]{0:T(1024)S(1)}, f32[6144]{0:T(1024)S(1)}, u32[]{:S(2)}, u32[]{:S(2)}) collective-permute-start(f32[6144]{0:T(1024)S(1)} %slice_add_fusion.18), channel_id=1, source_target_pairs={{0,1},{1,0},{2,3},{3,2},{4,5},{5,4},{6,7},{7,6},{8,9},{9,8},{10,11... | collective-permute-start | bytes 73736 | tf_op jit(solution)/shard_map/ppermute | solution.py:107
  16.4 0.8 %collective-permute-done.2 = f32[6144]{0:T(1024)S(1)} collective-permute-done((f32[6144]{0:T(1024)S(1)}, f32[6144]{0:T(1024)S(1)}, u32[]{:S(2)}, u32[]{:S(2)}) %collective-permute-start.2) | collective-permute-done | bytes 24608 | tf_op jit(solution)/shard_map/ppermute | solution.py:107
  17.2 2.4 %collective-permute-start.3 = (f32[6144]{0:T(1024)S(1)}, f32[6144]{0:T(1024)S(1)}, u32[]{:S(2)}, u32[]{:S(2)}) collective-permute-start(f32[6144]{0:T(1024)S(1)} %add.143), channel_id=1, source_target_pairs={{0,2},{1,3},{2,0},{3,1},{4,6},{5,7},{6,4},{7,5},{8,10},{9,11},{10,... | collective-permute-start | bytes 73736 | tf_op jit(solution)/shard_map/ppermute | solution.py:107
  19.6 1.8 %collective-permute-done.3 = f32[6144]{0:T(1024)S(1)} collective-permute-done((f32[6144]{0:T(1024)S(1)}, f32[6144]{0:T(1024)S(1)}, u32[]{:S(2)}, u32[]{:S(2)}) %collective-permute-start.3) | collective-permute-done | bytes 24608 | tf_op jit(solution)/shard_map/ppermute | solution.py:107
  21.5 1.6 %collective-permute-start.4 = (f32[6144]{0:T(1024)S(1)}, f32[6144]{0:T(1024)S(1)}, u32[]{:S(2)}, u32[]{:S(2)}) collective-permute-start(f32[6144]{0:T(1024)S(1)} %add.144), channel_id=1, source_target_pairs={{0,4},{1,5},{2,6},{3,7},{4,0},{5,1},{6,2},{7,3},{8,12},{9,13},{10,... | collective-permute-start | bytes 73736 | tf_op jit(solution)/shard_map/ppermute | solution.py:107
  23.1 2.2 %collective-permute-done.4 = f32[6144]{0:T(1024)S(1)} collective-permute-done((f32[6144]{0:T(1024)S(1)}, f32[6144]{0:T(1024)S(1)}, u32[]{:S(2)}, u32[]{:S(2)}) %collective-permute-start.4) | collective-permute-done | bytes 24608 | tf_op jit(solution)/shard_map/ppermute | solution.py:107
  25.3 2.6 %collective-permute-start.5 = (f32[6144]{0:T(1024)S(1)}, f32[6144]{0:T(1024)S(1)}, u32[]{:S(2)}, u32[]{:S(2)}) collective-permute-start(f32[6144]{0:T(1024)S(1)} %add.145), channel_id=1, source_target_pairs={{0,8},{1,9},{2,10},{3,11},{4,12},{5,13},{6,14},{7,15},{8,0},{9,1},... | collective-permute-start | bytes 73736 | tf_op jit(solution)/shard_map/ppermute | solution.py:107
  27.9 2.9 %scatter_custom_fusion = f32[6144]{0:T(1024)S(1)} fusion(s32[384]{0:T(512)S(1)} %compare_select_fusion, f32[384]{0:T(512)S(1)} %broadcast.30, f32[]{:T(128)} %constant.14.clone.1), kind=kCustom, calls=%fused_computation.49 | custom fusion | bytes 24580 | tf_op jit(solution)/shard_map/scatter | solution.py:138
  30.9 0.7 %reduce_sum.47 = f32[]{:T(128)} reduce(f32[6144]{0:T(1024)S(1)} %scatter_custom_fusion, f32[]{:T(128)} %constant.24.clone.1), dimensions={0}, to_apply=%region_3.4 | reduce | flops 6143 | bytes 24584 | tf_op jit(solution)/shard_map/reduce_sum | solution.py:87
  31.6 0.1 dynamic_slice.11
  31.7 0.1 slice.162
  31.8 0.1 reverse.2
  31.9 0.1 slice.236
  31.9 0.1 fusion.12
  32.1 0.2 tile.21
  32.4 0.2 reshape.40
  32.6 0.8 %rev.23 = f32[16,6144]{1,0:T(8,128)S(1)} reverse(f32[16,6144]{1,0:T(8,128)S(1)} %slice.164), dimensions={0} | reverse | bytes 786432 | tf_op jit(solution)/shard_map/rev | solution.py:68
  33.4 0.2 multiply_reduce_fusion.1
  33.6 0.7 %broadcast_divide_fusion.1 = f32[16]{0:T(128)S(1)} fusion(f32[16]{0:T(128)S(1)} %get-tuple-element.5, f32[]{:T(128)} %reduce_sum.47), kind=kLoop, calls=%fused_computation.54 | loop fusion | flops 16 | bytes 132 | tf_op jit(solution)/shard_map/div | solution.py:88
  34.3 0.3 multiply_reduce_fusion
  34.6 0.7 %add_rsqrt_fusion = f32[16]{0:T(128)S(1)} fusion(f32[16]{0:T(128)S(1)} %multiply_reduce_fusion, f32[]{:T(128)} %reduce_sum.47), kind=kLoop, calls=%fused_computation.53 | loop fusion | flops 32 | bytes 132 | tf_op jit(solution)/shard_map/rsqrt | solution.py:91
  35.3 0.1 multiply_convert_fusion
  35.5 12.9 %all_to_all.25 = bf16[16,16,384]{2,0,1:T(8,128)(2,1)S(1)} all-to-all(bf16[16,16,384]{2,0,1:T(8,128)(2,1)S(1)} %bitcast.22), channel_id=1, replica_groups=mesh['groups'=2,'blk'=16] {'blk'}, dimensions={1} | all-to-all | bytes 393216 | tf_op jit(solution)/shard_map/all_to_all | solution.py:115
  48.4 0.2 fusion.10
  48.7 12.6 %all_to_all.26 = f32[16,16,256]{2,1,0:T(8,128)S(1)} all-to-all(f32[16,16,256]{2,1,0:T(8,128)S(1)} %fusion.10), channel_id=1, replica_groups=mesh['groups'=2,'blk'=16] {'blk'}, dimensions={0} | all-to-all | bytes 524288 | tf_op jit(solution)/shard_map/all_to_all | solution.py:117
  61.3 1.3 %broadcast_divide_fusion = f32[16,256]{1,0:T(8,128)} fusion(f32[16,256]{1,0:T(8,128)S(1)} %reduce_sum.49, f32[]{:T(128)} %reduce_sum.47), kind=kLoop, calls=%fused_computation.51 | loop fusion | flops 4096 | bytes 32772 | tf_op jit(solution)/shard_map/div | solution.py:141
  (25 shorter events, 0.3 us)
Async XLA Ops:
  0.0 5.4 %copy-start.1 = (s32[6144]{0:T(1024)S(1)}, s32[6144]{0:T(1024)}, u32[]{:S(2)}) copy-start(s32[6144]{0:T(1024)} %param.5) | copy-start | bytes 73732
  1.1 6.1 %collective-permute-start = (f32[3,6144]{1,0:T(4,128)S(1)}, f32[3,6144]{1,0:T(4,128)S(1)}, u32[]{:S(2)}, u32[]{:S(2)}) collective-permute-start(f32[3,6144]{1,0:T(4,128)S(1)} %get-tuple-element.10), channel_id=1, source_target_pairs={{0,1},{1,2},{2,3},{3,4},{4,5},{5,6},{6,7},{7,8},{8,9},{9,10},{10,1... | collective-permute-start | bytes 221192 | tf_op jit(solution)/shard_map/ppermute | solution.py:17
  3.5 5.3 %collective-permute-start.1 = (f32[3,6144]{1,0:T(4,128)S(1)}, f32[3,6144]{1,0:T(4,128)S(1)}, u32[]{:S(2)}, u32[]{:S(2)}) collective-permute-start(f32[3,6144]{1,0:T(4,128)S(1)} %get-tuple-element.11), channel_id=1, source_target_pairs={{1,0},{2,1},{3,2},{4,3},{5,4},{6,5},{7,6},{8,7},{9,8},{10,9},{11,1... | collective-permute-start | bytes 221192 | tf_op jit(solution)/shard_map/ppermute | solution.py:19
  6.4 2.4 %copy-start = (f32[16,6144]{1,0:T(8,128)S(1)}, f32[16,6144]{1,0:T(8,128)}, u32[]{:S(2)}) copy-start(f32[16,6144]{1,0:T(8,128)} %param.4) | copy-start | bytes 1179652
  13.1 4.2 %collective-permute-start.2 = (f32[6144]{0:T(1024)S(1)}, f32[6144]{0:T(1024)S(1)}, u32[]{:S(2)}, u32[]{:S(2)}) collective-permute-start(f32[6144]{0:T(1024)S(1)} %slice_add_fusion.18), channel_id=1, source_target_pairs={{0,1},{1,0},{2,3},{3,2},{4,5},{5,4},{6,7},{7,6},{8,9},{9,8},{10,11... | collective-permute-start | bytes 73736 | tf_op jit(solution)/shard_map/ppermute | solution.py:107
  17.2 4.2 %collective-permute-start.3 = (f32[6144]{0:T(1024)S(1)}, f32[6144]{0:T(1024)S(1)}, u32[]{:S(2)}, u32[]{:S(2)}) collective-permute-start(f32[6144]{0:T(1024)S(1)} %add.143), channel_id=1, source_target_pairs={{0,2},{1,3},{2,0},{3,1},{4,6},{5,7},{6,4},{7,5},{8,10},{9,11},{10,... | collective-permute-start | bytes 73736 | tf_op jit(solution)/shard_map/ppermute | solution.py:107
  21.5 6.5 %copy-start.2 = (s32[384]{0:T(512)S(1)}, s32[384]{0:T(512)}, u32[]{:S(2)}) copy-start(s32[384]{0:T(512)} %param.6) | copy-start | bytes 4612
  21.5 3.9 %collective-permute-start.4 = (f32[6144]{0:T(1024)S(1)}, f32[6144]{0:T(1024)S(1)}, u32[]{:S(2)}, u32[]{:S(2)}) collective-permute-start(f32[6144]{0:T(1024)S(1)} %add.144), channel_id=1, source_target_pairs={{0,4},{1,5},{2,6},{3,7},{4,0},{5,1},{6,2},{7,3},{8,12},{9,13},{10,... | collective-permute-start | bytes 73736 | tf_op jit(solution)/shard_map/ppermute | solution.py:107
  25.3 6.3 %collective-permute-start.5 = (f32[6144]{0:T(1024)S(1)}, f32[6144]{0:T(1024)S(1)}, u32[]{:S(2)}, u32[]{:S(2)}) collective-permute-start(f32[6144]{0:T(1024)S(1)} %add.145), channel_id=1, source_target_pairs={{0,8},{1,9},{2,10},{3,11},{4,12},{5,13},{6,14},{7,15},{8,0},{9,1},... | collective-permute-start | bytes 73736 | tf_op jit(solution)/shard_map/ppermute | solution.py:107

commit v2 on v1

--- a/solution.py
+++ b/solution.py
@@ -56,19 +56,22 @@
     return jnp.maximum(pair_total, 1).astype(jnp.float32)
 
 
-def mirrored_table(table):
-    return jnp.concatenate([table[1:][::-1], table])
+def mirrored_table(table, margin=0):
+    mirrored = jnp.concatenate([table[1:][::-1], table])
+    return jnp.pad(mirrored, margin, mode="edge")
 
 
-def skewed_map(table, window_first, rows_here, col_count):
+def skewed_map(table, window_first, rows_here, col_count, margin=0):
     span = col_count + rows_here - 1
-    window = lax.dynamic_slice_in_dim(mirrored_table(table), window_first, span)
+    window = lax.dynamic_slice_in_dim(
+        mirrored_table(table, margin), window_first + margin, span
+    )
     tiled = jnp.tile(window, rows_here + 1)[: rows_here * (span + 1)]
     shifted = tiled.reshape(rows_here, span + 1)[:, :col_count]
     return shifted[::-1]
 
 
-def diagonal_totals(smoothed, window_first):
+def diagonal_totals(smoothed, window_first, margin=0):
     rows_here = smoothed.shape[0]
     col_count = smoothed.shape[1]
     span = col_count + rows_here - 1
@@ -76,8 +79,11 @@
     flat = flipped.reshape(rows_here * (col_count + rows_here))[: rows_here * span]
     offsets = jnp.sum(flat.reshape(rows_here, span), axis=0)
     spread = lax.dynamic_update_slice_in_dim(
-        jnp.zeros((2 * col_count - 1,), jnp.float32), offsets, window_first, 0
-    )
+        jnp.zeros((2 * col_count - 1 + 2 * margin,), jnp.float32),
+        offsets,
+        window_first + margin,
+        0,
+    )[margin : margin + 2 * col_count - 1]
     lower = jnp.concatenate([jnp.zeros((1,), jnp.float32), spread[: col_count - 1][::-1]])
     return spread[col_count - 1 :] + lower
 
@@ -127,11 +133,18 @@
     first_row = position * rows_here
     first_bin = row_start[0]
     window_first = col_count - 1 - (first_bin + first_row + rows_here - 1)
+    wide_rows = rows_here + 2 * WMAX
+    wide_first = window_first - WMAX
+    wide_radius = skewed_map(widths, wide_first, wide_rows, col_count, WMAX)
+    own = jnp.pad(contacts, ((2 * WMAX, 2 * WMAX), (WMAX, WMAX)))
+    target = first_row - WMAX + jnp.arange(wide_rows, dtype=jnp.int32)
+    inside = (target >= 0) & (target < nbins)
+    own_part = jnp.where(inside[:, None], smooth(own, wide_radius), 0.0)
+    local_total = diagonal_totals(own_part, wide_first, WMAX)
     radius_map = skewed_map(widths, window_first, rows_here, col_count)
     padded_rows = with_halo(contacts, (("blk", 0),), WMAX)
     padded = jnp.pad(padded_rows, ((0, 0), (WMAX, WMAX)))
     smoothed = smooth(padded, radius_map)
-    local_total = diagonal_totals(smoothed, window_first)
     denominator = pair_counts(first_bin, nbins, col_count)
     expected = tree_sum(local_total, "blk") / denominator
     expected_map = skewed_map(expected, window_first, rows_here, col_count)

time: 62.9 us -> 69.2 us (1.10)
  local copies, waits for them, and re-layouts: 9.23 us -> 13.4 us
  other arithmetic: 6.45 us -> 9.59 us
  waiting for transfers between devices: 6.51 us -> 4.61 us
  starting transfers between devices: 13.6 us -> 14.5 us
    select_n x0 -> x1, other arithmetic: none -> 2.2 us  [shards(): own_part = jnp.where(inside[:, None], smooth(own, wide_radius), 0.0)]
    ppermute x1, waiting for transfers between devices: 1.6 us -> 0.01 us  [with_halo(): lax.ppermute(head, axis, [((i + 1) % count, i) for i in range(ends)])]
    add x1 -> x0, other arithmetic: 1.51 us -> none  [smooth(): smoothed + jnp.where(radius_map == radius, box_sums / float((2 * radius +...]
    reduce_sum x1, other arithmetic: 0.2 us -> 1.6 us  [normalize(): jnp.sum(ratio * kept_cols[None, :], axis=1, keepdims=True) / kept_total]
    add x1 -> x2, other arithmetic: 0.24 us -> 1.6 us  [smooth(): row_sums + padded[WMAX - radius:WMAX - radius + rows_here]]
    rev x2 -> x3, local copies, waits for them, and re-layouts: 1.54 us -> 2.76 us  [skewed_map(): return shifted[::-1]]
    ppermute x4, starting transfers between devices: 9.95 us -> 10.8 us  [tree_sum(): lax.ppermute(values, axis, [(i, i ^ step) for i in range(count)])]
    reshape x0 -> x1, local copies, waits for them, and re-layouts: none -> 0.69 us  [mirrored_table(): return jnp.pad(mirrored, margin, mode='edge')]
  transfers between devices with their start and end apart: 6 -> 6, of which waited for: 4 -> 3; matrix products, arithmetic and copies ran while one was open for 9% -> 13% of each run, Pallas kernels for 0% -> 0%
where the time goes in v2:
time: 69.2 us; the launch traced here: 68.9 us
  blocking collectives  25.4 us (37%)
  starting transfers between devices  14.5 us (21%)
  local copies, waits for them, and re-layouts  13.4 us (19%)
  other arithmetic  9.59 us (14%)
  waiting for transfers between devices  4.61 us (7%)
  between operations  1.05 us (2%)
    all_to_all x1, blocking collectives, gram_rows(): columns = lax.all_to_all(zscores, axis, 1, 0, tiled=True)  12.8 us
    all_to_all x1, blocking collectives, gram_rows(): pieces = lax.all_to_all(partial, axis, 0, 0, tiled=True)  12.6 us
    ppermute x4, starting transfers between devices, tree_sum(): lax.ppermute(values, axis, [(i, i ^ step) for i in range(count)])  10.8 us
    ppermute x4, waiting for transfers between devices, tree_sum(): lax.ppermute(values, axis, [(i, i ^ step) for i in range(count)])  4.6 us
    scatter x1, local copies, waits for them, and re-layouts, shards(): kept_bins = jnp.ones((col_count,), jnp.float32).at[masked_bins].set(0.0)  2.95 us
    rev x3, local copies, waits for them, and re-layouts, skewed_map(): return shifted[::-1]  2.76 us
    ppermute x1, starting transfers between devices, with_halo(): lax.ppermute(tail, axis, [(i, (i + 1) % count) for i in range(ends)])  2.4 us
    select_n x1, other arithmetic, shards(): own_part = jnp.where(inside[:, None], smooth(own, wide_radius), 0.0)  2.2 us
  transfers between devices with their start and end apart: 6, of which 3 were waited for; matrix products, arithmetic and copies ran while one was open for 13% of the time, Pallas kernels for 0%

profile of v2, /device:TPU:0, one launch (start us, length us, event | category | flops | bytes accessed | tf_op | source)
XLA Modules:
  0.0 68.9 jit_solution(9582320588533059406)
XLA Ops:
  0.0 1.1 %fusion.37 = (f32[3,6144]{1,0:T(4,128)S(1)}, f32[3,6144]{1,0:T(4,128)S(1)}) fusion(f32[16,6144]{1,0:T(8,128)} %param.4), kind=kLoop, calls=%fused_computation.94 | loop fusion | bytes 294912 | tf_op jit(solution)/shard_map/slice | solution.py:14
  1.1 2.4 %collective-permute-start = (f32[3,6144]{1,0:T(4,128)S(1)}, f32[3,6144]{1,0:T(4,128)S(1)}, u32[]{:S(2)}, u32[]{:S(2)}) collective-permute-start(f32[3,6144]{1,0:T(4,128)S(1)} %get-tuple-element.14), channel_id=1, source_target_pairs={{0,1},{1,2},{2,3},{3,4},{4,5},{5,6},{6,7},{7,8},{8,9},{9,10},{10,1... | collective-permute-start | bytes 221192 | tf_op jit(solution)/shard_map/ppermute | solution.py:17
  3.5 1.3 %collective-permute-start.1 = (f32[3,6144]{1,0:T(4,128)S(1)}, f32[3,6144]{1,0:T(4,128)S(1)}, u32[]{:S(2)}, u32[]{:S(2)}) collective-permute-start(f32[3,6144]{1,0:T(4,128)S(1)} %get-tuple-element.15), channel_id=1, source_target_pairs={{1,0},{2,1},{3,2},{4,3},{5,4},{6,5},{7,6},{8,7},{9,8},{10,9},{11,1... | collective-permute-start | bytes 221192 | tf_op jit(solution)/shard_map/ppermute | solution.py:19
  4.9 0.7 slice.221
  6.2 0.1 reverse.1
  6.3 0.7 %reshape.57 = s32[3]{0:T(128)S(1)} broadcast(s32[]{:T(128)} %bitcast.1), dimensions={} | broadcast | bytes 16 | tf_op jit(solution)/shard_map/jit(_pad)/reshape | solution.py:61
  7.1 0.1 concatenate.20
  7.1 0.1 dynamic_slice.13
  7.3 0.3 tile.30
  7.6 0.4 reshape.58
  8.1 1.2 %rev.24 = s32[22,6144]{1,0:T(8,128)S(1)} reverse(s32[22,6144]{1,0:T(8,128)S(1)} %slice.279), dimensions={0} | reverse | bytes 1081344 | tf_op jit(solution)/shard_map/rev | solution.py:71
  9.3 1.4 %fusion.5 = (f32[22,6150]{1,0:T(8,128)S(1)}, f32[22,6150]{1,0:T(8,128)S(1)}, f32[22,6150]{1,0:T(8,128)S(1)}, f32[22,6150]{1,0:T(8,128)S(1)}) fusion(f32[16,6144]{1,0:T(8,128)S(1)} %copy-done, f32[3,6144]{1,0:T(4,128)S(1)} %collective-permute-done.1, f32[3,6144]{1,0:T(4,128)S(1)} %collective-permute-done), kind=kLoop, calls=%fused_computation.16 | loop fusion | flops 1894200 | bytes 2705472 | tf_op jit(solution)/shard_map/add | solution.py:34
  10.7 2.2 %fusion.11 = f32[22,6144]{1,0:T(8,128)S(1)} fusion(f32[16,6144]{1,0:T(8,128)S(1)} %copy-done, f32[22,6150]{1,0:T(8,128)S(1)} %get-tuple-element.10, f32[22,6150]{1,0:T(8,128)S(1)} %get-tuple-element.11, f32[22,6150]{1,0:T(8,128)S(1)} %get-tuple-element.12, s32[22,6144]{1,0:T(8,128)S(1)} %rev.24, pred[22]{0:T(512)(128)(4,1)S(1)} %compare_and_fusion), kind=kLoop, calls=%fused_computation.24 | loop fusion | flops 3649536 | bytes 9584662 | tf_op jit(solution)/shard_map/jit(_where)/select_n | solution.py:142
  12.9 1.2 %rev.25 = f32[22,6144]{1,0:T(8,128)S(1)} reverse(f32[22,6144]{1,0:T(8,128)S(1)} %fusion.11), dimensions={0} | reverse | bytes 1081344 | tf_op jit(solution)/shard_map/rev | solution.py:78
  14.2 0.3 reshape.59
  14.5 0.4 reshape.60
  14.9 0.5 dynamic_update_slice.3
  15.5 0.1 reverse.2
  15.6 0.1 slice.462
  15.6 0.1 slice_add_fusion.30
  15.7 3.3 %collective-permute-start.2 = (f32[6144]{0:T(1024)S(1)}, f32[6144]{0:T(1024)S(1)}, u32[]{:S(2)}, u32[]{:S(2)}) collective-permute-start(f32[6144]{0:T(1024)S(1)} %slice_add_fusion.30), channel_id=1, source_target_pairs={{0,1},{1,0},{2,3},{3,2},{4,5},{5,4},{6,7},{7,6},{8,9},{9,8},{10,11... | collective-permute-start | bytes 73736 | tf_op jit(solution)/shard_map/ppermute | solution.py:113
  19.1 0.8 %collective-permute-done.2 = f32[6144]{0:T(1024)S(1)} collective-permute-done((f32[6144]{0:T(1024)S(1)}, f32[6144]{0:T(1024)S(1)}, u32[]{:S(2)}, u32[]{:S(2)}) %collective-permute-start.2) | collective-permute-done | bytes 24608 | tf_op jit(solution)/shard_map/ppermute | solution.py:113
  19.9 2.0 %collective-permute-start.3 = (f32[6144]{0:T(1024)S(1)}, f32[6144]{0:T(1024)S(1)}, u32[]{:S(2)}, u32[]{:S(2)}) collective-permute-start(f32[6144]{0:T(1024)S(1)} %add.254), channel_id=1, source_target_pairs={{0,2},{1,3},{2,0},{3,1},{4,6},{5,7},{6,4},{7,5},{8,10},{9,11},{10,... | collective-permute-start | bytes 73736 | tf_op jit(solution)/shard_map/ppermute | solution.py:113
  21.9 1.9 %collective-permute-done.3 = f32[6144]{0:T(1024)S(1)} collective-permute-done((f32[6144]{0:T(1024)S(1)}, f32[6144]{0:T(1024)S(1)}, u32[]{:S(2)}, u32[]{:S(2)}) %collective-permute-start.3) | collective-permute-done | bytes 24608 | tf_op jit(solution)/shard_map/ppermute | solution.py:113
  23.7 2.9 %collective-permute-start.4 = (f32[6144]{0:T(1024)S(1)}, f32[6144]{0:T(1024)S(1)}, u32[]{:S(2)}, u32[]{:S(2)}) collective-permute-start(f32[6144]{0:T(1024)S(1)} %add.255), channel_id=1, source_target_pairs={{0,4},{1,5},{2,6},{3,7},{4,0},{5,1},{6,2},{7,3},{8,12},{9,13},{10,... | collective-permute-start | bytes 73736 | tf_op jit(solution)/shard_map/ppermute | solution.py:113
  26.7 0.1 fusion.31
  26.8 0.2 tile.13
  27.1 0.2 reshape.56
  27.4 0.8 %rev.23 = s32[16,6144]{1,0:T(8,128)S(1)} reverse(s32[16,6144]{1,0:T(8,128)S(1)} %slice.255), dimensions={0} | reverse | bytes 786432 | tf_op jit(solution)/shard_map/rev | solution.py:71
  28.2 3.0 %scatter_custom_fusion = f32[6144]{0:T(1024)S(1)} fusion(s32[384]{0:T(512)S(1)} %compare_select_fusion, f32[384]{0:T(512)S(1)} %broadcast.60, f32[]{:T(128)} %constant.38.clone.1), kind=kCustom, calls=%fused_computation.87 | custom fusion | bytes 24580 | tf_op jit(solution)/shard_map/scatter | solution.py:151
  31.1 0.7 reduce_sum.47
  31.9 2.6 %collective-permute-start.5 = (f32[6144]{0:T(1024)S(1)}, f32[6144]{0:T(1024)S(1)}, u32[]{:S(2)}, u32[]{:S(2)}) collective-permute-start(f32[6144]{0:T(1024)S(1)} %add.256), channel_id=1, source_target_pairs={{0,8},{1,9},{2,10},{3,11},{4,12},{5,13},{6,14},{7,15},{8,0},{9,1},... | collective-permute-start | bytes 73736 | tf_op jit(solution)/shard_map/ppermute | solution.py:113
  34.5 0.2 slice_add_fusion.12
  34.8 1.9 %collective-permute-done.5 = f32[6144]{0:T(1024)S(1)} collective-permute-done((f32[6144]{0:T(1024)S(1)}, f32[6144]{0:T(1024)S(1)}, u32[]{:S(2)}, u32[]{:S(2)}) %collective-permute-start.5) | collective-permute-done | bytes 24608 | tf_op jit(solution)/shard_map/ppermute | solution.py:113
  36.8 0.1 reverse.3
  36.9 0.1 fusion.30
  37.1 0.2 tile.32
  37.4 0.2 reshape.61
  37.7 0.8 %rev.28 = f32[16,6144]{1,0:T(8,128)S(1)} reverse(f32[16,6144]{1,0:T(8,128)S(1)} %slice.300), dimensions={0} | reverse | bytes 786432 | tf_op jit(solution)/shard_map/rev | solution.py:71
  38.4 1.6 %multiply_reduce_fusion.1 = (f32[16]{0:T(128)S(1)}, f32[16,6144]{1,0:T(8,128)S(1)}) fusion(f32[6144]{0:T(1024)S(1)} %scatter_custom_fusion, f32[16,6144]{1,0:T(8,128)S(1)} %rev.28, f32[16,6150]{1,0:T(8,128)S(1)} %get-tuple-element.7, s32[16,6144]{1,0:T(8,128)S(1)} %rev.23, f32[16,6150]{1,0:T(8,128)S(1)} %get-tuple-element.8, ...), kind=kLoop, calls=%fused_computation.74 | loop fusion | flops 2850800 | bytes 7495744 | tf_op jit(solution)/shard_map/reduce_sum | solution.py:94
  40.0 0.7 %broadcast_divide_fusion.1 = f32[16]{0:T(128)S(1)} fusion(f32[16]{0:T(128)S(1)} %get-tuple-element.5, f32[]{:T(128)} %reduce_sum.47), kind=kLoop, calls=%fused_computation.93 | loop fusion | flops 16 | bytes 132 | tf_op jit(solution)/shard_map/div | solution.py:94
  40.8 0.3 multiply_reduce_fusion
  41.0 0.7 %add_rsqrt_fusion = f32[16]{0:T(128)S(1)} fusion(f32[16]{0:T(128)S(1)} %multiply_reduce_fusion, f32[]{:T(128)} %reduce_sum.47), kind=kLoop, calls=%fused_computation.92 | loop fusion | flops 32 | bytes 132 | tf_op jit(solution)/shard_map/rsqrt | solution.py:97
  41.7 0.1 multiply_convert_fusion
  41.9 12.8 %all_to_all.25 = bf16[16,16,384]{2,0,1:T(8,128)(2,1)S(1)} all-to-all(bf16[16,16,384]{2,0,1:T(8,128)(2,1)S(1)} %bitcast.23), channel_id=1, replica_groups=mesh['groups'=2,'blk'=16] {'blk'}, dimensions={1} | all-to-all | bytes 393216 | tf_op jit(solution)/shard_map/all_to_all | solution.py:121
  54.7 0.2 fusion.28
  54.9 12.6 %all_to_all.26 = f32[16,16,256]{2,1,0:T(8,128)S(1)} all-to-all(f32[16,16,256]{2,1,0:T(8,128)S(1)} %fusion.28), channel_id=1, replica_groups=mesh['groups'=2,'blk'=16] {'blk'}, dimensions={0} | all-to-all | bytes 524288 | tf_op jit(solution)/shard_map/all_to_all | solution.py:123
  67.6 1.3 %broadcast_divide_fusion = f32[16,256]{1,0:T(8,128)} fusion(f32[16,256]{1,0:T(8,128)S(1)} %reduce_sum.49, f32[]{:T(128)} %reduce_sum.47), kind=kLoop, calls=%fused_computation.89 | loop fusion | flops 4096 | bytes 32772 | tf_op jit(solution)/shard_map/div | solution.py:154
  (36 shorter events, 1.0 us)
Async XLA Ops:
  0.0 4.8 %copy-start.1 = (s32[6144]{0:T(1024)S(1)}, s32[6144]{0:T(1024)}, u32[]{:S(2)}) copy-start(s32[6144]{0:T(1024)} %param.5) | copy-start | bytes 73732
  1.1 8.2 %collective-permute-start = (f32[3,6144]{1,0:T(4,128)S(1)}, f32[3,6144]{1,0:T(4,128)S(1)}, u32[]{:S(2)}, u32[]{:S(2)}) collective-permute-start(f32[3,6144]{1,0:T(4,128)S(1)} %get-tuple-element.14), channel_id=1, source_target_pairs={{0,1},{1,2},{2,3},{3,4},{4,5},{5,6},{6,7},{7,8},{8,9},{9,10},{10,1... | collective-permute-start | bytes 221192 | tf_op jit(solution)/shard_map/ppermute | solution.py:17
  3.5 5.8 %collective-permute-start.1 = (f32[3,6144]{1,0:T(4,128)S(1)}, f32[3,6144]{1,0:T(4,128)S(1)}, u32[]{:S(2)}, u32[]{:S(2)}) collective-permute-start(f32[3,6144]{1,0:T(4,128)S(1)} %get-tuple-element.15), channel_id=1, source_target_pairs={{1,0},{2,1},{3,2},{4,3},{5,4},{6,5},{7,6},{8,7},{9,8},{10,9},{11,1... | collective-permute-start | bytes 221192 | tf_op jit(solution)/shard_map/ppermute | solution.py:19
  8.0 1.3 %copy-start = (f32[16,6144]{1,0:T(8,128)S(1)}, f32[16,6144]{1,0:T(8,128)}, u32[]{:S(2)}) copy-start(f32[16,6144]{1,0:T(8,128)} %param.4) | copy-start | bytes 1179652
  15.7 6.1 %copy-start.2 = (s32[384]{0:T(512)S(1)}, s32[384]{0:T(512)}, u32[]{:S(2)}) copy-start(s32[384]{0:T(512)} %param.6) | copy-start | bytes 4612
  15.7 4.2 %collective-permute-start.2 = (f32[6144]{0:T(1024)S(1)}, f32[6144]{0:T(1024)S(1)}, u32[]{:S(2)}, u32[]{:S(2)}) collective-permute-start(f32[6144]{0:T(1024)S(1)} %slice_add_fusion.30), channel_id=1, source_target_pairs={{0,1},{1,0},{2,3},{3,2},{4,5},{5,4},{6,7},{7,6},{8,9},{9,8},{10,11... | collective-permute-start | bytes 73736 | tf_op jit(solution)/shard_map/ppermute | solution.py:113
  19.9 3.8 %collective-permute-start.3 = (f32[6144]{0:T(1024)S(1)}, f32[6144]{0:T(1024)S(1)}, u32[]{:S(2)}, u32[]{:S(2)}) collective-permute-start(f32[6144]{0:T(1024)S(1)} %add.254), channel_id=1, source_target_pairs={{0,2},{1,3},{2,0},{3,1},{4,6},{5,7},{6,4},{7,5},{8,10},{9,11},{10,... | collective-permute-start | bytes 73736 | tf_op jit(solution)/shard_map/ppermute | solution.py:113
  23.7 8.1 %collective-permute-start.4 = (f32[6144]{0:T(1024)S(1)}, f32[6144]{0:T(1024)S(1)}, u32[]{:S(2)}, u32[]{:S(2)}) collective-permute-start(f32[6144]{0:T(1024)S(1)} %add.255), channel_id=1, source_target_pairs={{0,4},{1,5},{2,6},{3,7},{4,0},{5,1},{6,2},{7,3},{8,12},{9,13},{10,... | collective-permute-start | bytes 73736 | tf_op jit(solution)/shard_map/ppermute | solution.py:113
  31.9 4.8 %collective-permute-start.5 = (f32[6144]{0:T(1024)S(1)}, f32[6144]{0:T(1024)S(1)}, u32[]{:S(2)}, u32[]{:S(2)}) collective-permute-start(f32[6144]{0:T(1024)S(1)} %add.256), channel_id=1, source_target_pairs={{0,8},{1,9},{2,10},{3,11},{4,12},{5,13},{6,14},{7,15},{8,0},{9,1},... | collective-permute-start | bytes 73736 | tf_op jit(solution)/shard_map/ppermute | solution.py:113

commit v3 on v1

--- a/solution.py
+++ b/solution.py
@@ -1,9 +1,64 @@
 import jax
 import jax.numpy as jnp
 from jax import lax
+from jax.experimental import pallas as pl
+from jax.experimental.pallas import tpu as pltpu
 from jax.sharding import PartitionSpec as P
 
 WMAX = 3
+LANE = 128
+
+def smooth_kernel(xp_ref, w_ref, s_ref, tot_ref):
+    rows, cols = s_ref.shape
+    width = w_ref.shape[1]
+    skew = pltpu.roll(jnp.broadcast_to(w_ref[...], (rows, width)), width - (rows - 1), 1, stride=1, stride_axis=0)
+    radius = skew[:, :cols]
+    col = lax.broadcasted_iota(jnp.int32, (rows, cols), 1)
+    row_sums = xp_ref[WMAX:WMAX + rows, :]
+    smoothed = jnp.zeros((rows, cols), jnp.float32)
+    for r in range(WMAX + 1):
+        if r > 0:
+            row_sums = row_sums + xp_ref[WMAX - r:WMAX - r + rows, :] + xp_ref[WMAX + r:WMAX + r + rows, :]
+        box = row_sums
+        for o in range(1, r + 1):
+            box = (box + jnp.where(col >= o, pltpu.roll(row_sums, o, 1), 0.0)
+                   + jnp.where(col < cols - o, pltpu.roll(row_sums, cols - o, 1), 0.0))
+        smoothed = smoothed + jnp.where(radius == float(r), box / float((2 * r + 1) ** 2), 0.0)
+    s_ref[...] = smoothed
+    placed = jnp.concatenate([jnp.zeros((rows, width - cols), jnp.float32), smoothed], axis=1)
+    total = placed[0:1, :]
+    for i in range(1, rows):
+        total = total + pltpu.roll(placed[i:i + 1, :], width - i, 1)
+    tot_ref[...] = total
+
+def smooth_call(xp, wrow, rows):
+    cols = xp.shape[1]
+    return pl.pallas_call(
+        smooth_kernel,
+        out_shape=(jax.ShapeDtypeStruct((rows, cols), jnp.float32), jax.ShapeDtypeStruct((1, wrow.shape[1]), jnp.float32)),
+        in_specs=[pl.BlockSpec(memory_space=pltpu.VMEM)] * 2,
+        out_specs=(pl.BlockSpec(memory_space=pltpu.VMEM),) * 2,
+    )(xp, wrow)
+
+def zscore_kernel(s_ref, e_ref, keep_ref, krow_ref, kt_ref, z_ref):
+    rows, cols = s_ref.shape
+    width = e_ref.shape[1]
+    skew = pltpu.roll(jnp.broadcast_to(e_ref[...], (rows, width)), width - (rows - 1), 1, stride=1, stride_axis=0)
+    ratio = s_ref[...] / skew[:, :cols]
+    keep = keep_ref[...]
+    kt = kt_ref[...]
+    mean = jnp.sum(ratio * keep, axis=1, keepdims=True) / kt
+    centred = (ratio - mean) * keep
+    var = jnp.sum(centred * centred, axis=1, keepdims=True) / kt
+    z_ref[...] = (centred * lax.rsqrt(var + 1e-05) * krow_ref[...]).astype(z_ref.dtype)
+
+def zscore_call(s, erow, keep, krow, kt):
+    return pl.pallas_call(
+        zscore_kernel,
+        out_shape=jax.ShapeDtypeStruct(s.shape, jnp.bfloat16),
+        in_specs=[pl.BlockSpec(memory_space=pltpu.VMEM)] * 5,
+        out_specs=pl.BlockSpec(memory_space=pltpu.VMEM),
+    )(s, erow, keep, krow, kt)
 
 
 def with_halo(cells, sides, width):
@@ -118,6 +173,23 @@
     return jnp.sum(pieces.reshape(blocks, rows_here, pieces.shape[1]), axis=0)
 
 
+def window_row(table, window_first, width):
+    mirrored = jnp.pad(mirrored_table(table.astype(jnp.float32)), (0, width))
+    return lax.dynamic_slice_in_dim(mirrored, window_first, width)[None]
+
+
+def signed_totals(totals, first_bin, col_count):
+    width = totals.shape[1]
+    spread = lax.dynamic_update_slice_in_dim(
+        jnp.zeros((2 * col_count - 1 + 2 * width,), jnp.float32),
+        totals[0],
+        col_count - 1 - (width - col_count) - first_bin + width,
+        0,
+    )[width : width + 2 * col_count - 1]
+    lower = jnp.concatenate([jnp.zeros((1,), jnp.float32), spread[: col_count - 1][::-1]])
+    return spread[col_count - 1 :] + lower
+
+
 def shards(contacts, widths, masked_bins, row_start):
     blocks = lax.axis_size("blk")
     position = lax.axis_index("blk")
@@ -127,17 +199,24 @@
     first_row = position * rows_here
     first_bin = row_start[0]
     window_first = col_count - 1 - (first_bin + first_row + rows_here - 1)
-    radius_map = skewed_map(widths, window_first, rows_here, col_count)
+    width = col_count + LANE
     padded_rows = with_halo(contacts, (("blk", 0),), WMAX)
-    padded = jnp.pad(padded_rows, ((0, 0), (WMAX, WMAX)))
-    smoothed = smooth(padded, radius_map)
-    local_total = diagonal_totals(smoothed, window_first)
+    extra = -padded_rows.shape[0] % 8
+    padded = jnp.pad(padded_rows, ((0, extra), (0, 0)))
+    smoothed, totals = smooth_call(padded, window_row(widths, window_first, width), rows_here)
+    local_total = signed_totals(totals, first_bin + first_row, col_count)
     denominator = pair_counts(first_bin, nbins, col_count)
     expected = tree_sum(local_total, "blk") / denominator
-    expected_map = skewed_map(expected, window_first, rows_here, col_count)
     kept_bins = jnp.ones((col_count,), jnp.float32).at[masked_bins].set(0.0)
     kept_rows = lax.dynamic_slice_in_dim(kept_bins, first_bin + first_row, rows_here)
-    zscores, kept_total = normalize(smoothed, expected_map, kept_rows, kept_bins)
+    kept_total = jnp.sum(kept_bins)
+    zscores = zscore_call(
+        smoothed,
+        window_row(expected, window_first, width),
+        kept_bins[None],
+        kept_rows[:, None],
+        kept_total.reshape(1, 1),
+    )
     return gram_rows(zscores, "blk") / kept_total
 
 

time: 62.9 us -> 66.8 us (1.062)
  Pallas kernels: 0 us -> 7.13 us
  other arithmetic: 6.45 us -> 4.56 us
  blocking collectives: 25.6 us -> 26.7 us
  local copies, waits for them, and re-layouts: 9.23 us -> 8.19 us
  waiting for transfers between devices: 6.51 us -> 5.5 us
    pallas_call x0 -> x2, Pallas kernels: none -> 7.13 us  [the longest x1 4.3 us: smooth_call(): pl.pallas_call(smooth_kernel, out_shape=(jax.ShapeDtypeStruct((rows, cols...]
    rev x3 -> x0, local copies, waits for them, and re-layouts: 2.31 us -> none  [the longest x2 1.54 us: skewed_map(): return shifted[::-1]]
    broadcast_in_dim x1 -> x5, local copies, waits for them, and re-layouts: 0.01 us -> 2.03 us  [the longest x2 1.26 us: window_row(): return lax.dynamic_slice_in_dim(mirrored, window_first, width)[None]]
    add x3 -> x1, other arithmetic: 1.83 us -> 0.08 us  [signed_totals(): return spread[col_count - 1:] + lower]
    all_to_all x1, blocking collectives: 12.9 us -> 14.1 us  [gram_rows(): columns = lax.all_to_all(zscores, axis, 1, 0, tiled=True)]
    ppermute x4, waiting for transfers between devices: 4.91 us -> 3.86 us  [tree_sum(): lax.ppermute(values, axis, [(i, i ^ step) for i in range(count)])]
    reshape x4 -> x0, local copies, waits for them, and re-layouts: 1.02 us -> none  [the longest x2 0.47 us: skewed_map(): shifted = tiled.reshape(rows_here, span + 1)[:, :col_count]]
    all_to_all x1, local copies, waits for them, and re-layouts: 0.02 us -> 0.95 us  [gram_rows(): columns = lax.all_to_all(zscores, axis, 1, 0, tiled=True)]
where the time goes in v3:
time: 66.8 us; the launch traced here: 66.4 us
  blocking collectives  26.7 us (40%)
  starting transfers between devices  13.3 us (20%)
  local copies, waits for them, and re-layouts  8.19 us (12%)
  Pallas kernels  7.13 us (11%)
  waiting for transfers between devices  5.5 us (8%)
  other arithmetic  4.56 us (7%)
  between operations  0.78 us (1%)
    all_to_all x1, blocking collectives, gram_rows(): columns = lax.all_to_all(zscores, axis, 1, 0, tiled=True)  14.1 us
    all_to_all x1, blocking collectives, gram_rows(): pieces = lax.all_to_all(partial, axis, 0, 0, tiled=True)  12.6 us
    ppermute x4, starting transfers between devices, tree_sum(): lax.ppermute(values, axis, [(i, i ^ step) for i in range(count)])  9.56 us
    pallas_call x1, Pallas kernels, smooth_call(): pl.pallas_call(smooth_kernel, out_shape=(jax.ShapeDtypeStruct((rows, cols...  4.3 us
    ppermute x4, waiting for transfers between devices, tree_sum(): lax.ppermute(values, axis, [(i, i ^ step) for i in range(count)])  3.86 us
    scatter x1, local copies, waits for them, and re-layouts, shards(): kept_bins = jnp.ones((col_count,), jnp.float32).at[masked_bins].set(0.0)  2.95 us
    pallas_call x1, Pallas kernels, zscore_call(): pl.pallas_call(zscore_kernel, out_shape=jax.ShapeDtypeStruct(s.shape, jnp...  2.83 us
    ppermute x1, starting transfers between devices, with_halo(): lax.ppermute(tail, axis, [(i, (i + 1) % count) for i in range(ends)])  2.4 us
  transfers between devices with their start and end apart: 6, of which 4 were waited for; matrix products, arithmetic and copies ran while one was open for 9% of the time, Pallas kernels for 0%

profile of v3, /device:TPU:0, one launch (start us, length us, event | category | flops | bytes accessed | tf_op | source)
XLA Modules:
  0.0 66.4 jit_solution(13799333544418523448)
XLA Ops:
  0.0 0.0 copy-start
  0.0 1.1 %fusion.10 = (f32[3,6144]{1,0:T(4,128)S(1)}, f32[3,6144]{1,0:T(4,128)S(1)}) fusion(f32[16,6144]{1,0:T(8,128)} %param.4), kind=kLoop, calls=%fused_computation.26 | loop fusion | bytes 294912 | tf_op jit(solution)/shard_map/slice | solution.py:69
  1.1 2.4 %collective-permute-start = (f32[3,6144]{1,0:T(4,128)S(1)}, f32[3,6144]{1,0:T(4,128)S(1)}, u32[]{:S(2)}, u32[]{:S(2)}) collective-permute-start(f32[3,6144]{1,0:T(4,128)S(1)} %get-tuple-element.9), channel_id=1, source_target_pairs={{0,1},{1,2},{2,3},{3,4},{4,5},{5,6},{6,7},{7,8},{8,9},{9,10},{10,1... | collective-permute-start | bytes 221192 | tf_op jit(solution)/shard_map/ppermute | solution.py:72
  3.5 1.3 %collective-permute-start.1 = (f32[3,6144]{1,0:T(4,128)S(1)}, f32[3,6144]{1,0:T(4,128)S(1)}, u32[]{:S(2)}, u32[]{:S(2)}) collective-permute-start(f32[3,6144]{1,0:T(4,128)S(1)} %get-tuple-element.10), channel_id=1, source_target_pairs={{1,0},{2,1},{3,2},{4,3},{5,4},{6,5},{7,6},{8,7},{9,8},{10,9},{11,1... | collective-permute-start | bytes 221192 | tf_op jit(solution)/shard_map/ppermute | solution.py:74
  5.5 0.7 %convert_element_type.11 = f32[6144]{0:T(1024)S(1)} convert(s32[6144]{0:T(1024)} %param.5) | non-fusion elementwise | flops 6144 | bytes 49152 | tf_op jit(solution)/shard_map/convert_element_type | solution.py:177
  6.2 0.1 slice.27
  6.3 0.1 reverse
  6.4 0.1 slice.32
  6.5 0.1 fusion.3
  6.6 0.6 broadcast_in_dim.28.w_ref
  7.2 0.0 collective-permute-done
  7.2 1.6 %collective-permute-done.1 = f32[3,6144]{1,0:T(4,128)S(1)} collective-permute-done((f32[3,6144]{1,0:T(4,128)S(1)}, f32[3,6144]{1,0:T(4,128)S(1)}, u32[]{:S(2)}, u32[]{:S(2)}) %collective-permute-start.1) | collective-permute-done | bytes 73760 | tf_op jit(solution)/shard_map/ppermute | solution.py:74
  8.8 0.0 copy-done
  8.8 0.9 %select_maximum_fusion.xp_ref = f32[24,6144]{1,0:T(8,128)} fusion(f32[3,6144]{1,0:T(4,128)S(1)} %collective-permute-done.1, f32[16,6144]{1,0:T(8,128)S(1)} %copy-done, f32[3,6144]{1,0:T(4,128)S(1)} %collective-permute-done), kind=kLoop, calls=%fused_computation.1 | loop fusion | flops 884736 | bytes 1130496 | tf_op jit(solution)/shard_map/concatenate | solution.py:70
  9.8 4.3 %shard_map.46 = (f32[16,6144]{1,0:T(8,128)}, f32[1,6272]{1,0:T(1,128)}) custom-call(f32[24,6144]{1,0:T(8,128)} %select_maximum_fusion.xp_ref, f32[1,6272]{1,0:T(1,128)} %broadcast_in_dim.28.w_ref), custom_call_target="tpu_custom_call" | custom-call | tf_op jit(solution)/shard_map/pallas_call | solution.py:36
  14.1 0.8 %reduce.1 = f32[6272]{0:T(1024)S(1)} reduce(f32[1,6272]{1,0:T(1,128)} %get-tuple-element.8, f32[]{:T(128)} %constant.51), dimensions={0}, to_apply=%get-tuple-element.8.reduce_sub_computation | reduce | bytes 50180 | tf_op jit(solution)/shard_map/pallas_call | solution.py:36
  14.9 0.5 dynamic_update_slice.3
  15.4 0.1 reverse.1
  15.5 0.1 slice.33
  15.6 0.1 slice_add_fusion
  15.7 3.3 %collective-permute-start.2 = (f32[6144]{0:T(1024)S(1)}, f32[6144]{0:T(1024)S(1)}, u32[]{:S(2)}, u32[]{:S(2)}) collective-permute-start(f32[6144]{0:T(1024)S(1)} %slice_add_fusion), channel_id=1, source_target_pairs={{0,1},{1,0},{2,3},{3,2},{4,5},{5,4},{6,7},{7,6},{8,9},{9,8},{10,11... | collective-permute-start | bytes 73736 | tf_op jit(solution)/shard_map/ppermute | solution.py:162
  19.0 0.8 %collective-permute-done.2 = f32[6144]{0:T(1024)S(1)} collective-permute-done((f32[6144]{0:T(1024)S(1)}, f32[6144]{0:T(1024)S(1)}, u32[]{:S(2)}, u32[]{:S(2)}) %collective-permute-start.2) | collective-permute-done | bytes 24608 | tf_op jit(solution)/shard_map/ppermute | solution.py:162
  19.8 0.0 copy-start.2
  19.8 2.4 %collective-permute-start.3 = (f32[6144]{0:T(1024)S(1)}, f32[6144]{0:T(1024)S(1)}, u32[]{:S(2)}, u32[]{:S(2)}) collective-permute-start(f32[6144]{0:T(1024)S(1)} %add.63), channel_id=1, source_target_pairs={{0,2},{1,3},{2,0},{3,1},{4,6},{5,7},{6,4},{7,5},{8,10},{9,11},{10,... | collective-permute-start | bytes 73736 | tf_op jit(solution)/shard_map/ppermute | solution.py:162
  22.2 1.8 %collective-permute-done.3 = f32[6144]{0:T(1024)S(1)} collective-permute-done((f32[6144]{0:T(1024)S(1)}, f32[6144]{0:T(1024)S(1)}, u32[]{:S(2)}, u32[]{:S(2)}) %collective-permute-start.3) | collective-permute-done | bytes 24608 | tf_op jit(solution)/shard_map/ppermute | solution.py:162
  24.1 1.6 %collective-permute-start.4 = (f32[6144]{0:T(1024)S(1)}, f32[6144]{0:T(1024)S(1)}, u32[]{:S(2)}, u32[]{:S(2)}) collective-permute-start(f32[6144]{0:T(1024)S(1)} %add.64), channel_id=1, source_target_pairs={{0,4},{1,5},{2,6},{3,7},{4,0},{5,1},{6,2},{7,3},{8,12},{9,13},{10,... | collective-permute-start | bytes 73736 | tf_op jit(solution)/shard_map/ppermute | solution.py:162
  25.6 0.0 copy-done.2
  25.6 2.9 %scatter_custom_fusion = f32[6144]{0:T(1024)S(1)} fusion(s32[384]{0:T(512)S(1)} %compare_select_fusion, f32[384]{0:T(512)S(1)} %broadcast.6, f32[]{:T(128)} %constant.12.clone.1), kind=kCustom, calls=%fused_computation.21 | custom fusion | bytes 24580 | tf_op jit(solution)/shard_map/scatter | solution.py:210
  28.6 0.0 copy-start.1
  28.6 0.0 collective-permute-done.4
  28.6 2.3 %collective-permute-start.5 = (f32[6144]{0:T(1024)S(1)}, f32[6144]{0:T(1024)S(1)}, u32[]{:S(2)}, u32[]{:S(2)}) collective-permute-start(f32[6144]{0:T(1024)S(1)} %add.65), channel_id=1, source_target_pairs={{0,8},{1,9},{2,10},{3,11},{4,12},{5,13},{6,14},{7,15},{8,0},{9,1},... | collective-permute-start | bytes 73736 | tf_op jit(solution)/shard_map/ppermute | solution.py:162
  30.9 0.1 dynamic-slice_bitcast_fusion
  31.0 0.0 copy-done.1
  31.0 0.6 reduce_sum.18
  31.5 0.7 %copy.5.krow_ref = f32[16,1]{1,0:T(8,128)} copy(f32[16,1]{0,1:T(1,128)S(1)} %dynamic-slice_bitcast_fusion) | data formatting | bytes 128 | tf_op jit(solution)/shard_map/broadcast_in_dim | solution.py:217
  32.2 1.2 %collective-permute-done.5 = f32[6144]{0:T(1024)S(1)} collective-permute-done((f32[6144]{0:T(1024)S(1)}, f32[6144]{0:T(1024)S(1)}, u32[]{:S(2)}, u32[]{:S(2)}) %collective-permute-start.5) | collective-permute-done | bytes 24608 | tf_op jit(solution)/shard_map/ppermute | solution.py:162
  33.5 0.1 slice.30
  33.5 0.1 reverse.2
  33.6 0.1 slice.34
  33.7 0.1 fusion.6
  33.8 0.6 broadcast_in_dim.31.e_ref
  34.4 2.8 %shard_map.47 = bf16[16,6144]{1,0:T(8,128)(2,1)} custom-call(f32[16,6144]{1,0:T(8,128)} %get-tuple-element.7.s_ref, f32[1,6272]{1,0:T(1,128)} %broadcast_in_dim.31.e_ref, f32[1,6144]{1,0:T(1,128)} %bitcast.26, f32[16,1]{1,0:T(8,128)} %copy.5.krow_ref, f32[1,1]{1,0:T(1,128)} %bitcast.3.kt_ref), custom_call_target="tpu_custom_call" | custom-call | tf_op jit(solution)/shard_map/pallas_call | solution.py:56
  37.3 0.9 %copy.9 = bf16[2,16,8,384]{3,2,0,1:T(8,128)(2,1)S(1)} copy(bf16[2,16,8,384]{3,2,1,0:T(8,128)(2,1)} %bitcast.25) | data formatting | bytes 393216 | tf_op jit(solution)/shard_map/all_to_all | solution.py:170
  38.2 14.1 %all_to_all.25 = bf16[16,16,384]{2,0,1:T(8,128)(2,1)S(1)} all-to-all(bf16[16,16,384]{2,0,1:T(8,128)(2,1)S(1)} %bitcast.24), channel_id=1, replica_groups=mesh['groups'=2,'blk'=16] {'blk'}, dimensions={1} | all-to-all | bytes 393216 | tf_op jit(solution)/shard_map/all_to_all | solution.py:170
  52.3 0.2 fusion
  52.6 12.6 %all_to_all.26 = f32[16,16,256]{2,1,0:T(8,128)S(1)} all-to-all(f32[16,16,256]{2,1,0:T(8,128)S(1)} %fusion), channel_id=1, replica_groups=mesh['groups'=2,'blk'=16] {'blk'}, dimensions={0} | all-to-all | bytes 524288 | tf_op jit(solution)/shard_map/all_to_all | solution.py:172
  65.2 1.2 %broadcast_divide_fusion = f32[16,256]{1,0:T(8,128)} fusion(f32[16,256]{1,0:T(8,128)S(1)} %reduce_sum.19, f32[]{:T(128)} %reduce_sum.18), kind=kLoop, calls=%fused_computation.23 | loop fusion | flops 4096 | bytes 32772 | tf_op jit(solution)/shard_map/div | solution.py:220
  (9 shorter events, 0.1 us)
Async XLA Ops:
  0.0 8.8 %copy-start = (f32[16,6144]{1,0:T(8,128)S(1)}, f32[16,6144]{1,0:T(8,128)}, u32[]{:S(2)}) copy-start(f32[16,6144]{1,0:T(8,128)} %param.4) | copy-start | bytes 1179652
  1.1 6.1 %collective-permute-start = (f32[3,6144]{1,0:T(4,128)S(1)}, f32[3,6144]{1,0:T(4,128)S(1)}, u32[]{:S(2)}, u32[]{:S(2)}) collective-permute-start(f32[3,6144]{1,0:T(4,128)S(1)} %get-tuple-element.9), channel_id=1, source_target_pairs={{0,1},{1,2},{2,3},{3,4},{4,5},{5,6},{6,7},{7,8},{8,9},{9,10},{10,1... | collective-permute-start | bytes 221192 | tf_op jit(solution)/shard_map/ppermute | solution.py:72
  3.5 5.3 %collective-permute-start.1 = (f32[3,6144]{1,0:T(4,128)S(1)}, f32[3,6144]{1,0:T(4,128)S(1)}, u32[]{:S(2)}, u32[]{:S(2)}) collective-permute-start(f32[3,6144]{1,0:T(4,128)S(1)} %get-tuple-element.10), channel_id=1, source_target_pairs={{1,0},{2,1},{3,2},{4,3},{5,4},{6,5},{7,6},{8,7},{9,8},{10,9},{11,1... | collective-permute-start | bytes 221192 | tf_op jit(solution)/shard_map/ppermute | solution.py:74
  15.7 4.2 %collective-permute-start.2 = (f32[6144]{0:T(1024)S(1)}, f32[6144]{0:T(1024)S(1)}, u32[]{:S(2)}, u32[]{:S(2)}) collective-permute-start(f32[6144]{0:T(1024)S(1)} %slice_add_fusion), channel_id=1, source_target_pairs={{0,1},{1,0},{2,3},{3,2},{4,5},{5,4},{6,7},{7,6},{8,9},{9,8},{10,11... | collective-permute-start | bytes 73736 | tf_op jit(solution)/shard_map/ppermute | solution.py:162
  19.8 5.8 %copy-start.2 = (s32[384]{0:T(512)S(1)}, s32[384]{0:T(512)}, u32[]{:S(2)}) copy-start(s32[384]{0:T(512)} %param.6) | copy-start | bytes 4612
  19.8 4.2 %collective-permute-start.3 = (f32[6144]{0:T(1024)S(1)}, f32[6144]{0:T(1024)S(1)}, u32[]{:S(2)}, u32[]{:S(2)}) collective-permute-start(f32[6144]{0:T(1024)S(1)} %add.63), channel_id=1, source_target_pairs={{0,2},{1,3},{2,0},{3,1},{4,6},{5,7},{6,4},{7,5},{8,10},{9,11},{10,... | collective-permute-start | bytes 73736 | tf_op jit(solution)/shard_map/ppermute | solution.py:162
  24.1 4.6 %collective-permute-start.4 = (f32[6144]{0:T(1024)S(1)}, f32[6144]{0:T(1024)S(1)}, u32[]{:S(2)}, u32[]{:S(2)}) collective-permute-start(f32[6144]{0:T(1024)S(1)} %add.64), channel_id=1, source_target_pairs={{0,4},{1,5},{2,6},{3,7},{4,0},{5,1},{6,2},{7,3},{8,12},{9,13},{10,... | collective-permute-start | bytes 73736 | tf_op jit(solution)/shard_map/ppermute | solution.py:162
  28.6 2.4 %copy-start.1 = (f32[6144]{0:T(1024)}, f32[6144]{0:T(1024)S(1)}, u32[]{:S(2)}) copy-start(f32[6144]{0:T(1024)S(1)} %scatter_custom_fusion) | copy-start | bytes 73732
  28.6 4.8 %collective-permute-start.5 = (f32[6144]{0:T(1024)S(1)}, f32[6144]{0:T(1024)S(1)}, u32[]{:S(2)}, u32[]{:S(2)}) collective-permute-start(f32[6144]{0:T(1024)S(1)} %add.65), channel_id=1, source_target_pairs={{0,8},{1,9},{2,10},{3,11},{4,12},{5,13},{6,14},{7,15},{8,0},{9,1},... | collective-permute-start | bytes 73736 | tf_op jit(solution)/shard_map/ppermute | solution.py:162

commit v4 on v1

--- a/solution.py
+++ b/solution.py
@@ -63,18 +63,18 @@
 def skewed_map(table, window_first, rows_here, col_count):
     span = col_count + rows_here - 1
     window = lax.dynamic_slice_in_dim(mirrored_table(table), window_first, span)
-    tiled = jnp.tile(window, rows_here + 1)[: rows_here * (span + 1)]
-    shifted = tiled.reshape(rows_here, span + 1)[:, :col_count]
-    return shifted[::-1]
+    tiled = jnp.tile(window, rows_here + 1)
+    flat = tiled[rows_here - 1 : rows_here - 1 + rows_here * (span - 1)]
+    return flat.reshape(rows_here, span - 1)[:, :col_count]
 
 
 def diagonal_totals(smoothed, window_first):
     rows_here = smoothed.shape[0]
     col_count = smoothed.shape[1]
     span = col_count + rows_here - 1
-    flipped = jnp.pad(smoothed[::-1], ((0, 0), (0, rows_here)))
-    flat = flipped.reshape(rows_here * (col_count + rows_here))[: rows_here * span]
-    offsets = jnp.sum(flat.reshape(rows_here, span), axis=0)
+    placed = jnp.pad(smoothed, ((0, 0), (rows_here - 1, 0)))
+    flat = jnp.pad(placed.reshape(rows_here * span), (0, rows_here))
+    offsets = jnp.sum(flat.reshape(rows_here, span + 1), axis=0)[:span]
     spread = lax.dynamic_update_slice_in_dim(
         jnp.zeros((2 * col_count - 1,), jnp.float32), offsets, window_first, 0
     )
@@ -82,14 +82,12 @@
     return spread[col_count - 1 :] + lower
 
 
-def normalize(smoothed, expected_map, kept_rows, kept_cols):
+def normalize(smoothed, expected_map, kept_rows, kept_cols, kept_total):
     ratio = smoothed / expected_map
-    kept_total = jnp.sum(kept_cols)
     row_mean = jnp.sum(ratio * kept_cols[None, :], axis=1, keepdims=True) / kept_total
     centred = (ratio - row_mean) * kept_cols[None, :]
     variance = jnp.sum(centred * centred, axis=1, keepdims=True) / kept_total
-    zscores = (centred * lax.rsqrt(variance + 1e-05) * kept_rows[:, None]).astype(jnp.bfloat16)
-    return (zscores, kept_total)
+    return (centred * lax.rsqrt(variance + 1e-05) * kept_rows[:, None]).astype(jnp.bfloat16)
 
 
 def cross_block(left, right):
@@ -137,7 +135,8 @@
     expected_map = skewed_map(expected, window_first, rows_here, col_count)
     kept_bins = jnp.ones((col_count,), jnp.float32).at[masked_bins].set(0.0)
     kept_rows = lax.dynamic_slice_in_dim(kept_bins, first_bin + first_row, rows_here)
-    zscores, kept_total = normalize(smoothed, expected_map, kept_rows, kept_bins)
+    kept_total = jnp.float32(col_count - masked_bins.shape[0])
+    zscores = normalize(smoothed, expected_map, kept_rows, kept_bins, kept_total)
     return gram_rows(zscores, "blk") / kept_total
 
 

time: 62.9 us -> 58.9 us (0.936)
  other arithmetic: 6.45 us -> 3.72 us
  local copies, waits for them, and re-layouts: 9.23 us -> 7.03 us
  waiting for transfers between devices: 6.51 us -> 7.17 us
    rev x3 -> x0, local copies, waits for them, and re-layouts: 2.31 us -> none  [the longest x2 1.54 us: skewed_map(): return shifted[::-1]]
    div x1, other arithmetic: 1.3 us -> 0.61 us  [shards(): return gram_rows(zscores, 'blk') / kept_total]
    div x1, other arithmetic: 0.69 us -> 0.01 us  [normalize(): jnp.sum(ratio * kept_cols[None, :], axis=1, keepdims=True) / kept_total]
    rsqrt x1, other arithmetic: 0.7 us -> 0.01 us  [normalize(): lax.rsqrt(variance + 1e-05)]
    reduce_sum x2 -> x1, other arithmetic: 0.75 us -> 0.06 us  [diagonal_totals(): offsets = jnp.sum(flat.reshape(rows_here, span + 1), axis=0)[:span]]
    ppermute x1, waiting for transfers between devices: 1.6 us -> 2.26 us  [with_halo(): lax.ppermute(head, axis, [((i + 1) % count, i) for i in range(ends)])]
  transfers between devices with their start and end apart: 6 -> 6, of which waited for: 4 -> 4; matrix products, arithmetic and copies ran while one was open for 9% -> 7% of each run, Pallas kernels for 0% -> 0%
where the time goes in v4:
time: 58.9 us; the launch traced here: 58.6 us
  blocking collectives  25.9 us (44%)
  starting transfers between devices  13.6 us (23%)
  waiting for transfers between devices  7.17 us (12%)
  local copies, waits for them, and re-layouts  7.03 us (12%)
  other arithmetic  3.72 us (6%)
  between operations  0.9 us (2%)
    all_to_all x1, blocking collectives, gram_rows(): columns = lax.all_to_all(zscores, axis, 1, 0, tiled=True)  13.3 us
    all_to_all x1, blocking collectives, gram_rows(): pieces = lax.all_to_all(partial, axis, 0, 0, tiled=True)  12.6 us
    ppermute x4, starting transfers between devices, tree_sum(): lax.ppermute(values, axis, [(i, i ^ step) for i in range(count)])  9.95 us
    ppermute x4, waiting for transfers between devices, tree_sum(): lax.ppermute(values, axis, [(i, i ^ step) for i in range(count)])  4.91 us
    scatter x1, local copies, waits for them, and re-layouts, shards(): kept_bins = jnp.ones((col_count,), jnp.float32).at[masked_bins].set(0.0)  2.95 us
    ppermute x1, starting transfers between devices, with_halo(): lax.ppermute(tail, axis, [(i, (i + 1) % count) for i in range(ends)])  2.4 us
    ppermute x1, waiting for transfers between devices, with_halo(): lax.ppermute(head, axis, [((i + 1) % count, i) for i in range(ends)])  2.26 us
    add x1, other arithmetic, smooth(): smoothed + jnp.where(radius_map == radius, box_sums / float((2 * radius +...  1.51 us
  transfers between devices with their start and end apart: 6, of which 4 were waited for; matrix products, arithmetic and copies ran while one was open for 7% of the time, Pallas kernels for 0%

profile of v4, /device:TPU:0, one launch (start us, length us, event | category | flops | bytes accessed | tf_op | source)
XLA Modules:
  0.0 58.6 jit_solution(13706128706130532576)
XLA Ops:
  0.0 1.1 %fusion.16 = (f32[3,6144]{1,0:T(4,128)S(1)}, f32[3,6144]{1,0:T(4,128)S(1)}) fusion(f32[16,6144]{1,0:T(8,128)} %param.4), kind=kLoop, calls=%fused_computation.57 | loop fusion | bytes 294912 | tf_op jit(solution)/shard_map/slice | solution.py:14
  1.1 2.4 %collective-permute-start = (f32[3,6144]{1,0:T(4,128)S(1)}, f32[3,6144]{1,0:T(4,128)S(1)}, u32[]{:S(2)}, u32[]{:S(2)}) collective-permute-start(f32[3,6144]{1,0:T(4,128)S(1)} %get-tuple-element.10), channel_id=1, source_target_pairs={{0,1},{1,2},{2,3},{3,4},{4,5},{5,6},{6,7},{7,8},{8,9},{9,10},{10,1... | collective-permute-start | bytes 221192 | tf_op jit(solution)/shard_map/ppermute | solution.py:17
  3.5 1.3 %collective-permute-start.1 = (f32[3,6144]{1,0:T(4,128)S(1)}, f32[3,6144]{1,0:T(4,128)S(1)}, u32[]{:S(2)}, u32[]{:S(2)}) collective-permute-start(f32[3,6144]{1,0:T(4,128)S(1)} %get-tuple-element.11), channel_id=1, source_target_pairs={{1,0},{2,1},{3,2},{4,3},{5,4},{6,5},{7,6},{8,7},{9,8},{10,9},{11,1... | collective-permute-start | bytes 221192 | tf_op jit(solution)/shard_map/ppermute | solution.py:19
  5.4 0.1 slice.102
  5.5 0.1 reverse
  5.6 0.1 slice.237
  5.7 0.1 fusion.13
  5.8 0.2 tile.9
  6.1 0.2 slice.135
  6.2 0.0 copy-start
  6.3 0.3 reshape.37
  6.5 0.0 collective-permute-done
  6.5 2.3 %collective-permute-done.1 = f32[3,6144]{1,0:T(4,128)S(1)} collective-permute-done((f32[3,6144]{1,0:T(4,128)S(1)}, f32[3,6144]{1,0:T(4,128)S(1)}, u32[]{:S(2)}, u32[]{:S(2)}) %collective-permute-start.1) | collective-permute-done | bytes 73760 | tf_op jit(solution)/shard_map/ppermute | solution.py:19
  8.8 0.3 select_maximum_fusion
  9.1 0.2 slice_add_fusion
  9.4 1.5 %fusion.3 = f32[16,6144]{1,0:T(8,128)S(1)} fusion(f32[16,6150]{1,0:T(8,128)S(1)} %get-tuple-element.7, f32[16,6150]{1,0:T(8,128)S(1)} %get-tuple-element.8, f32[16,6150]{1,0:T(8,128)S(1)} %get-tuple-element.9, f32[16,6144]{1,0:T(8,128)S(1)} %copy-done, s32[16,6158]{1,0:T(8,128)S(1)} %reshape.37), kind=kLoop, calls=%fused_computation.16 | loop fusion | flops 2555904 | bytes 7077888 | tf_op jit(solution)/shard_map/add | solution.py:45
  10.9 0.2 pad.13
  11.1 0.2 reshape.38
  11.3 0.2 reshape.39
  11.6 0.1 reduce_sum.36
  11.7 0.2 slice_dynamic-update-slice_fusion
  11.9 0.1 reverse.1
  12.0 0.1 slice.238
  12.0 0.1 slice_add_fusion.18
  12.1 3.3 %collective-permute-start.2 = (f32[6144]{0:T(1024)S(1)}, f32[6144]{0:T(1024)S(1)}, u32[]{:S(2)}, u32[]{:S(2)}) collective-permute-start(f32[6144]{0:T(1024)S(1)} %slice_add_fusion.18), channel_id=1, source_target_pairs={{0,1},{1,0},{2,3},{3,2},{4,5},{5,4},{6,7},{7,6},{8,9},{9,8},{10,11... | collective-permute-start | bytes 73736 | tf_op jit(solution)/shard_map/ppermute | solution.py:105
  15.4 0.8 %collective-permute-done.2 = f32[6144]{0:T(1024)S(1)} collective-permute-done((f32[6144]{0:T(1024)S(1)}, f32[6144]{0:T(1024)S(1)}, u32[]{:S(2)}, u32[]{:S(2)}) %collective-permute-start.2) | collective-permute-done | bytes 24608 | tf_op jit(solution)/shard_map/ppermute | solution.py:105
  16.3 2.4 %collective-permute-start.3 = (f32[6144]{0:T(1024)S(1)}, f32[6144]{0:T(1024)S(1)}, u32[]{:S(2)}, u32[]{:S(2)}) collective-permute-start(f32[6144]{0:T(1024)S(1)} %add.145), channel_id=1, source_target_pairs={{0,2},{1,3},{2,0},{3,1},{4,6},{5,7},{6,4},{7,5},{8,10},{9,11},{10,... | collective-permute-start | bytes 73736 | tf_op jit(solution)/shard_map/ppermute | solution.py:105
  18.7 1.8 %collective-permute-done.3 = f32[6144]{0:T(1024)S(1)} collective-permute-done((f32[6144]{0:T(1024)S(1)}, f32[6144]{0:T(1024)S(1)}, u32[]{:S(2)}, u32[]{:S(2)}) %collective-permute-start.3) | collective-permute-done | bytes 24608 | tf_op jit(solution)/shard_map/ppermute | solution.py:105
  20.5 1.6 %collective-permute-start.4 = (f32[6144]{0:T(1024)S(1)}, f32[6144]{0:T(1024)S(1)}, u32[]{:S(2)}, u32[]{:S(2)}) collective-permute-start(f32[6144]{0:T(1024)S(1)} %add.146), channel_id=1, source_target_pairs={{0,4},{1,5},{2,6},{3,7},{4,0},{5,1},{6,2},{7,3},{8,12},{9,13},{10,... | collective-permute-start | bytes 73736 | tf_op jit(solution)/shard_map/ppermute | solution.py:105
  22.2 2.2 %collective-permute-done.4 = f32[6144]{0:T(1024)S(1)} collective-permute-done((f32[6144]{0:T(1024)S(1)}, f32[6144]{0:T(1024)S(1)}, u32[]{:S(2)}, u32[]{:S(2)}) %collective-permute-start.4) | collective-permute-done | bytes 24608 | tf_op jit(solution)/shard_map/ppermute | solution.py:105
  24.4 2.6 %collective-permute-start.5 = (f32[6144]{0:T(1024)S(1)}, f32[6144]{0:T(1024)S(1)}, u32[]{:S(2)}, u32[]{:S(2)}) collective-permute-start(f32[6144]{0:T(1024)S(1)} %add.147), channel_id=1, source_target_pairs={{0,8},{1,9},{2,10},{3,11},{4,12},{5,13},{6,14},{7,15},{8,0},{9,1},... | collective-permute-start | bytes 73736 | tf_op jit(solution)/shard_map/ppermute | solution.py:105
  27.0 2.9 %scatter_custom_fusion = f32[6144]{0:T(1024)S(1)} fusion(s32[384]{0:T(512)S(1)} %compare_select_fusion, f32[384]{0:T(512)S(1)} %broadcast.39, f32[]{:T(128)} %constant.16.clone.1), kind=kCustom, calls=%fused_computation.51 | custom fusion | bytes 24580 | tf_op jit(solution)/shard_map/scatter | solution.py:136
  30.0 0.1 dynamic_slice.11
  30.1 0.0 collective-permute-done.5
  30.1 0.1 slice.162
  30.2 0.1 reverse.2
  30.2 0.1 slice.239
  30.3 0.1 fusion.12
  30.5 0.2 tile.21
  30.7 0.2 slice.163
  30.9 0.3 reshape.40
  31.2 0.2 multiply_reduce_fusion.1
  31.4 0.3 multiply_reduce_fusion
  31.6 0.1 multiply_convert_fusion
  31.8 13.3 %all_to_all.25 = bf16[16,16,384]{2,0,1:T(8,128)(2,1)S(1)} all-to-all(bf16[16,16,384]{2,0,1:T(8,128)(2,1)S(1)} %bitcast.20), channel_id=1, replica_groups=mesh['groups'=2,'blk'=16] {'blk'}, dimensions={1} | all-to-all | bytes 393216 | tf_op jit(solution)/shard_map/all_to_all | solution.py:113
  45.1 0.3 fusion.10
  45.4 12.6 %all_to_all.26 = f32[16,16,256]{2,1,0:T(8,128)S(1)} all-to-all(f32[16,16,256]{2,1,0:T(8,128)S(1)} %fusion.10), channel_id=1, replica_groups=mesh['groups'=2,'blk'=16] {'blk'}, dimensions={0} | all-to-all | bytes 524288 | tf_op jit(solution)/shard_map/all_to_all | solution.py:115
  58.0 0.6 %broadcast_multiply_fusion = f32[16,256]{1,0:T(8,128)} fusion(f32[16,256]{1,0:T(8,128)S(1)} %reduce_sum.39), kind=kLoop, calls=%fused_computation.53 | loop fusion | flops 4096 | bytes 32768 | tf_op jit(solution)/shard_map/div | solution.py:140
  (20 shorter events, 0.2 us)
Async XLA Ops:
  0.0 5.4 %copy-start.1 = (s32[6144]{0:T(1024)S(1)}, s32[6144]{0:T(1024)}, u32[]{:S(2)}) copy-start(s32[6144]{0:T(1024)} %param.5) | copy-start | bytes 73732
  1.1 5.5 %collective-permute-start = (f32[3,6144]{1,0:T(4,128)S(1)}, f32[3,6144]{1,0:T(4,128)S(1)}, u32[]{:S(2)}, u32[]{:S(2)}) collective-permute-start(f32[3,6144]{1,0:T(4,128)S(1)} %get-tuple-element.10), channel_id=1, source_target_pairs={{0,1},{1,2},{2,3},{3,4},{4,5},{5,6},{6,7},{7,8},{8,9},{9,10},{10,1... | collective-permute-start | bytes 221192 | tf_op jit(solution)/shard_map/ppermute | solution.py:17
  3.5 5.3 %collective-permute-start.1 = (f32[3,6144]{1,0:T(4,128)S(1)}, f32[3,6144]{1,0:T(4,128)S(1)}, u32[]{:S(2)}, u32[]{:S(2)}) collective-permute-start(f32[3,6144]{1,0:T(4,128)S(1)} %get-tuple-element.11), channel_id=1, source_target_pairs={{1,0},{2,1},{3,2},{4,3},{5,4},{6,5},{7,6},{8,7},{9,8},{10,9},{11,1... | collective-permute-start | bytes 221192 | tf_op jit(solution)/shard_map/ppermute | solution.py:19
  6.2 2.5 %copy-start = (f32[16,6144]{1,0:T(8,128)S(1)}, f32[16,6144]{1,0:T(8,128)}, u32[]{:S(2)}) copy-start(f32[16,6144]{1,0:T(8,128)} %param.4) | copy-start | bytes 1179652
  12.1 4.2 %collective-permute-start.2 = (f32[6144]{0:T(1024)S(1)}, f32[6144]{0:T(1024)S(1)}, u32[]{:S(2)}, u32[]{:S(2)}) collective-permute-start(f32[6144]{0:T(1024)S(1)} %slice_add_fusion.18), channel_id=1, source_target_pairs={{0,1},{1,0},{2,3},{3,2},{4,5},{5,4},{6,7},{7,6},{8,9},{9,8},{10,11... | collective-permute-start | bytes 73736 | tf_op jit(solution)/shard_map/ppermute | solution.py:105
  16.3 4.2 %collective-permute-start.3 = (f32[6144]{0:T(1024)S(1)}, f32[6144]{0:T(1024)S(1)}, u32[]{:S(2)}, u32[]{:S(2)}) collective-permute-start(f32[6144]{0:T(1024)S(1)} %add.145), channel_id=1, source_target_pairs={{0,2},{1,3},{2,0},{3,1},{4,6},{5,7},{6,4},{7,5},{8,10},{9,11},{10,... | collective-permute-start | bytes 73736 | tf_op jit(solution)/shard_map/ppermute | solution.py:105
  20.5 6.5 %copy-start.2 = (s32[384]{0:T(512)S(1)}, s32[384]{0:T(512)}, u32[]{:S(2)}) copy-start(s32[384]{0:T(512)} %param.6) | copy-start | bytes 4612
  20.5 3.9 %collective-permute-start.4 = (f32[6144]{0:T(1024)S(1)}, f32[6144]{0:T(1024)S(1)}, u32[]{:S(2)}, u32[]{:S(2)}) collective-permute-start(f32[6144]{0:T(1024)S(1)} %add.146), channel_id=1, source_target_pairs={{0,4},{1,5},{2,6},{3,7},{4,0},{5,1},{6,2},{7,3},{8,12},{9,13},{10,... | collective-permute-start | bytes 73736 | tf_op jit(solution)/shard_map/ppermute | solution.py:105
  24.4 5.6 %collective-permute-start.5 = (f32[6144]{0:T(1024)S(1)}, f32[6144]{0:T(1024)S(1)}, u32[]{:S(2)}, u32[]{:S(2)}) collective-permute-start(f32[6144]{0:T(1024)S(1)} %add.147), channel_id=1, source_target_pairs={{0,8},{1,9},{2,10},{3,11},{4,12},{5,13},{6,14},{7,15},{8,0},{9,1},... | collective-permute-start | bytes 73736 | tf_op jit(solution)/shard_map/ppermute | solution.py:105

commit v5 on v2

--- a/solution.py
+++ b/solution.py
@@ -66,18 +66,18 @@
     window = lax.dynamic_slice_in_dim(
         mirrored_table(table, margin), window_first + margin, span
     )
-    tiled = jnp.tile(window, rows_here + 1)[: rows_here * (span + 1)]
-    shifted = tiled.reshape(rows_here, span + 1)[:, :col_count]
-    return shifted[::-1]
+    tiled = jnp.tile(window, rows_here + 1)
+    flat = tiled[rows_here - 1 : rows_here - 1 + rows_here * (span - 1)]
+    return flat.reshape(rows_here, span - 1)[:, :col_count]
 
 
 def diagonal_totals(smoothed, window_first, margin=0):
     rows_here = smoothed.shape[0]
     col_count = smoothed.shape[1]
     span = col_count + rows_here - 1
-    flipped = jnp.pad(smoothed[::-1], ((0, 0), (0, rows_here)))
-    flat = flipped.reshape(rows_here * (col_count + rows_here))[: rows_here * span]
-    offsets = jnp.sum(flat.reshape(rows_here, span), axis=0)
+    placed = jnp.pad(smoothed, ((0, 0), (rows_here - 1, 0)))
+    flat = jnp.pad(placed.reshape(rows_here * span), (0, rows_here))
+    offsets = jnp.sum(flat.reshape(rows_here, span + 1), axis=0)[:span]
     spread = lax.dynamic_update_slice_in_dim(
         jnp.zeros((2 * col_count - 1 + 2 * margin,), jnp.float32),
         offsets,
@@ -88,14 +88,12 @@
     return spread[col_count - 1 :] + lower
 
 
-def normalize(smoothed, expected_map, kept_rows, kept_cols):
+def normalize(smoothed, expected_map, kept_rows, kept_cols, kept_total):
     ratio = smoothed / expected_map
-    kept_total = jnp.sum(kept_cols)
     row_mean = jnp.sum(ratio * kept_cols[None, :], axis=1, keepdims=True) / kept_total
     centred = (ratio - row_mean) * kept_cols[None, :]
     variance = jnp.sum(centred * centred, axis=1, keepdims=True) / kept_total
-    zscores = (centred * lax.rsqrt(variance + 1e-05) * kept_rows[:, None]).astype(jnp.bfloat16)
-    return (zscores, kept_total)
+    return (centred * lax.rsqrt(variance + 1e-05) * kept_rows[:, None]).astype(jnp.bfloat16)
 
 
 def cross_block(left, right):
@@ -141,8 +139,9 @@
     inside = (target >= 0) & (target < nbins)
     own_part = jnp.where(inside[:, None], smooth(own, wide_radius), 0.0)
     local_total = diagonal_totals(own_part, wide_first, WMAX)
+    local_total, later = lax.optimization_barrier((local_total, contacts))
     radius_map = skewed_map(widths, window_first, rows_here, col_count)
-    padded_rows = with_halo(contacts, (("blk", 0),), WMAX)
+    padded_rows = with_halo(later, (("blk", 0),), WMAX)
     padded = jnp.pad(padded_rows, ((0, 0), (WMAX, WMAX)))
     smoothed = smooth(padded, radius_map)
     denominator = pair_counts(first_bin, nbins, col_count)
@@ -150,7 +149,8 @@
     expected_map = skewed_map(expected, window_first, rows_here, col_count)
     kept_bins = jnp.ones((col_count,), jnp.float32).at[masked_bins].set(0.0)
     kept_rows = lax.dynamic_slice_in_dim(kept_bins, first_bin + first_row, rows_here)
-    zscores, kept_total = normalize(smoothed, expected_map, kept_rows, kept_bins)
+    kept_total = jnp.float32(col_count - masked_bins.shape[0])
+    zscores = normalize(smoothed, expected_map, kept_rows, kept_bins, kept_total)
     return gram_rows(zscores, "blk") / kept_total
 
 

time: 69.2 us -> 61.8 us (0.89)
  local copies, waits for them, and re-layouts: 13.4 us -> 10.2 us
  other arithmetic: 9.59 us -> 6.92 us
  starting transfers between devices: 14.5 us -> 13.4 us
    rev x4 -> x0, local copies, waits for them, and re-layouts: 3.99 us -> none  [the longest x3 2.76 us: skewed_map(): return shifted[::-1]]
    slice x1, local copies, waits for them, and re-layouts: 1.06 us -> 0.04 us  [with_halo(): lax.slice_in_dim(cells, cells.shape[dim] - width, cells.shape[dim], axis=...]
    slice x2, local copies, waits for them, and re-layouts: 0.15 us -> 0.96 us  [mirrored_table(): mirrored = jnp.concatenate([table[1:][::-1], table])]
    div x1, other arithmetic: 1.3 us -> 0.61 us  [shards(): return gram_rows(zscores, 'blk') / kept_total]
    div x1, other arithmetic: 0.7 us -> 0.01 us  [normalize(): jnp.sum(ratio * kept_cols[None, :], axis=1, keepdims=True) / kept_total]
  transfers between devices with their start and end apart: 6 -> 6, of which waited for: 3 -> 2; matrix products, arithmetic and copies ran while one was open for 13% -> 7% of each run, Pallas kernels for 0% -> 0%
where the time goes in v5:
time: 61.8 us; the launch traced here: 61.5 us
  blocking collectives  25.4 us (41%)
  starting transfers between devices  13.4 us (22%)
  local copies, waits for them, and re-layouts  10.2 us (17%)
  other arithmetic  6.92 us (11%)
  waiting for transfers between devices  4.3 us (7%)
  between operations  0.97 us (2%)
    all_to_all x1, blocking collectives, gram_rows(): columns = lax.all_to_all(zscores, axis, 1, 0, tiled=True)  12.8 us
    all_to_all x1, blocking collectives, gram_rows(): pieces = lax.all_to_all(partial, axis, 0, 0, tiled=True)  12.6 us
    ppermute x4, starting transfers between devices, tree_sum(): lax.ppermute(values, axis, [(i, i ^ step) for i in range(count)])  10.2 us
    ppermute x4, waiting for transfers between devices, tree_sum(): lax.ppermute(values, axis, [(i, i ^ step) for i in range(count)])  4.29 us
    scatter x1, local copies, waits for them, and re-layouts, shards(): kept_bins = jnp.ones((col_count,), jnp.float32).at[masked_bins].set(0.0)  2.95 us
    select_n x1, other arithmetic, shards(): own_part = jnp.where(inside[:, None], smooth(own, wide_radius), 0.0)  2.2 us
    ppermute x1, starting transfers between devices, with_halo(): lax.ppermute(tail, axis, [(i, (i + 1) % count) for i in range(ends)])  1.93 us
    reduce_sum x1, other arithmetic, normalize(): jnp.sum(ratio * kept_cols[None, :], axis=1, keepdims=True) / kept_total  1.61 us
  transfers between devices with their start and end apart: 6, of which 2 were waited for; matrix products, arithmetic and copies ran while one was open for 7% of the time, Pallas kernels for 0%

profile of v5, /device:TPU:0, one launch (start us, length us, event | category | flops | bytes accessed | tf_op | source)
XLA Modules:
  0.0 61.5 jit_solution(10037246201385059545)
XLA Ops:
  0.0 0.9 %slice.194 = s32[6143]{0:T(1024)S(1)} slice(s32[6144]{0:T(1024)} %param.5), slice={[1:6144]} | slice | bytes 49144 | tf_op jit(solution)/shard_map/slice | solution.py:60
  0.9 0.7 %slice.197 = s32[1]{0:T(128)} slice(s32[6144]{0:T(1024)S(1)} %copy-done.1), slice={[6143:6144]} | slice | bytes 8 | tf_op jit(solution)/shard_map/jit(_pad)/slice | solution.py:61
  2.2 0.1 reverse.1
  2.3 0.1 slice.465
  2.4 0.7 %reshape.57 = s32[3]{0:T(128)S(1)} broadcast(s32[]{:T(128)} %bitcast.1), dimensions={} | broadcast | bytes 16 | tf_op jit(solution)/shard_map/jit(_pad)/reshape | solution.py:61
  3.1 0.1 concatenate.19
  3.2 0.1 dynamic_slice.13
  3.3 0.3 tile.30
  3.6 0.2 slice.256
  3.8 0.4 reshape.58
  4.2 0.6 %copy-done = f32[16,6144]{1,0:T(8,128)S(1)} copy-done((f32[16,6144]{1,0:T(8,128)S(1)}, f32[16,6144]{1,0:T(8,128)}, u32[]{:S(2)}) %copy-start) | copy-done | bytes 393240
  4.8 1.1 %fusion.5 = (f32[22,6150]{1,0:T(8,128)S(1)}, f32[22,6150]{1,0:T(8,128)S(1)}, f32[22,6150]{1,0:T(8,128)S(1)}) fusion(f32[16,6144]{1,0:T(8,128)S(1)} %copy-done), kind=kLoop, calls=%fused_computation.16 | loop fusion | flops 811800 | bytes 2016816 | tf_op jit(solution)/shard_map/add | solution.py:34
  5.9 2.2 %fusion.11 = f32[22,6144]{1,0:T(8,128)S(1)} fusion(f32[16,6144]{1,0:T(8,128)S(1)} %copy-done, f32[22,6150]{1,0:T(8,128)S(1)} %get-tuple-element.14, f32[22,6150]{1,0:T(8,128)S(1)} %get-tuple-element.15, f32[22,6150]{1,0:T(8,128)S(1)} %get-tuple-element.16, s32[22,6164]{1,0:T(8,128)S(1)} %reshape.58, pred[22]{0:T(512)(128)(4,1)S(1)} %compare_and_fusion), kind=kLoop, calls=%fused_computation.24 | loop fusion | flops 3649536 | bytes 9584662 | tf_op jit(solution)/shard_map/jit(_where)/select_n | solution.py:140
  8.2 0.2 pad.17
  8.4 0.3 reshape.59
  8.7 0.4 reshape.60
  9.2 0.2 slice_dynamic-update-slice_fusion
  9.5 0.1 reverse.2
  9.6 0.1 slice_add_fusion.30
  9.7 0.6 collective-permute-start.2
  10.3 1.9 %collective-permute-start = (f32[3,6144]{1,0:T(4,128)S(1)}, f32[3,6144]{1,0:T(4,128)S(1)}, u32[]{:S(2)}, u32[]{:S(2)}) collective-permute-start(f32[3,6144]{1,0:T(4,128)S(1)} %get-tuple-element.17), channel_id=1, source_target_pairs={{0,1},{1,2},{2,3},{3,4},{4,5},{5,6},{6,7},{7,8},{8,9},{9,10},{10,1... | collective-permute-start | bytes 221192 | tf_op jit(solution)/shard_map/ppermute | solution.py:17
  12.3 1.3 %collective-permute-start.1 = (f32[3,6144]{1,0:T(4,128)S(1)}, f32[3,6144]{1,0:T(4,128)S(1)}, u32[]{:S(2)}, u32[]{:S(2)}) collective-permute-start(f32[3,6144]{1,0:T(4,128)S(1)} %get-tuple-element.18), channel_id=1, source_target_pairs={{1,0},{2,1},{3,2},{4,3},{5,4},{6,5},{7,6},{8,7},{9,8},{10,9},{11,1... | collective-permute-start | bytes 221192 | tf_op jit(solution)/shard_map/ppermute | solution.py:19
  13.6 4.9 %collective-permute-start.3 = (f32[6144]{0:T(1024)S(1)}, f32[6144]{0:T(1024)S(1)}, u32[]{:S(2)}, u32[]{:S(2)}) collective-permute-start(f32[6144]{0:T(1024)S(1)} %add.256), channel_id=1, source_target_pairs={{0,2},{1,3},{2,0},{3,1},{4,6},{5,7},{6,4},{7,5},{8,10},{9,11},{10,... | collective-permute-start | bytes 73736 | tf_op jit(solution)/shard_map/ppermute | solution.py:111
  18.5 2.7 %collective-permute-done.3 = f32[6144]{0:T(1024)S(1)} collective-permute-done((f32[6144]{0:T(1024)S(1)}, f32[6144]{0:T(1024)S(1)}, u32[]{:S(2)}, u32[]{:S(2)}) %collective-permute-start.3) | collective-permute-done | bytes 24608 | tf_op jit(solution)/shard_map/ppermute | solution.py:111
  21.3 2.0 %collective-permute-start.4 = (f32[6144]{0:T(1024)S(1)}, f32[6144]{0:T(1024)S(1)}, u32[]{:S(2)}, u32[]{:S(2)}) collective-permute-start(f32[6144]{0:T(1024)S(1)} %add.257), channel_id=1, source_target_pairs={{0,4},{1,5},{2,6},{3,7},{4,0},{5,1},{6,2},{7,3},{8,12},{9,13},{10,... | collective-permute-start | bytes 73736 | tf_op jit(solution)/shard_map/ppermute | solution.py:111
  23.3 0.1 fusion.30
  23.5 0.2 tile.13
  23.7 0.2 slice.254
  23.9 0.3 reshape.56
  24.2 3.0 %scatter_custom_fusion = f32[6144]{0:T(1024)S(1)} fusion(s32[384]{0:T(512)S(1)} %compare_select_fusion, f32[384]{0:T(512)S(1)} %broadcast.69, f32[]{:T(128)} %constant.39.clone.1), kind=kCustom, calls=%fused_computation.88 | custom fusion | bytes 24580 | tf_op jit(solution)/shard_map/scatter | solution.py:150
  27.1 0.1 dynamic_slice.15
  27.2 2.6 %collective-permute-start.5 = (f32[6144]{0:T(1024)S(1)}, f32[6144]{0:T(1024)S(1)}, u32[]{:S(2)}, u32[]{:S(2)}) collective-permute-start(f32[6144]{0:T(1024)S(1)} %add.258), channel_id=1, source_target_pairs={{0,8},{1,9},{2,10},{3,11},{4,12},{5,13},{6,14},{7,15},{8,0},{9,1},... | collective-permute-start | bytes 73736 | tf_op jit(solution)/shard_map/ppermute | solution.py:111
  29.9 0.3 select_maximum_fusion
  30.2 0.2 slice_add_fusion.12
  30.5 1.6 %collective-permute-done.5 = f32[6144]{0:T(1024)S(1)} collective-permute-done((f32[6144]{0:T(1024)S(1)}, f32[6144]{0:T(1024)S(1)}, u32[]{:S(2)}, u32[]{:S(2)}) %collective-permute-start.5) | collective-permute-done | bytes 24608 | tf_op jit(solution)/shard_map/ppermute | solution.py:111
  32.1 0.1 reverse.3
  32.2 0.1 slice.467
  32.3 0.1 fusion.29
  32.4 0.2 tile.32
  32.7 0.2 slice.299
  32.8 0.3 reshape.61
  33.1 1.6 %multiply_reduce_fusion.1 = (f32[16]{0:T(128)S(1)}, f32[16,6144]{1,0:T(8,128)S(1)}) fusion(f32[6144]{0:T(1024)S(1)} %scatter_custom_fusion, f32[16,6158]{1,0:T(8,128)S(1)} %reshape.61, f32[16,6150]{1,0:T(8,128)S(1)} %get-tuple-element.11, f32[16,6150]{1,0:T(8,128)S(1)} %get-tuple-element.12, f32[16,6150]{1,0:T(8,128)S(1)} %get-tuple-element.13, ...), kind=kLoop, calls=%fused_computation.74 | loop fusion | flops 2850800 | bytes 7495744 | tf_op jit(solution)/shard_map/reduce_sum | solution.py:93
  34.7 0.3 multiply_reduce_fusion
  35.0 0.1 multiply_convert_fusion
  35.2 12.8 %all_to_all.25 = bf16[16,16,384]{2,0,1:T(8,128)(2,1)S(1)} all-to-all(bf16[16,16,384]{2,0,1:T(8,128)(2,1)S(1)} %bitcast.21), channel_id=1, replica_groups=mesh['groups'=2,'blk'=16] {'blk'}, dimensions={1} | all-to-all | bytes 393216 | tf_op jit(solution)/shard_map/all_to_all | solution.py:119
  48.0 0.3 fusion.27
  48.2 12.6 %all_to_all.26 = f32[16,16,256]{2,1,0:T(8,128)S(1)} all-to-all(f32[16,16,256]{2,1,0:T(8,128)S(1)} %fusion.27), channel_id=1, replica_groups=mesh['groups'=2,'blk'=16] {'blk'}, dimensions={0} | all-to-all | bytes 524288 | tf_op jit(solution)/shard_map/all_to_all | solution.py:121
  60.8 0.6 broadcast_multiply_fusion
  (30 shorter events, 0.6 us)
Async XLA Ops:
  0.0 0.9 %copy-start.1 = (s32[6144]{0:T(1024)S(1)}, s32[6144]{0:T(1024)}, u32[]{:S(2)}) copy-start(s32[6144]{0:T(1024)} %param.5) | copy-start | bytes 73732
  3.8 1.0 %copy-start = (f32[16,6144]{1,0:T(8,128)S(1)}, f32[16,6144]{1,0:T(8,128)}, u32[]{:S(2)}) copy-start(f32[16,6144]{1,0:T(8,128)} %param.4) | copy-start | bytes 1179652
  9.7 3.8 %collective-permute-start.2 = (f32[6144]{0:T(1024)S(1)}, f32[6144]{0:T(1024)S(1)}, u32[]{:S(2)}, u32[]{:S(2)}) collective-permute-start(f32[6144]{0:T(1024)S(1)} %slice_add_fusion.30), channel_id=1, source_target_pairs={{0,1},{1,0},{2,3},{3,2},{4,5},{5,4},{6,7},{7,6},{8,9},{9,8},{10,11... | collective-permute-start | bytes 73736 | tf_op jit(solution)/shard_map/ppermute | solution.py:111
  10.3 19.6 %collective-permute-start = (f32[3,6144]{1,0:T(4,128)S(1)}, f32[3,6144]{1,0:T(4,128)S(1)}, u32[]{:S(2)}, u32[]{:S(2)}) collective-permute-start(f32[3,6144]{1,0:T(4,128)S(1)} %get-tuple-element.17), channel_id=1, source_target_pairs={{0,1},{1,2},{2,3},{3,4},{4,5},{5,6},{6,7},{7,8},{8,9},{9,10},{10,1... | collective-permute-start | bytes 221192 | tf_op jit(solution)/shard_map/ppermute | solution.py:17
  12.3 6.3 %copy-start.2 = (s32[384]{0:T(512)S(1)}, s32[384]{0:T(512)}, u32[]{:S(2)}) copy-start(s32[384]{0:T(512)} %param.6) | copy-start | bytes 4612
  12.3 17.6 %collective-permute-start.1 = (f32[3,6144]{1,0:T(4,128)S(1)}, f32[3,6144]{1,0:T(4,128)S(1)}, u32[]{:S(2)}, u32[]{:S(2)}) collective-permute-start(f32[3,6144]{1,0:T(4,128)S(1)} %get-tuple-element.18), channel_id=1, source_target_pairs={{1,0},{2,1},{3,2},{4,3},{5,4},{6,5},{7,6},{8,7},{9,8},{10,9},{11,1... | collective-permute-start | bytes 221192 | tf_op jit(solution)/shard_map/ppermute | solution.py:19
  13.6 7.7 %collective-permute-start.3 = (f32[6144]{0:T(1024)S(1)}, f32[6144]{0:T(1024)S(1)}, u32[]{:S(2)}, u32[]{:S(2)}) collective-permute-start(f32[6144]{0:T(1024)S(1)} %add.256), channel_id=1, source_target_pairs={{0,2},{1,3},{2,0},{3,1},{4,6},{5,7},{6,4},{7,5},{8,10},{9,11},{10,... | collective-permute-start | bytes 73736 | tf_op jit(solution)/shard_map/ppermute | solution.py:111
  21.3 5.9 %collective-permute-start.4 = (f32[6144]{0:T(1024)S(1)}, f32[6144]{0:T(1024)S(1)}, u32[]{:S(2)}, u32[]{:S(2)}) collective-permute-start(f32[6144]{0:T(1024)S(1)} %add.257), channel_id=1, source_target_pairs={{0,4},{1,5},{2,6},{3,7},{4,0},{5,1},{6,2},{7,3},{8,12},{9,13},{10,... | collective-permute-start | bytes 73736 | tf_op jit(solution)/shard_map/ppermute | solution.py:111
  27.2 4.8 %collective-permute-start.5 = (f32[6144]{0:T(1024)S(1)}, f32[6144]{0:T(1024)S(1)}, u32[]{:S(2)}, u32[]{:S(2)}) collective-permute-start(f32[6144]{0:T(1024)S(1)} %add.258), channel_id=1, source_target_pairs={{0,8},{1,9},{2,10},{3,11},{4,12},{5,13},{6,14},{7,15},{8,0},{9,1},... | collective-permute-start | bytes 73736 | tf_op jit(solution)/shard_map/ppermute | solution.py:111

commit v6 on v4

--- a/solution.py
+++ b/solution.py
@@ -126,14 +126,16 @@
     first_bin = row_start[0]
     window_first = col_count - 1 - (first_bin + first_row + rows_here - 1)
     radius_map = skewed_map(widths, window_first, rows_here, col_count)
-    padded_rows = with_halo(contacts, (("blk", 0),), WMAX)
+    kept_bins = jnp.ones((col_count,), jnp.float32).at[masked_bins].set(0.0)
+    padded_rows, kept_bins = lax.optimization_barrier(
+        (with_halo(contacts, (("blk", 0),), WMAX), kept_bins)
+    )
     padded = jnp.pad(padded_rows, ((0, 0), (WMAX, WMAX)))
     smoothed = smooth(padded, radius_map)
     local_total = diagonal_totals(smoothed, window_first)
     denominator = pair_counts(first_bin, nbins, col_count)
     expected = tree_sum(local_total, "blk") / denominator
     expected_map = skewed_map(expected, window_first, rows_here, col_count)
-    kept_bins = jnp.ones((col_count,), jnp.float32).at[masked_bins].set(0.0)
     kept_rows = lax.dynamic_slice_in_dim(kept_bins, first_bin + first_row, rows_here)
     kept_total = jnp.float32(col_count - masked_bins.shape[0])
     zscores = normalize(smoothed, expected_map, kept_rows, kept_bins, kept_total)

time: 58.9 us -> 61.1 us (1.037)
  starting transfers between devices: 13.6 us -> 14.9 us
  blocking collectives: 25.9 us -> 26.9 us
  waiting for transfers between devices: 7.17 us -> 6.25 us
    ppermute x1, waiting for transfers between devices: 2.26 us -> 0.01 us  [with_halo(): lax.ppermute(head, axis, [((i + 1) % count, i) for i in range(ends)])]
    ppermute x4, waiting for transfers between devices: 4.91 us -> 6.24 us  [tree_sum(): lax.ppermute(values, axis, [(i, i ^ step) for i in range(count)])]
    ppermute x4, starting transfers between devices: 9.95 us -> 11.2 us  [tree_sum(): lax.ppermute(values, axis, [(i, i ^ step) for i in range(count)])]
    all_to_all x1, blocking collectives: 13.3 us -> 14.3 us  [gram_rows(): columns = lax.all_to_all(zscores, axis, 1, 0, tiled=True)]
where the time goes in v6:
time: 61.1 us; the launch traced here: 60.9 us
  blocking collectives  26.9 us (44%)
  starting transfers between devices  14.9 us (24%)
  local copies, waits for them, and re-layouts  7.64 us (13%)
  waiting for transfers between devices  6.25 us (10%)
  other arithmetic  3.99 us (7%)
  between operations  0.92 us (2%)
    all_to_all x1, blocking collectives, gram_rows(): columns = lax.all_to_all(zscores, axis, 1, 0, tiled=True)  14.3 us
    all_to_all x1, blocking collectives, gram_rows(): pieces = lax.all_to_all(partial, axis, 0, 0, tiled=True)  12.6 us
    ppermute x4, starting transfers between devices, tree_sum(): lax.ppermute(values, axis, [(i, i ^ step) for i in range(count)])  11.2 us
    ppermute x4, waiting for transfers between devices, tree_sum(): lax.ppermute(values, axis, [(i, i ^ step) for i in range(count)])  6.24 us
    scatter x1, local copies, waits for them, and re-layouts, shards(): kept_bins = jnp.ones((col_count,), jnp.float32).at[masked_bins].set(0.0)  2.95 us
    ppermute x1, starting transfers between devices, with_halo(): lax.ppermute(tail, axis, [(i, (i + 1) % count) for i in range(ends)])  2.4 us
    add x1, other arithmetic, smooth(): smoothed + jnp.where(radius_map == radius, box_sums / float((2 * radius +...  1.49 us
    ppermute x1, starting transfers between devices, with_halo(): lax.ppermute(head, axis, [((i + 1) % count, i) for i in range(ends)])  1.29 us
  transfers between devices with their start and end apart: 6, of which 4 were waited for; matrix products, arithmetic and copies ran while one was open for 7% of the time, Pallas kernels for 0%

profile of v6, /device:TPU:0, one launch (start us, length us, event | category | flops | bytes accessed | tf_op | source)
XLA Modules:
  0.0 60.9 jit_solution(14913272261202544670)
XLA Ops:
  0.0 1.1 %fusion.23 = (f32[3,6144]{1,0:T(4,128)S(1)}, f32[3,6144]{1,0:T(4,128)S(1)}) fusion(f32[16,6144]{1,0:T(8,128)} %param.4), kind=kLoop, calls=%fused_computation.60 | loop fusion | bytes 294912 | tf_op jit(solution)/shard_map/slice | solution.py:14
  1.1 2.4 %collective-permute-start = (f32[3,6144]{1,0:T(4,128)S(1)}, f32[3,6144]{1,0:T(4,128)S(1)}, u32[]{:S(2)}, u32[]{:S(2)}) collective-permute-start(f32[3,6144]{1,0:T(4,128)S(1)} %get-tuple-element.14), channel_id=1, source_target_pairs={{0,1},{1,2},{2,3},{3,4},{4,5},{5,6},{6,7},{7,8},{8,9},{9,10},{10,1... | collective-permute-start | bytes 221192 | tf_op jit(solution)/shard_map/ppermute | solution.py:17
  3.5 1.3 %collective-permute-start.1 = (f32[3,6144]{1,0:T(4,128)S(1)}, f32[3,6144]{1,0:T(4,128)S(1)}, u32[]{:S(2)}, u32[]{:S(2)}) collective-permute-start(f32[3,6144]{1,0:T(4,128)S(1)} %get-tuple-element.15), channel_id=1, source_target_pairs={{1,0},{2,1},{3,2},{4,3},{5,4},{6,5},{7,6},{8,7},{9,8},{10,9},{11,1... | collective-permute-start | bytes 221192 | tf_op jit(solution)/shard_map/ppermute | solution.py:19
  5.4 0.1 slice.104
  5.5 0.1 reverse
  5.6 0.1 slice.248
  5.7 0.6 copy-done.2
  6.3 0.1 fusion.18
  6.4 0.2 tile.9
  6.7 0.2 slice.138
  6.9 0.0 copy-start
  6.9 0.3 reshape.37
  7.1 3.0 %scatter_custom_fusion = f32[6144]{0:T(1024)S(1)} fusion(s32[384]{0:T(512)S(1)} %compare_select_fusion, f32[384]{0:T(512)S(1)} %broadcast.39, f32[]{:T(128)} %constant.25.clone.1), kind=kCustom, calls=%fused_computation.54 | custom fusion | bytes 24580 | tf_op jit(solution)/shard_map/scatter | solution.py:129
  10.1 0.0 collective-permute-done
  10.1 0.1 pad_maximum_fusion
  10.2 0.8 %fusion.5 = (f32[16,6150]{1,0:T(8,128)S(1)}, f32[16,6150]{1,0:T(8,128)S(1)}, f32[16,6150]{1,0:T(8,128)S(1)}) fusion(f32[22,6144]{1,0:T(8,128)S(1)} %pad_maximum_fusion), kind=kLoop, calls=%fused_computation.14 | loop fusion | flops 590400 | bytes 1721472 | tf_op jit(solution)/shard_map/add | solution.py:34
  11.0 1.5 %fusion.8 = f32[16,6144]{1,0:T(8,128)S(1)} fusion(f32[16,6150]{1,0:T(8,128)S(1)} %get-tuple-element.11, f32[16,6150]{1,0:T(8,128)S(1)} %get-tuple-element.12, f32[16,6150]{1,0:T(8,128)S(1)} %get-tuple-element.13, f32[22,6144]{1,0:T(8,128)S(1)} %pad_maximum_fusion, s32[16,6158]{1,0:T(8,128)S(1)} %reshape.37), kind=kLoop, calls=%fused_computation.19 | loop fusion | flops 2555904 | bytes 7077888 | tf_op jit(solution)/shard_map/add | solution.py:45
  12.5 0.2 pad.13
  12.7 0.2 reshape.38
  12.9 0.2 reshape.39
  13.2 0.1 reduce_sum.36
  13.3 0.2 slice_dynamic-update-slice_fusion
  13.5 0.1 reverse.1
  13.6 0.1 slice.249
  13.7 0.1 slice_add_fusion.12
  13.8 3.3 %collective-permute-start.2 = (f32[6144]{0:T(1024)S(1)}, f32[6144]{0:T(1024)S(1)}, u32[]{:S(2)}, u32[]{:S(2)}) collective-permute-start(f32[6144]{0:T(1024)S(1)} %slice_add_fusion.12), channel_id=1, source_target_pairs={{0,1},{1,0},{2,3},{3,2},{4,5},{5,4},{6,7},{7,6},{8,9},{9,8},{10,11... | collective-permute-start | bytes 73736 | tf_op jit(solution)/shard_map/ppermute | solution.py:105
  17.1 0.8 %collective-permute-done.2 = f32[6144]{0:T(1024)S(1)} collective-permute-done((f32[6144]{0:T(1024)S(1)}, f32[6144]{0:T(1024)S(1)}, u32[]{:S(2)}, u32[]{:S(2)}) %collective-permute-start.2) | collective-permute-done | bytes 24608 | tf_op jit(solution)/shard_map/ppermute | solution.py:105
  17.9 2.0 %collective-permute-start.3 = (f32[6144]{0:T(1024)S(1)}, f32[6144]{0:T(1024)S(1)}, u32[]{:S(2)}, u32[]{:S(2)}) collective-permute-start(f32[6144]{0:T(1024)S(1)} %add.147), channel_id=1, source_target_pairs={{0,2},{1,3},{2,0},{3,1},{4,6},{5,7},{6,4},{7,5},{8,10},{9,11},{10,... | collective-permute-start | bytes 73736 | tf_op jit(solution)/shard_map/ppermute | solution.py:105
  19.9 1.9 %collective-permute-done.3 = f32[6144]{0:T(1024)S(1)} collective-permute-done((f32[6144]{0:T(1024)S(1)}, f32[6144]{0:T(1024)S(1)}, u32[]{:S(2)}, u32[]{:S(2)}) %collective-permute-start.3) | collective-permute-done | bytes 24608 | tf_op jit(solution)/shard_map/ppermute | solution.py:105
  21.8 2.9 %collective-permute-start.4 = (f32[6144]{0:T(1024)S(1)}, f32[6144]{0:T(1024)S(1)}, u32[]{:S(2)}, u32[]{:S(2)}) collective-permute-start(f32[6144]{0:T(1024)S(1)} %add.148), channel_id=1, source_target_pairs={{0,4},{1,5},{2,6},{3,7},{4,0},{5,1},{6,2},{7,3},{8,12},{9,13},{10,... | collective-permute-start | bytes 73736 | tf_op jit(solution)/shard_map/ppermute | solution.py:105
  24.7 1.8 %collective-permute-done.4 = f32[6144]{0:T(1024)S(1)} collective-permute-done((f32[6144]{0:T(1024)S(1)}, f32[6144]{0:T(1024)S(1)}, u32[]{:S(2)}, u32[]{:S(2)}) %collective-permute-start.4) | collective-permute-done | bytes 24608 | tf_op jit(solution)/shard_map/ppermute | solution.py:105
  26.5 3.0 %collective-permute-start.5 = (f32[6144]{0:T(1024)S(1)}, f32[6144]{0:T(1024)S(1)}, u32[]{:S(2)}, u32[]{:S(2)}) collective-permute-start(f32[6144]{0:T(1024)S(1)} %add.149), channel_id=1, source_target_pairs={{0,8},{1,9},{2,10},{3,11},{4,12},{5,13},{6,14},{7,15},{8,0},{9,1},... | collective-permute-start | bytes 73736 | tf_op jit(solution)/shard_map/ppermute | solution.py:105
  29.5 0.1 dynamic_slice.11
  29.6 1.7 %collective-permute-done.5 = f32[6144]{0:T(1024)S(1)} collective-permute-done((f32[6144]{0:T(1024)S(1)}, f32[6144]{0:T(1024)S(1)}, u32[]{:S(2)}, u32[]{:S(2)}) %collective-permute-start.5) | collective-permute-done | bytes 24608 | tf_op jit(solution)/shard_map/ppermute | solution.py:105
  31.3 0.1 slice.158
  31.4 0.1 reverse.2
  31.5 0.1 slice.250
  31.6 0.1 fusion.17
  31.7 0.2 tile.21
  32.0 0.2 slice.159
  32.2 0.3 reshape.40
  32.4 0.2 multiply_reduce_fusion.1
  32.6 0.3 multiply_reduce_fusion
  32.9 0.1 multiply_convert_fusion
  33.1 14.3 %all_to_all.25 = bf16[16,16,384]{2,0,1:T(8,128)(2,1)S(1)} all-to-all(bf16[16,16,384]{2,0,1:T(8,128)(2,1)S(1)} %bitcast.20), channel_id=1, replica_groups=mesh['groups'=2,'blk'=16] {'blk'}, dimensions={1} | all-to-all | bytes 393216 | tf_op jit(solution)/shard_map/all_to_all | solution.py:113
  47.4 0.3 fusion.15
  47.6 12.6 %all_to_all.26 = f32[16,16,256]{2,1,0:T(8,128)S(1)} all-to-all(f32[16,16,256]{2,1,0:T(8,128)S(1)} %fusion.15), channel_id=1, replica_groups=mesh['groups'=2,'blk'=16] {'blk'}, dimensions={0} | all-to-all | bytes 524288 | tf_op jit(solution)/shard_map/all_to_all | solution.py:115
  60.3 0.6 broadcast_multiply_fusion
  (20 shorter events, 0.2 us)
Async XLA Ops:
  0.0 5.4 %copy-start.1 = (s32[6144]{0:T(1024)S(1)}, s32[6144]{0:T(1024)}, u32[]{:S(2)}) copy-start(s32[6144]{0:T(1024)} %param.5) | copy-start | bytes 73732
  1.1 9.0 %collective-permute-start = (f32[3,6144]{1,0:T(4,128)S(1)}, f32[3,6144]{1,0:T(4,128)S(1)}, u32[]{:S(2)}, u32[]{:S(2)}) collective-permute-start(f32[3,6144]{1,0:T(4,128)S(1)} %get-tuple-element.14), channel_id=1, source_target_pairs={{0,1},{1,2},{2,3},{3,4},{4,5},{5,6},{6,7},{7,8},{8,9},{9,10},{10,1... | collective-permute-start | bytes 221192 | tf_op jit(solution)/shard_map/ppermute | solution.py:17
  3.5 6.6 %collective-permute-start.1 = (f32[3,6144]{1,0:T(4,128)S(1)}, f32[3,6144]{1,0:T(4,128)S(1)}, u32[]{:S(2)}, u32[]{:S(2)}) collective-permute-start(f32[3,6144]{1,0:T(4,128)S(1)} %get-tuple-element.15), channel_id=1, source_target_pairs={{1,0},{2,1},{3,2},{4,3},{5,4},{6,5},{7,6},{8,7},{9,8},{10,9},{11,1... | collective-permute-start | bytes 221192 | tf_op jit(solution)/shard_map/ppermute | solution.py:19
  5.6 0.7 %copy-start.2 = (s32[384]{0:T(512)S(1)}, s32[384]{0:T(512)}, u32[]{:S(2)}) copy-start(s32[384]{0:T(512)} %param.6) | copy-start | bytes 4612
  6.9 3.3 %copy-start = (f32[16,6144]{1,0:T(8,128)S(1)}, f32[16,6144]{1,0:T(8,128)}, u32[]{:S(2)}) copy-start(f32[16,6144]{1,0:T(8,128)} %param.4) | copy-start | bytes 1179652
  13.8 4.2 %collective-permute-start.2 = (f32[6144]{0:T(1024)S(1)}, f32[6144]{0:T(1024)S(1)}, u32[]{:S(2)}, u32[]{:S(2)}) collective-permute-start(f32[6144]{0:T(1024)S(1)} %slice_add_fusion.12), channel_id=1, source_target_pairs={{0,1},{1,0},{2,3},{3,2},{4,5},{5,4},{6,7},{7,6},{8,9},{9,8},{10,11... | collective-permute-start | bytes 73736 | tf_op jit(solution)/shard_map/ppermute | solution.py:105
  17.9 3.8 %collective-permute-start.3 = (f32[6144]{0:T(1024)S(1)}, f32[6144]{0:T(1024)S(1)}, u32[]{:S(2)}, u32[]{:S(2)}) collective-permute-start(f32[6144]{0:T(1024)S(1)} %add.147), channel_id=1, source_target_pairs={{0,2},{1,3},{2,0},{3,1},{4,6},{5,7},{6,4},{7,5},{8,10},{9,11},{10,... | collective-permute-start | bytes 73736 | tf_op jit(solution)/shard_map/ppermute | solution.py:105
  21.8 4.7 %collective-permute-start.4 = (f32[6144]{0:T(1024)S(1)}, f32[6144]{0:T(1024)S(1)}, u32[]{:S(2)}, u32[]{:S(2)}) collective-permute-start(f32[6144]{0:T(1024)S(1)} %add.148), channel_id=1, source_target_pairs={{0,4},{1,5},{2,6},{3,7},{4,0},{5,1},{6,2},{7,3},{8,12},{9,13},{10,... | collective-permute-start | bytes 73736 | tf_op jit(solution)/shard_map/ppermute | solution.py:105
  26.5 4.8 %collective-permute-start.5 = (f32[6144]{0:T(1024)S(1)}, f32[6144]{0:T(1024)S(1)}, u32[]{:S(2)}, u32[]{:S(2)}) collective-permute-start(f32[6144]{0:T(1024)S(1)} %add.149), channel_id=1, source_target_pairs={{0,8},{1,9},{2,10},{3,11},{4,12},{5,13},{6,14},{7,15},{8,0},{9,1},... | collective-permute-start | bytes 73736 | tf_op jit(solution)/shard_map/ppermute | solution.py:105

commit v7 on v4

--- a/solution.py
+++ b/solution.py
@@ -9,17 +9,26 @@
 def with_halo(cells, sides, width):
     for axis, dim in sides:
         count = lax.axis_size(axis)
-        ends = count - 1
         head = lax.slice_in_dim(cells, 0, width, axis=dim)
         tail = lax.slice_in_dim(cells, cells.shape[dim] - width, cells.shape[dim], axis=dim)
-        cells = jnp.concatenate(
-            [
-                lax.ppermute(tail, axis, [(i, (i + 1) % count) for i in range(ends)]),
-                cells,
-                lax.ppermute(head, axis, [((i + 1) % count, i) for i in range(ends)]),
-            ],
-            axis=dim,
-        )
+        if count % 2:
+            ends = count - 1
+            before = lax.ppermute(tail, axis, [(i, (i + 1) % count) for i in range(ends)])
+            after = lax.ppermute(head, axis, [((i + 1) % count, i) for i in range(ends)])
+        else:
+            odd = lax.axis_index(axis) % 2 == 1
+            inner = lax.ppermute(
+                jnp.where(odd, head, tail), axis, [(i, i ^ 1) for i in range(count)]
+            )
+            outer = lax.ppermute(
+                jnp.where(odd, tail, head),
+                axis,
+                [(i, i - 1) for i in range(2, count, 2)]
+                + [(i, i + 1) for i in range(1, count - 1, 2)],
+            )
+            before = jnp.where(odd, inner, outer)
+            after = jnp.where(odd, outer, inner)
+        cells = jnp.concatenate([before, cells, after], axis=dim)
     return cells
 
 

time: 58.9 us -> 56.3 us (0.956)
  waiting for transfers between devices: 7.17 us -> 4.47 us
  other arithmetic: 3.72 us -> 4.8 us
    ppermute x2, starting transfers between devices: 3.69 us -> 1.21 us  [the longest x1 0.65 us: with_halo(): lax.ppermute(jnp.where(odd, tail, head), axis, [(i, i - 1) for i in range...]
    ppermute x2, waiting for transfers between devices: 2.26 us -> 0.01 us  [the longest x1 0.01 us: with_halo(): lax.ppermute(jnp.where(odd, head, tail), axis, [(i, i ^ 1) for i in range...]
    ppermute x4, starting transfers between devices: 9.95 us -> 11.9 us  [tree_sum(): lax.ppermute(values, axis, [(i, i ^ step) for i in range(count)])]
    select_n x0 -> x2, other arithmetic: none -> 1.11 us  [the longest x1 1.07 us: with_halo(): jnp.where(odd, head, tail)]
    slice x1 -> x0, local copies, waits for them, and re-layouts: 1.06 us -> none  [with_halo(): lax.slice_in_dim(cells, cells.shape[dim] - width, cells.shape[dim], axis=...]
    unnamed x12, local copies, waits for them, and re-layouts: 0.49 us -> 1.4 us
  transfers between devices with their start and end apart: 6 -> 6, of which waited for: 4 -> 3; matrix products, arithmetic and copies ran while one was open for 7% -> 7% of each run, Pallas kernels for 0% -> 0%
where the time goes in v7:
time: 56.3 us; the launch traced here: 56 us
  blocking collectives  25.6 us (45%)
  starting transfers between devices  13.1 us (23%)
  local copies, waits for them, and re-layouts  6.89 us (12%)
  other arithmetic  4.8 us (9%)
  waiting for transfers between devices  4.47 us (8%)
  between operations  0.91 us (2%)
    all_to_all x1, blocking collectives, gram_rows(): columns = lax.all_to_all(zscores, axis, 1, 0, tiled=True)  13 us
    all_to_all x1, blocking collectives, gram_rows(): pieces = lax.all_to_all(partial, axis, 0, 0, tiled=True)  12.6 us
    ppermute x4, starting transfers between devices, tree_sum(): lax.ppermute(values, axis, [(i, i ^ step) for i in range(count)])  11.9 us
    ppermute x4, waiting for transfers between devices, tree_sum(): lax.ppermute(values, axis, [(i, i ^ step) for i in range(count)])  4.46 us
    scatter x1, local copies, waits for them, and re-layouts, shards(): kept_bins = jnp.ones((col_count,), jnp.float32).at[masked_bins].set(0.0)  2.95 us
    add x1, other arithmetic, smooth(): smoothed + jnp.where(radius_map == radius, box_sums / float((2 * radius +...  1.49 us
    unnamed x12, local copies, waits for them, and re-layouts  1.4 us
  transfers between devices with their start and end apart: 6, of which 3 were waited for; matrix products, arithmetic and copies ran while one was open for 7% of the time, Pallas kernels for 0%

profile of v7, /device:TPU:0, one launch (start us, length us, event | category | flops | bytes accessed | tf_op | source)
XLA Modules:
  0.0 56.0 jit_solution(16538288672072097951)
XLA Ops:
  0.0 1.1 %slice_select_fusion.1 = (f32[3,6144]{1,0:T(4,128)S(1)}, f32[3,6144]{1,0:T(4,128)S(1)}) fusion(f32[16,6144]{1,0:T(8,128)} %param.4, pred[]{:T(512)S(6)} %eq.39), kind=kLoop, calls=%fused_computation.42 | loop fusion | flops 36864 | bytes 294913 | tf_op jit(solution)/shard_map/jit(_where)/select_n | solution.py:21
  1.1 0.6 collective-permute-start
  1.6 0.7 %collective-permute-start.1 = (f32[3,6144]{1,0:T(4,128)S(1)}, f32[3,6144]{1,0:T(4,128)S(1)}, u32[]{:S(2)}, u32[]{:S(2)}) collective-permute-start(f32[3,6144]{1,0:T(4,128)S(1)} %get-tuple-element.11), channel_id=1, source_target_pairs={{2,1},{4,3},{6,5},{8,7},{10,9},{12,11},{14,13},{1,2},{3,4},{5,6},{... | collective-permute-start | bytes 221192 | tf_op jit(solution)/shard_map/ppermute | solution.py:23
  3.0 0.1 slice.102
  3.0 0.1 reverse
  3.1 0.1 slice.241
  3.2 0.1 fusion.13
  3.4 0.2 tile.9
  3.6 0.2 slice.135
  3.8 0.3 reshape.37
  4.0 0.0 copy-start
  4.0 0.0 collective-permute-done
  4.1 0.0 collective-permute-done.1
  4.1 0.9 %copy-done = f32[16,6144]{1,0:T(8,128)S(1)} copy-done((f32[16,6144]{1,0:T(8,128)S(1)}, f32[16,6144]{1,0:T(8,128)}, u32[]{:S(2)}) %copy-start) | copy-done | bytes 393240
  5.0 0.3 select_maximum_fusion
  5.4 0.2 slice_add_fusion
  5.6 1.5 %fusion.3 = f32[16,6144]{1,0:T(8,128)S(1)} fusion(f32[16,6150]{1,0:T(8,128)S(1)} %get-tuple-element.7, f32[16,6150]{1,0:T(8,128)S(1)} %get-tuple-element.8, f32[16,6150]{1,0:T(8,128)S(1)} %get-tuple-element.9, f32[16,6144]{1,0:T(8,128)S(1)} %copy-done, s32[16,6158]{1,0:T(8,128)S(1)} %reshape.37), kind=kLoop, calls=%fused_computation.16 | loop fusion | flops 2555904 | bytes 7077888 | tf_op jit(solution)/shard_map/add | solution.py:54
  7.1 0.2 pad.13
  7.3 0.2 reshape.38
  7.5 0.2 reshape.39
  7.8 0.1 reduce_sum.36
  7.9 0.2 slice_dynamic-update-slice_fusion
  8.1 0.1 reverse.1
  8.2 0.1 slice.242
  8.3 0.1 slice_add_fusion.18
  8.3 4.0 %collective-permute-start.2 = (f32[6144]{0:T(1024)S(1)}, f32[6144]{0:T(1024)S(1)}, u32[]{:S(2)}, u32[]{:S(2)}) collective-permute-start(f32[6144]{0:T(1024)S(1)} %slice_add_fusion.18), channel_id=1, source_target_pairs={{0,1},{1,0},{2,3},{3,2},{4,5},{5,4},{6,7},{7,6},{8,9},{9,8},{10,11... | collective-permute-start | bytes 73736 | tf_op jit(solution)/shard_map/ppermute | solution.py:114
  12.3 0.8 %collective-permute-done.2 = f32[6144]{0:T(1024)S(1)} collective-permute-done((f32[6144]{0:T(1024)S(1)}, f32[6144]{0:T(1024)S(1)}, u32[]{:S(2)}, u32[]{:S(2)}) %collective-permute-start.2) | collective-permute-done | bytes 24608 | tf_op jit(solution)/shard_map/ppermute | solution.py:114
  13.2 2.6 %collective-permute-start.3 = (f32[6144]{0:T(1024)S(1)}, f32[6144]{0:T(1024)S(1)}, u32[]{:S(2)}, u32[]{:S(2)}) collective-permute-start(f32[6144]{0:T(1024)S(1)} %add.150), channel_id=1, source_target_pairs={{0,2},{1,3},{2,0},{3,1},{4,6},{5,7},{6,4},{7,5},{8,10},{9,11},{10,... | collective-permute-start | bytes 73736 | tf_op jit(solution)/shard_map/ppermute | solution.py:114
  15.8 1.8 %collective-permute-done.3 = f32[6144]{0:T(1024)S(1)} collective-permute-done((f32[6144]{0:T(1024)S(1)}, f32[6144]{0:T(1024)S(1)}, u32[]{:S(2)}, u32[]{:S(2)}) %collective-permute-start.3) | collective-permute-done | bytes 24608 | tf_op jit(solution)/shard_map/ppermute | solution.py:114
  17.6 2.3 %collective-permute-start.4 = (f32[6144]{0:T(1024)S(1)}, f32[6144]{0:T(1024)S(1)}, u32[]{:S(2)}, u32[]{:S(2)}) collective-permute-start(f32[6144]{0:T(1024)S(1)} %add.151), channel_id=1, source_target_pairs={{0,4},{1,5},{2,6},{3,7},{4,0},{5,1},{6,2},{7,3},{8,12},{9,13},{10,... | collective-permute-start | bytes 73736 | tf_op jit(solution)/shard_map/ppermute | solution.py:114
  19.9 1.8 %collective-permute-done.4 = f32[6144]{0:T(1024)S(1)} collective-permute-done((f32[6144]{0:T(1024)S(1)}, f32[6144]{0:T(1024)S(1)}, u32[]{:S(2)}, u32[]{:S(2)}) %collective-permute-start.4) | collective-permute-done | bytes 24608 | tf_op jit(solution)/shard_map/ppermute | solution.py:114
  21.7 3.0 %collective-permute-start.5 = (f32[6144]{0:T(1024)S(1)}, f32[6144]{0:T(1024)S(1)}, u32[]{:S(2)}, u32[]{:S(2)}) collective-permute-start(f32[6144]{0:T(1024)S(1)} %add.152), channel_id=1, source_target_pairs={{0,8},{1,9},{2,10},{3,11},{4,12},{5,13},{6,14},{7,15},{8,0},{9,1},... | collective-permute-start | bytes 73736 | tf_op jit(solution)/shard_map/ppermute | solution.py:114
  24.7 2.9 %scatter_custom_fusion = f32[6144]{0:T(1024)S(1)} fusion(s32[384]{0:T(512)S(1)} %compare_select_fusion, f32[384]{0:T(512)S(1)} %broadcast.40, f32[]{:T(128)} %constant.67.clone.1), kind=kCustom, calls=%fused_computation.55 | custom fusion | bytes 24580 | tf_op jit(solution)/shard_map/scatter | solution.py:145
  27.7 0.1 dynamic_slice.11
  27.8 0.1 slice.162
  27.9 0.1 reverse.2
  27.9 0.1 slice.243
  28.0 0.1 fusion.12
  28.2 0.2 tile.21
  28.4 0.2 slice.163
  28.6 0.3 reshape.40
  28.9 0.2 multiply_reduce_fusion.1
  29.1 0.3 multiply_reduce_fusion
  29.3 0.1 multiply_convert_fusion
  29.5 13.0 %all_to_all.25 = bf16[16,16,384]{2,0,1:T(8,128)(2,1)S(1)} all-to-all(bf16[16,16,384]{2,0,1:T(8,128)(2,1)S(1)} %bitcast.20), channel_id=1, replica_groups=mesh['groups'=2,'blk'=16] {'blk'}, dimensions={1} | all-to-all | bytes 393216 | tf_op jit(solution)/shard_map/all_to_all | solution.py:122
  42.5 0.3 fusion.10
  42.8 12.6 %all_to_all.26 = f32[16,16,256]{2,1,0:T(8,128)S(1)} all-to-all(f32[16,16,256]{2,1,0:T(8,128)S(1)} %fusion.10), channel_id=1, replica_groups=mesh['groups'=2,'blk'=16] {'blk'}, dimensions={0} | all-to-all | bytes 524288 | tf_op jit(solution)/shard_map/all_to_all | solution.py:124
  55.4 0.6 %broadcast_multiply_fusion = f32[16,256]{1,0:T(8,128)} fusion(f32[16,256]{1,0:T(8,128)S(1)} %reduce_sum.39), kind=kLoop, calls=%fused_computation.57 | loop fusion | flops 4096 | bytes 32768 | tf_op jit(solution)/shard_map/div | solution.py:149
  (21 shorter events, 0.3 us)
Async XLA Ops:
  0.0 3.0 %copy-start.1 = (s32[6144]{0:T(1024)S(1)}, s32[6144]{0:T(1024)}, u32[]{:S(2)}) copy-start(s32[6144]{0:T(1024)} %param.5) | copy-start | bytes 73732
  1.1 3.0 %collective-permute-start = (f32[3,6144]{1,0:T(4,128)S(1)}, f32[3,6144]{1,0:T(4,128)S(1)}, u32[]{:S(2)}, u32[]{:S(2)}) collective-permute-start(f32[3,6144]{1,0:T(4,128)S(1)} %get-tuple-element.10), channel_id=1, source_target_pairs={{0,1},{1,0},{2,3},{3,2},{4,5},{5,4},{6,7},{7,6},{8,9},{9,8},{10,11... | collective-permute-start | bytes 221192 | tf_op jit(solution)/shard_map/ppermute | solution.py:20
  1.6 2.4 %collective-permute-start.1 = (f32[3,6144]{1,0:T(4,128)S(1)}, f32[3,6144]{1,0:T(4,128)S(1)}, u32[]{:S(2)}, u32[]{:S(2)}) collective-permute-start(f32[3,6144]{1,0:T(4,128)S(1)} %get-tuple-element.11), channel_id=1, source_target_pairs={{2,1},{4,3},{6,5},{8,7},{10,9},{12,11},{14,13},{1,2},{3,4},{5,6},{... | collective-permute-start | bytes 221192 | tf_op jit(solution)/shard_map/ppermute | solution.py:23
  4.0 1.0 %copy-start = (f32[16,6144]{1,0:T(8,128)S(1)}, f32[16,6144]{1,0:T(8,128)}, u32[]{:S(2)}) copy-start(f32[16,6144]{1,0:T(8,128)} %param.4) | copy-start | bytes 1179652
  8.3 4.8 %collective-permute-start.2 = (f32[6144]{0:T(1024)S(1)}, f32[6144]{0:T(1024)S(1)}, u32[]{:S(2)}, u32[]{:S(2)}) collective-permute-start(f32[6144]{0:T(1024)S(1)} %slice_add_fusion.18), channel_id=1, source_target_pairs={{0,1},{1,0},{2,3},{3,2},{4,5},{5,4},{6,7},{7,6},{8,9},{9,8},{10,11... | collective-permute-start | bytes 73736 | tf_op jit(solution)/shard_map/ppermute | solution.py:114
  13.2 4.4 %collective-permute-start.3 = (f32[6144]{0:T(1024)S(1)}, f32[6144]{0:T(1024)S(1)}, u32[]{:S(2)}, u32[]{:S(2)}) collective-permute-start(f32[6144]{0:T(1024)S(1)} %add.150), channel_id=1, source_target_pairs={{0,2},{1,3},{2,0},{3,1},{4,6},{5,7},{6,4},{7,5},{8,10},{9,11},{10,... | collective-permute-start | bytes 73736 | tf_op jit(solution)/shard_map/ppermute | solution.py:114
  17.6 7.1 %copy-start.2 = (s32[384]{0:T(512)S(1)}, s32[384]{0:T(512)}, u32[]{:S(2)}) copy-start(s32[384]{0:T(512)} %param.6) | copy-start | bytes 4612
  17.6 4.1 %collective-permute-start.4 = (f32[6144]{0:T(1024)S(1)}, f32[6144]{0:T(1024)S(1)}, u32[]{:S(2)}, u32[]{:S(2)}) collective-permute-start(f32[6144]{0:T(1024)S(1)} %add.151), channel_id=1, source_target_pairs={{0,4},{1,5},{2,6},{3,7},{4,0},{5,1},{6,2},{7,3},{8,12},{9,13},{10,... | collective-permute-start | bytes 73736 | tf_op jit(solution)/shard_map/ppermute | solution.py:114
  21.7 6.1 %collective-permute-start.5 = (f32[6144]{0:T(1024)S(1)}, f32[6144]{0:T(1024)S(1)}, u32[]{:S(2)}, u32[]{:S(2)}) collective-permute-start(f32[6144]{0:T(1024)S(1)} %add.152), channel_id=1, source_target_pairs={{0,8},{1,9},{2,10},{3,11},{4,12},{5,13},{6,14},{7,15},{8,0},{9,1},... | collective-permute-start | bytes 73736 | tf_op jit(solution)/shard_map/ppermute | solution.py:114

commit v8 on v7

--- a/solution.py
+++ b/solution.py
@@ -109,10 +109,10 @@
     count = lax.axis_size(axis)
     if count & (count - 1):
         return lax.psum(values, axis)
-    step = 1
-    while step < count:
+    step = count // 2
+    while step:
         values = values + lax.ppermute(values, axis, [(i, i ^ step) for i in range(count)])
-        step *= 2
+        step //= 2
     return values
 
 

time: 56.3 us -> 58.3 us (1.036)
  waiting for transfers between devices: 4.47 us -> 7.05 us
  starting transfers between devices: 13.1 us -> 11 us
  blocking collectives: 25.6 us -> 27 us
    ppermute x4, waiting for transfers between devices: 4.46 us -> 7.04 us  [tree_sum(): lax.ppermute(values, axis, [(i, i ^ step) for i in range(count)])]
    ppermute x4, starting transfers between devices: 11.9 us -> 9.83 us  [tree_sum(): lax.ppermute(values, axis, [(i, i ^ step) for i in range(count)])]
    all_to_all x1, blocking collectives: 13 us -> 14.4 us  [gram_rows(): columns = lax.all_to_all(zscores, axis, 1, 0, tiled=True)]
where the time goes in v8:
time: 58.3 us; the launch traced here: 58 us
  blocking collectives  27 us (46%)
  starting transfers between devices  11 us (19%)
  waiting for transfers between devices  7.05 us (12%)
  local copies, waits for them, and re-layouts  6.89 us (12%)
  other arithmetic  4.8 us (8%)
  between operations  0.94 us (2%)
    all_to_all x1, blocking collectives, gram_rows(): columns = lax.all_to_all(zscores, axis, 1, 0, tiled=True)  14.4 us
    all_to_all x1, blocking collectives, gram_rows(): pieces = lax.all_to_all(partial, axis, 0, 0, tiled=True)  12.6 us
    ppermute x4, starting transfers between devices, tree_sum(): lax.ppermute(values, axis, [(i, i ^ step) for i in range(count)])  9.83 us
    ppermute x4, waiting for transfers between devices, tree_sum(): lax.ppermute(values, axis, [(i, i ^ step) for i in range(count)])  7.04 us
    scatter x1, local copies, waits for them, and re-layouts, shards(): kept_bins = jnp.ones((col_count,), jnp.float32).at[masked_bins].set(0.0)  2.95 us
    add x1, other arithmetic, smooth(): smoothed + jnp.where(radius_map == radius, box_sums / float((2 * radius +...  1.49 us
    unnamed x12, local copies, waits for them, and re-layouts  1.4 us
  transfers between devices with their start and end apart: 6, of which 3 were waited for; matrix products, arithmetic and copies ran while one was open for 7% of the time, Pallas kernels for 0%

profile of v8, /device:TPU:0, one launch (start us, length us, event | category | flops | bytes accessed | tf_op | source)
XLA Modules:
  0.0 58.0 jit_solution(15692664148311477444)
XLA Ops:
  0.0 1.1 %slice_select_fusion.1 = (f32[3,6144]{1,0:T(4,128)S(1)}, f32[3,6144]{1,0:T(4,128)S(1)}) fusion(f32[16,6144]{1,0:T(8,128)} %param.4, pred[]{:T(512)S(6)} %eq.39), kind=kLoop, calls=%fused_computation.42 | loop fusion | flops 36864 | bytes 294913 | tf_op jit(solution)/shard_map/jit(_where)/select_n | solution.py:21
  1.1 0.6 collective-permute-start
  1.6 0.7 %collective-permute-start.1 = (f32[3,6144]{1,0:T(4,128)S(1)}, f32[3,6144]{1,0:T(4,128)S(1)}, u32[]{:S(2)}, u32[]{:S(2)}) collective-permute-start(f32[3,6144]{1,0:T(4,128)S(1)} %get-tuple-element.11), channel_id=1, source_target_pairs={{2,1},{4,3},{6,5},{8,7},{10,9},{12,11},{14,13},{1,2},{3,4},{5,6},{... | collective-permute-start | bytes 221192 | tf_op jit(solution)/shard_map/ppermute | solution.py:23
  3.0 0.1 slice.102
  3.0 0.1 reverse
  3.1 0.1 slice.241
  3.2 0.1 fusion.13
  3.4 0.2 tile.9
  3.6 0.2 slice.135
  3.8 0.3 reshape.37
  4.0 0.0 copy-start
  4.0 0.0 collective-permute-done
  4.1 0.0 collective-permute-done.1
  4.1 0.9 %copy-done = f32[16,6144]{1,0:T(8,128)S(1)} copy-done((f32[16,6144]{1,0:T(8,128)S(1)}, f32[16,6144]{1,0:T(8,128)}, u32[]{:S(2)}) %copy-start) | copy-done | bytes 393240
  5.0 0.3 select_maximum_fusion
  5.4 0.2 slice_add_fusion
  5.6 1.5 %fusion.3 = f32[16,6144]{1,0:T(8,128)S(1)} fusion(f32[16,6150]{1,0:T(8,128)S(1)} %get-tuple-element.7, f32[16,6150]{1,0:T(8,128)S(1)} %get-tuple-element.8, f32[16,6150]{1,0:T(8,128)S(1)} %get-tuple-element.9, f32[16,6144]{1,0:T(8,128)S(1)} %copy-done, s32[16,6158]{1,0:T(8,128)S(1)} %reshape.37), kind=kLoop, calls=%fused_computation.16 | loop fusion | flops 2555904 | bytes 7077888 | tf_op jit(solution)/shard_map/add | solution.py:54
  7.1 0.2 pad.13
  7.3 0.2 reshape.38
  7.5 0.2 reshape.39
  7.8 0.1 reduce_sum.36
  7.9 0.2 slice_dynamic-update-slice_fusion
  8.1 0.1 reverse.1
  8.2 0.1 slice.242
  8.2 0.1 slice_add_fusion.18
  8.3 7.2 %collective-permute-start.2 = (f32[6144]{0:T(1024)S(1)}, f32[6144]{0:T(1024)S(1)}, u32[]{:S(2)}, u32[]{:S(2)}) collective-permute-start(f32[6144]{0:T(1024)S(1)} %slice_add_fusion.18), channel_id=1, source_target_pairs={{0,8},{1,9},{2,10},{3,11},{4,12},{5,13},{6,14},{7,15},{8,0},{9,1},... | collective-permute-start | bytes 73736 | tf_op jit(solution)/shard_map/ppermute | solution.py:114
  15.6 1.9 %collective-permute-done.2 = f32[6144]{0:T(1024)S(1)} collective-permute-done((f32[6144]{0:T(1024)S(1)}, f32[6144]{0:T(1024)S(1)}, u32[]{:S(2)}, u32[]{:S(2)}) %collective-permute-start.2) | collective-permute-done | bytes 24608 | tf_op jit(solution)/shard_map/ppermute | solution.py:114
  17.5 1.8 %collective-permute-start.3 = (f32[6144]{0:T(1024)S(1)}, f32[6144]{0:T(1024)S(1)}, u32[]{:S(2)}, u32[]{:S(2)}) collective-permute-start(f32[6144]{0:T(1024)S(1)} %add.150), channel_id=1, source_target_pairs={{0,4},{1,5},{2,6},{3,7},{4,0},{5,1},{6,2},{7,3},{8,12},{9,13},{10,... | collective-permute-start | bytes 73736 | tf_op jit(solution)/shard_map/ppermute | solution.py:114
  19.3 2.0 %collective-permute-done.3 = f32[6144]{0:T(1024)S(1)} collective-permute-done((f32[6144]{0:T(1024)S(1)}, f32[6144]{0:T(1024)S(1)}, u32[]{:S(2)}, u32[]{:S(2)}) %collective-permute-start.3) | collective-permute-done | bytes 24608 | tf_op jit(solution)/shard_map/ppermute | solution.py:114
  21.3 0.8 %collective-permute-start.4 = (f32[6144]{0:T(1024)S(1)}, f32[6144]{0:T(1024)S(1)}, u32[]{:S(2)}, u32[]{:S(2)}) collective-permute-start(f32[6144]{0:T(1024)S(1)} %add.151), channel_id=1, source_target_pairs={{0,2},{1,3},{2,0},{3,1},{4,6},{5,7},{6,4},{7,5},{8,10},{9,11},{10,... | collective-permute-start | bytes 73736 | tf_op jit(solution)/shard_map/ppermute | solution.py:114
  22.1 3.1 %collective-permute-done.4 = f32[6144]{0:T(1024)S(1)} collective-permute-done((f32[6144]{0:T(1024)S(1)}, f32[6144]{0:T(1024)S(1)}, u32[]{:S(2)}, u32[]{:S(2)}) %collective-permute-start.4) | collective-permute-done | bytes 24608 | tf_op jit(solution)/shard_map/ppermute | solution.py:114
  25.3 3.0 %scatter_custom_fusion = f32[6144]{0:T(1024)S(1)} fusion(s32[384]{0:T(512)S(1)} %compare_select_fusion, f32[384]{0:T(512)S(1)} %broadcast.40, f32[]{:T(128)} %constant.67.clone.1), kind=kCustom, calls=%fused_computation.55 | custom fusion | bytes 24580 | tf_op jit(solution)/shard_map/scatter | solution.py:145
  28.2 0.1 dynamic_slice.11
  28.3 0.0 collective-permute-done.5
  28.3 0.1 slice.162
  28.4 0.1 reverse.2
  28.5 0.1 slice.243
  28.6 0.1 fusion.12
  28.7 0.2 tile.21
  29.0 0.2 slice.163
  29.2 0.3 reshape.40
  29.4 0.2 multiply_reduce_fusion.1
  29.6 0.3 multiply_reduce_fusion
  29.9 0.1 multiply_convert_fusion
  30.1 14.4 %all_to_all.25 = bf16[16,16,384]{2,0,1:T(8,128)(2,1)S(1)} all-to-all(bf16[16,16,384]{2,0,1:T(8,128)(2,1)S(1)} %bitcast.20), channel_id=1, replica_groups=mesh['groups'=2,'blk'=16] {'blk'}, dimensions={1} | all-to-all | bytes 393216 | tf_op jit(solution)/shard_map/all_to_all | solution.py:122
  44.5 0.3 fusion.10
  44.7 12.6 %all_to_all.26 = f32[16,16,256]{2,1,0:T(8,128)S(1)} all-to-all(f32[16,16,256]{2,1,0:T(8,128)S(1)} %fusion.10), channel_id=1, replica_groups=mesh['groups'=2,'blk'=16] {'blk'}, dimensions={0} | all-to-all | bytes 524288 | tf_op jit(solution)/shard_map/all_to_all | solution.py:124
  57.4 0.6 %broadcast_multiply_fusion = f32[16,256]{1,0:T(8,128)} fusion(f32[16,256]{1,0:T(8,128)S(1)} %reduce_sum.39), kind=kLoop, calls=%fused_computation.57 | loop fusion | flops 4096 | bytes 32768 | tf_op jit(solution)/shard_map/div | solution.py:149
  (21 shorter events, 0.3 us)
Async XLA Ops:
  0.0 3.0 %copy-start.1 = (s32[6144]{0:T(1024)S(1)}, s32[6144]{0:T(1024)}, u32[]{:S(2)}) copy-start(s32[6144]{0:T(1024)} %param.5) | copy-start | bytes 73732
  1.1 3.0 %collective-permute-start = (f32[3,6144]{1,0:T(4,128)S(1)}, f32[3,6144]{1,0:T(4,128)S(1)}, u32[]{:S(2)}, u32[]{:S(2)}) collective-permute-start(f32[3,6144]{1,0:T(4,128)S(1)} %get-tuple-element.10), channel_id=1, source_target_pairs={{0,1},{1,0},{2,3},{3,2},{4,5},{5,4},{6,7},{7,6},{8,9},{9,8},{10,11... | collective-permute-start | bytes 221192 | tf_op jit(solution)/shard_map/ppermute | solution.py:20
  1.6 2.4 %collective-permute-start.1 = (f32[3,6144]{1,0:T(4,128)S(1)}, f32[3,6144]{1,0:T(4,128)S(1)}, u32[]{:S(2)}, u32[]{:S(2)}) collective-permute-start(f32[3,6144]{1,0:T(4,128)S(1)} %get-tuple-element.11), channel_id=1, source_target_pairs={{2,1},{4,3},{6,5},{8,7},{10,9},{12,11},{14,13},{1,2},{3,4},{5,6},{... | collective-permute-start | bytes 221192 | tf_op jit(solution)/shard_map/ppermute | solution.py:23
  4.0 1.0 %copy-start = (f32[16,6144]{1,0:T(8,128)S(1)}, f32[16,6144]{1,0:T(8,128)}, u32[]{:S(2)}) copy-start(f32[16,6144]{1,0:T(8,128)} %param.4) | copy-start | bytes 1179652
  8.3 9.2 %collective-permute-start.2 = (f32[6144]{0:T(1024)S(1)}, f32[6144]{0:T(1024)S(1)}, u32[]{:S(2)}, u32[]{:S(2)}) collective-permute-start(f32[6144]{0:T(1024)S(1)} %slice_add_fusion.18), channel_id=1, source_target_pairs={{0,8},{1,9},{2,10},{3,11},{4,12},{5,13},{6,14},{7,15},{8,0},{9,1},... | collective-permute-start | bytes 73736 | tf_op jit(solution)/shard_map/ppermute | solution.py:114
  17.5 3.8 %collective-permute-start.3 = (f32[6144]{0:T(1024)S(1)}, f32[6144]{0:T(1024)S(1)}, u32[]{:S(2)}, u32[]{:S(2)}) collective-permute-start(f32[6144]{0:T(1024)S(1)} %add.150), channel_id=1, source_target_pairs={{0,4},{1,5},{2,6},{3,7},{4,0},{5,1},{6,2},{7,3},{8,12},{9,13},{10,... | collective-permute-start | bytes 73736 | tf_op jit(solution)/shard_map/ppermute | solution.py:114
  21.3 3.9 %copy-start.2 = (s32[384]{0:T(512)S(1)}, s32[384]{0:T(512)}, u32[]{:S(2)}) copy-start(s32[384]{0:T(512)} %param.6) | copy-start | bytes 4612
  21.3 3.9 %collective-permute-start.4 = (f32[6144]{0:T(1024)S(1)}, f32[6144]{0:T(1024)S(1)}, u32[]{:S(2)}, u32[]{:S(2)}) collective-permute-start(f32[6144]{0:T(1024)S(1)} %add.151), channel_id=1, source_target_pairs={{0,2},{1,3},{2,0},{3,1},{4,6},{5,7},{6,4},{7,5},{8,10},{9,11},{10,... | collective-permute-start | bytes 73736 | tf_op jit(solution)/shard_map/ppermute | solution.py:114
  25.2 3.1 %collective-permute-start.5 = (f32[6144]{0:T(1024)S(1)}, f32[6144]{0:T(1024)S(1)}, u32[]{:S(2)}, u32[]{:S(2)}) collective-permute-start(f32[6144]{0:T(1024)S(1)} %add.152), channel_id=1, source_target_pairs={{0,1},{1,0},{2,3},{3,2},{4,5},{5,4},{6,7},{7,6},{8,9},{9,8},{10,11... | collective-permute-start | bytes 73736 | tf_op jit(solution)/shard_map/ppermute | solution.py:114

commit v9 on v7

--- a/solution.py
+++ b/solution.py
@@ -135,14 +135,15 @@
     first_bin = row_start[0]
     window_first = col_count - 1 - (first_bin + first_row + rows_here - 1)
     radius_map = skewed_map(widths, window_first, rows_here, col_count)
-    padded_rows = with_halo(contacts, (("blk", 0),), WMAX)
-    padded = jnp.pad(padded_rows, ((0, 0), (WMAX, WMAX)))
+    own = lax.optimization_barrier(jnp.pad(contacts, WMAX))
+    halo = with_halo(contacts, (("blk", 0),), WMAX)
+    padded = own.at[:WMAX, WMAX:-WMAX].set(halo[:WMAX]).at[-WMAX:, WMAX:-WMAX].set(halo[-WMAX:])
     smoothed = smooth(padded, radius_map)
     local_total = diagonal_totals(smoothed, window_first)
     denominator = pair_counts(first_bin, nbins, col_count)
     expected = tree_sum(local_total, "blk") / denominator
     expected_map = skewed_map(expected, window_first, rows_here, col_count)
-    kept_bins = jnp.ones((col_count,), jnp.float32).at[masked_bins].set(0.0)
+    kept_bins = jnp.ones((col_count,), jnp.float32).at[masked_bins].set(0.0, unique_indices=True)
     kept_rows = lax.dynamic_slice_in_dim(kept_bins, first_bin + first_row, rows_here)
     kept_total = jnp.float32(col_count - masked_bins.shape[0])
     zscores = normalize(smoothed, expected_map, kept_rows, kept_bins, kept_total)

time: 56.3 us -> 65.3 us (1.16)
  local copies, waits for them, and re-layouts: 6.89 us -> 14.4 us
  other arithmetic: 4.8 us -> 7.16 us
  starting transfers between devices: 13.1 us -> 10.9 us
  waiting for transfers between devices: 4.47 us -> 5.74 us
    scatter x1 -> x3, local copies, waits for them, and re-layouts: 2.95 us -> 9.2 us  [the longest x2 6.25 us: shards(): own.at[:WMAX, WMAX:-WMAX].set(halo[:WMAX]).at[-WMAX:, WMAX:-WMAX]]
    ppermute x4, starting transfers between devices: 11.9 us -> 5.83 us  [tree_sum(): lax.ppermute(values, axis, [(i, i ^ step) for i in range(count)])]
    ppermute x1, starting transfers between devices: 0.56 us -> 4.42 us  [with_halo(): lax.ppermute(jnp.where(odd, head, tail), axis, [(i, i ^ 1) for i in range...]
    select_n x3, other arithmetic: 1.11 us -> 3.04 us  [the longest x1 1.97 us: with_halo(): after = jnp.where(odd, outer, inner)]
    ppermute x4, waiting for transfers between devices: 4.46 us -> 5.74 us  [tree_sum(): lax.ppermute(values, axis, [(i, i ^ step) for i in range(count)])]
    another operation x0 -> x2, other arithmetic: none -> 0.66 us
    unnamed x12 -> x14, local copies, waits for them, and re-layouts: 1.4 us -> 1.86 us
  transfers between devices with their start and end apart: 6 -> 6, of which waited for: 3 -> 3; matrix products, arithmetic and copies ran while one was open for 7% -> 9% of each run, Pallas kernels for 0% -> 0%
where the time goes in v9:
time: 65.3 us; the launch traced here: 65 us
  blocking collectives  25.6 us (39%)
  local copies, waits for them, and re-layouts  14.4 us (22%)
  starting transfers between devices  10.9 us (17%)
  other arithmetic  7.16 us (11%)
  waiting for transfers between devices  5.74 us (9%)
  between operations  0.91 us (1%)
    all_to_all x1, blocking collectives, gram_rows(): columns = lax.all_to_all(zscores, axis, 1, 0, tiled=True)  13 us
    all_to_all x1, blocking collectives, gram_rows(): pieces = lax.all_to_all(partial, axis, 0, 0, tiled=True)  12.6 us
    scatter x2, local copies, waits for them, and re-layouts, shards(): own.at[:WMAX, WMAX:-WMAX].set(halo[:WMAX]).at[-WMAX:, WMAX:-WMAX]  6.25 us
    ppermute x4, starting transfers between devices, tree_sum(): lax.ppermute(values, axis, [(i, i ^ step) for i in range(count)])  5.83 us
    ppermute x4, waiting for transfers between devices, tree_sum(): lax.ppermute(values, axis, [(i, i ^ step) for i in range(count)])  5.74 us
    ppermute x1, starting transfers between devices, with_halo(): lax.ppermute(jnp.where(odd, head, tail), axis, [(i, i ^ 1) for i in range...  4.42 us
    scatter x1, local copies, waits for them, and re-layouts, shards(): jnp.ones((col_count,), jnp.float32).at[masked_bins]  2.95 us
    select_n x1, other arithmetic, with_halo(): after = jnp.where(odd, outer, inner)  1.97 us
  transfers between devices with their start and end apart: 6, of which 3 were waited for; matrix products, arithmetic and copies ran while one was open for 9% of the time, Pallas kernels for 0%

profile of v9, /device:TPU:0, one launch (start us, length us, event | category | flops | bytes accessed | tf_op | source)
XLA Modules:
  0.0 65.0 jit_solution(7737452812250859108)
XLA Ops:
  0.0 1.1 %slice_select_fusion.1 = (f32[3,6144]{1,0:T(4,128)S(1)}, f32[3,6144]{1,0:T(4,128)S(1)}) fusion(f32[16,6144]{1,0:T(8,128)} %param.8, pred[]{:T(512)S(6)} %eq.37), kind=kLoop, calls=%fused_computation.38 | loop fusion | flops 36864 | bytes 294913 | tf_op jit(solution)/shard_map/jit(_where)/select_n | solution.py:24
  1.1 0.7 %collective-permute-start.1 = (f32[3,6144]{1,0:T(4,128)S(1)}, f32[3,6144]{1,0:T(4,128)S(1)}, u32[]{:S(2)}, u32[]{:S(2)}) collective-permute-start(f32[3,6144]{1,0:T(4,128)S(1)} %get-tuple-element.34), channel_id=1, source_target_pairs={{2,1},{4,3},{6,5},{8,7},{10,9},{12,11},{14,13},{1,2},{3,4},{5,6},{... | collective-permute-start | bytes 221192 | tf_op jit(solution)/shard_map/ppermute | solution.py:23
  1.8 4.4 %collective-permute-start = (f32[3,6144]{1,0:T(4,128)S(1)}, f32[3,6144]{1,0:T(4,128)S(1)}, u32[]{:S(2)}, u32[]{:S(2)}) collective-permute-start(f32[3,6144]{1,0:T(4,128)S(1)} %get-tuple-element.35), channel_id=1, source_target_pairs={{0,1},{1,0},{2,3},{3,2},{4,5},{5,4},{6,7},{7,6},{8,9},{9,8},{10,11... | collective-permute-start | bytes 221192 | tf_op jit(solution)/shard_map/ppermute | solution.py:20
  6.8 0.6 copy-done.3
  7.5 0.7 %and_reduce_fusion = pred[]{:T(512)} fusion(s32[2]{0:T(128)S(1)} %copy-done.3), kind=kLoop, calls=%fused_computation.55 | loop fusion | flops 9 | bytes 9 | tf_op jit(solution)/shard_map/reduce.2
  8.2 0.1 reverse
  8.3 0.1 slice.298
  8.4 0.1 fusion.12
  8.5 0.2 tile.9
  8.8 0.2 slice.188
  9.0 0.3 reshape.104
  9.2 0.7 %copy-done = f32[16,6144]{1,0:T(8,128)S(1)} copy-done((f32[16,6144]{1,0:T(8,128)S(1)}, f32[16,6144]{1,0:T(8,128)}, u32[]{:S(2)}) %copy-start) | copy-done | bytes 393240
  10.0 0.2 pad.20
  10.2 0.6 fusion.15
  10.8 2.0 %broadcast_select_fusion = (f32[3,6144]{1,0:T(4,128)S(1)}, f32[3,6144]{1,0:T(4,128)S(1)}) fusion(f32[3,6144]{1,0:T(4,128)S(1)} %collective-permute-done.1, f32[3,6144]{1,0:T(4,128)S(1)} %collective-permute-done, pred[]{:T(512)S(6)} %eq.37, f32[22,6150]{1,0:T(8,128)S(1)} %pad.20, s32[]{:T(128)} %bitcast.1, s32[]{:T(128)} %bitcast.2, pred[]{:T(512)} %and_reduce_fusion), kind=kLoop, calls=%fused_computation.44 | loop fusion | flops 55296 | bytes 368650 | tf_op jit(solution)/shard_map/jit(_where)/select_n | solution.py:30
  12.7 4.0 %scatter.14 = f32[22,6150]{1,0:T(8,128)S(1)} dynamic-update-slice(f32[22,6150]{1,0:T(8,128)S(1)} %pad.20, f32[3,6144]{1,0:T(4,128)S(1)} %get-tuple-element.37, s32[]{:T(128)} %bitcast.1, s32[]{:T(128)} %bitcast.2) | dynamic-update-slice | bytes 147460 | tf_op jit(solution)/shard_map/scatter | solution.py:140
  16.8 2.2 %scatter.18 = f32[22,6150]{1,0:T(8,128)S(1)} dynamic-update-slice(f32[22,6150]{1,0:T(8,128)S(1)} %scatter.14, f32[3,6144]{1,0:T(4,128)S(1)} %get-tuple-element.36, s32[]{:T(128)} %constant.110.clone.1, s32[]{:T(128)} %constant.105.clone.1) | dynamic-update-slice | bytes 147460 | tf_op jit(solution)/shard_map/scatter | solution.py:140
  19.0 0.2 slice_add_fusion
  19.3 1.6 %fusion.2 = f32[16,6144]{1,0:T(8,128)S(1)} fusion(f32[16,6150]{1,0:T(8,128)S(1)} %get-tuple-element.31, f32[16,6150]{1,0:T(8,128)S(1)} %get-tuple-element.32, f32[16,6150]{1,0:T(8,128)S(1)} %get-tuple-element.33, f32[22,6150]{1,0:T(8,128)S(1)} %scatter.18, s32[16,6158]{1,0:T(8,128)S(1)} %reshape.104), kind=kLoop, calls=%fused_computation.11 | loop fusion | flops 2555904 | bytes 7077888 | tf_op jit(solution)/shard_map/add | solution.py:54
  20.9 0.2 pad.21
  21.0 0.2 reshape.107
  21.3 0.2 reshape.108
  21.6 0.2 slice_dynamic-update-slice_fusion
  21.8 0.1 reverse.1
  21.9 0.1 slice.299
  22.0 0.1 slice_add_fusion.18
  22.1 0.1 collective-permute-start.2
  22.2 1.2 %collective-permute-done.2 = f32[6144]{0:T(1024)S(1)} collective-permute-done((f32[6144]{0:T(1024)S(1)}, f32[6144]{0:T(1024)S(1)}, u32[]{:S(2)}, u32[]{:S(2)}) %collective-permute-start.2) | collective-permute-done | bytes 24608 | tf_op jit(solution)/shard_map/ppermute | solution.py:114
  23.4 1.5 %collective-permute-start.3 = (f32[6144]{0:T(1024)S(1)}, f32[6144]{0:T(1024)S(1)}, u32[]{:S(2)}, u32[]{:S(2)}) collective-permute-start(f32[6144]{0:T(1024)S(1)} %add.154), channel_id=1, source_target_pairs={{0,2},{1,3},{2,0},{3,1},{4,6},{5,7},{6,4},{7,5},{8,10},{9,11},{10,... | collective-permute-start | bytes 73736 | tf_op jit(solution)/shard_map/ppermute | solution.py:114
  24.9 2.3 %collective-permute-done.3 = f32[6144]{0:T(1024)S(1)} collective-permute-done((f32[6144]{0:T(1024)S(1)}, f32[6144]{0:T(1024)S(1)}, u32[]{:S(2)}, u32[]{:S(2)}) %collective-permute-start.3) | collective-permute-done | bytes 24608 | tf_op jit(solution)/shard_map/ppermute | solution.py:114
  27.2 1.6 %collective-permute-start.4 = (f32[6144]{0:T(1024)S(1)}, f32[6144]{0:T(1024)S(1)}, u32[]{:S(2)}, u32[]{:S(2)}) collective-permute-start(f32[6144]{0:T(1024)S(1)} %add.155), channel_id=1, source_target_pairs={{0,4},{1,5},{2,6},{3,7},{4,0},{5,1},{6,2},{7,3},{8,12},{9,13},{10,... | collective-permute-start | bytes 73736 | tf_op jit(solution)/shard_map/ppermute | solution.py:114
  28.8 2.2 %collective-permute-done.4 = f32[6144]{0:T(1024)S(1)} collective-permute-done((f32[6144]{0:T(1024)S(1)}, f32[6144]{0:T(1024)S(1)}, u32[]{:S(2)}, u32[]{:S(2)}) %collective-permute-start.4) | collective-permute-done | bytes 24608 | tf_op jit(solution)/shard_map/ppermute | solution.py:114
  31.1 2.6 %collective-permute-start.5 = (f32[6144]{0:T(1024)S(1)}, f32[6144]{0:T(1024)S(1)}, u32[]{:S(2)}, u32[]{:S(2)}) collective-permute-start(f32[6144]{0:T(1024)S(1)} %add.156), channel_id=1, source_target_pairs={{0,8},{1,9},{2,10},{3,11},{4,12},{5,13},{6,14},{7,15},{8,0},{9,1},... | collective-permute-start | bytes 73736 | tf_op jit(solution)/shard_map/ppermute | solution.py:114
  33.7 2.9 %scatter_custom_fusion = f32[6144]{0:T(1024)S(1)} fusion(s32[384]{0:T(512)S(1)} %compare_select_fusion, f32[384]{0:T(512)S(1)} %broadcast.78, f32[]{:T(128)} %constant.117.clone.1), kind=kCustom, calls=%fused_computation.51 | custom fusion | bytes 24580 | tf_op jit(solution)/shard_map/scatter | solution.py:146
  36.6 0.1 dynamic_slice.11
  36.8 0.1 reverse.2
  36.9 0.1 slice.300
  37.0 0.1 fusion.11
  37.2 0.2 tile.21
  37.4 0.2 slice.217
  37.6 0.3 reshape.109
  37.8 0.2 multiply_reduce_fusion.1
  38.0 0.3 multiply_reduce_fusion
  38.3 0.1 multiply_convert_fusion
  38.5 13.0 %all_to_all.25 = bf16[16,16,384]{2,0,1:T(8,128)(2,1)S(1)} all-to-all(bf16[16,16,384]{2,0,1:T(8,128)(2,1)S(1)} %bitcast.23), channel_id=1, replica_groups=mesh['groups'=2,'blk'=16] {'blk'}, dimensions={1} | all-to-all | bytes 393216 | tf_op jit(solution)/shard_map/all_to_all | solution.py:122
  51.5 0.3 fusion.9
  51.7 12.6 %all_to_all.26 = f32[16,16,256]{2,1,0:T(8,128)S(1)} all-to-all(f32[16,16,256]{2,1,0:T(8,128)S(1)} %fusion.9), channel_id=1, replica_groups=mesh['groups'=2,'blk'=16] {'blk'}, dimensions={0} | all-to-all | bytes 524288 | tf_op jit(solution)/shard_map/all_to_all | solution.py:124
  64.4 0.6 broadcast_multiply_fusion
  (28 shorter events, 0.5 us)
Async XLA Ops:
  0.0 8.2 %copy-start.1 = (s32[6144]{0:T(1024)S(1)}, s32[6144]{0:T(1024)}, u32[]{:S(2)}) copy-start(s32[6144]{0:T(1024)} %param.9) | copy-start | bytes 73732
  1.1 9.7 %collective-permute-start.1 = (f32[3,6144]{1,0:T(4,128)S(1)}, f32[3,6144]{1,0:T(4,128)S(1)}, u32[]{:S(2)}, u32[]{:S(2)}) collective-permute-start(f32[3,6144]{1,0:T(4,128)S(1)} %get-tuple-element.34), channel_id=1, source_target_pairs={{2,1},{4,3},{6,5},{8,7},{10,9},{12,11},{14,13},{1,2},{3,4},{5,6},{... | collective-permute-start | bytes 221192 | tf_op jit(solution)/shard_map/ppermute | solution.py:23
  1.8 9.0 %collective-permute-start = (f32[3,6144]{1,0:T(4,128)S(1)}, f32[3,6144]{1,0:T(4,128)S(1)}, u32[]{:S(2)}, u32[]{:S(2)}) collective-permute-start(f32[3,6144]{1,0:T(4,128)S(1)} %get-tuple-element.35), channel_id=1, source_target_pairs={{0,1},{1,0},{2,3},{3,2},{4,5},{5,4},{6,7},{7,6},{8,9},{9,8},{10,11... | collective-permute-start | bytes 221192 | tf_op jit(solution)/shard_map/ppermute | solution.py:20
  6.8 0.7 %copy-start.3 = (s32[2]{0:T(128)S(1)}, s32[2]{0:T(128)}, u32[]{:S(2)}) copy-start(s32[2]{0:T(128)} %constant.106.clone.1) | copy-start | bytes 28
  9.0 1.0 %copy-start = (f32[16,6144]{1,0:T(8,128)S(1)}, f32[16,6144]{1,0:T(8,128)}, u32[]{:S(2)}) copy-start(f32[16,6144]{1,0:T(8,128)} %param.8) | copy-start | bytes 1179652
  22.1 1.3 %collective-permute-start.2 = (f32[6144]{0:T(1024)S(1)}, f32[6144]{0:T(1024)S(1)}, u32[]{:S(2)}, u32[]{:S(2)}) collective-permute-start(f32[6144]{0:T(1024)S(1)} %slice_add_fusion.18), channel_id=1, source_target_pairs={{0,1},{1,0},{2,3},{3,2},{4,5},{5,4},{6,7},{7,6},{8,9},{9,8},{10,11... | collective-permute-start | bytes 73736 | tf_op jit(solution)/shard_map/ppermute | solution.py:114
  23.4 3.8 %collective-permute-start.3 = (f32[6144]{0:T(1024)S(1)}, f32[6144]{0:T(1024)S(1)}, u32[]{:S(2)}, u32[]{:S(2)}) collective-permute-start(f32[6144]{0:T(1024)S(1)} %add.154), channel_id=1, source_target_pairs={{0,2},{1,3},{2,0},{3,1},{4,6},{5,7},{6,4},{7,5},{8,10},{9,11},{10,... | collective-permute-start | bytes 73736 | tf_op jit(solution)/shard_map/ppermute | solution.py:114
  27.2 6.5 %copy-start.2 = (s32[384]{0:T(512)S(1)}, s32[384]{0:T(512)}, u32[]{:S(2)}) copy-start(s32[384]{0:T(512)} %param.10) | copy-start | bytes 4612
  27.2 3.9 %collective-permute-start.4 = (f32[6144]{0:T(1024)S(1)}, f32[6144]{0:T(1024)S(1)}, u32[]{:S(2)}, u32[]{:S(2)}) collective-permute-start(f32[6144]{0:T(1024)S(1)} %add.155), channel_id=1, source_target_pairs={{0,4},{1,5},{2,6},{3,7},{4,0},{5,1},{6,2},{7,3},{8,12},{9,13},{10,... | collective-permute-start | bytes 73736 | tf_op jit(solution)/shard_map/ppermute | solution.py:114
  31.1 5.6 %collective-permute-start.5 = (f32[6144]{0:T(1024)S(1)}, f32[6144]{0:T(1024)S(1)}, u32[]{:S(2)}, u32[]{:S(2)}) collective-permute-start(f32[6144]{0:T(1024)S(1)} %add.156), channel_id=1, source_target_pairs={{0,8},{1,9},{2,10},{3,11},{4,12},{5,13},{6,14},{7,15},{8,0},{9,1},... | collective-permute-start | bytes 73736 | tf_op jit(solution)/shard_map/ppermute | solution.py:114

commit v10 on v9

--- a/solution.py
+++ b/solution.py
@@ -137,13 +137,14 @@
     radius_map = skewed_map(widths, window_first, rows_here, col_count)
     own = lax.optimization_barrier(jnp.pad(contacts, WMAX))
     halo = with_halo(contacts, (("blk", 0),), WMAX)
-    padded = own.at[:WMAX, WMAX:-WMAX].set(halo[:WMAX]).at[-WMAX:, WMAX:-WMAX].set(halo[-WMAX:])
+    padded = lax.dynamic_update_slice(own, halo[:WMAX], (0, WMAX))
+    padded = lax.dynamic_update_slice(padded, halo[-WMAX:], (rows_here + WMAX, WMAX))
     smoothed = smooth(padded, radius_map)
     local_total = diagonal_totals(smoothed, window_first)
     denominator = pair_counts(first_bin, nbins, col_count)
     expected = tree_sum(local_total, "blk") / denominator
     expected_map = skewed_map(expected, window_first, rows_here, col_count)
-    kept_bins = jnp.ones((col_count,), jnp.float32).at[masked_bins].set(0.0, unique_indices=True)
+    kept_bins = jnp.ones((col_count,), jnp.float32).at[masked_bins].set(0.0)
     kept_rows = lax.dynamic_slice_in_dim(kept_bins, first_bin + first_row, rows_here)
     kept_total = jnp.float32(col_count - masked_bins.shape[0])
     zscores = normalize(smoothed, expected_map, kept_rows, kept_bins, kept_total)

time: 65.3 us -> 60.8 us (0.931)
  other arithmetic: 7.16 us -> 4.57 us
  local copies, waits for them, and re-layouts: 14.4 us -> 12 us
  starting transfers between devices: 10.9 us -> 12.5 us
  waiting for transfers between devices: 5.74 us -> 4.8 us
    scatter x3 -> x1, local copies, waits for them, and re-layouts: 9.2 us -> 2.95 us  [shards(): kept_bins = jnp.ones((col_count,), jnp.float32).at[masked_bins].set(0.0)]
    dynamic_update_slice x0 -> x2, local copies, waits for them, and re-layouts: none -> 5.05 us  [the longest x1 2.82 us: shards(): padded = lax.dynamic_update_slice(own, halo[:WMAX], (0, WMAX))]
    select_n x1, other arithmetic: 1.97 us -> 0.04 us  [with_halo(): after = jnp.where(odd, outer, inner)]
    ppermute x4, starting transfers between devices: 5.83 us -> 7.37 us  [tree_sum(): lax.ppermute(values, axis, [(i, i ^ step) for i in range(count)])]
    ppermute x4, waiting for transfers between devices: 5.74 us -> 4.79 us  [tree_sum(): lax.ppermute(values, axis, [(i, i ^ step) for i in range(count)])]
    another operation x2 -> x0, other arithmetic: 0.66 us -> none
    unnamed x14 -> x12, local copies, waits for them, and re-layouts: 1.86 us -> 1.21 us
  transfers between devices with their start and end apart: 6 -> 6, of which waited for: 3 -> 3; matrix products, arithmetic and copies ran while one was open for 9% -> 7% of each run, Pallas kernels for 0% -> 0%
where the time goes in v10:
time: 60.8 us; the launch traced here: 60.6 us
  blocking collectives  25.6 us (42%)
  starting transfers between devices  12.5 us (21%)
  local copies, waits for them, and re-layouts  12 us (20%)
  waiting for transfers between devices  4.8 us (8%)
  other arithmetic  4.57 us (8%)
  between operations  0.93 us (2%)
    all_to_all x1, blocking collectives, gram_rows(): columns = lax.all_to_all(zscores, axis, 1, 0, tiled=True)  13 us
    all_to_all x1, blocking collectives, gram_rows(): pieces = lax.all_to_all(partial, axis, 0, 0, tiled=True)  12.6 us
    ppermute x4, starting transfers between devices, tree_sum(): lax.ppermute(values, axis, [(i, i ^ step) for i in range(count)])  7.37 us
    ppermute x4, waiting for transfers between devices, tree_sum(): lax.ppermute(values, axis, [(i, i ^ step) for i in range(count)])  4.79 us
    ppermute x1, starting transfers between devices, with_halo(): lax.ppermute(jnp.where(odd, head, tail), axis, [(i, i ^ 1) for i in range...  4.42 us
    scatter x1, local copies, waits for them, and re-layouts, shards(): kept_bins = jnp.ones((col_count,), jnp.float32).at[masked_bins].set(0.0)  2.95 us
    dynamic_update_slice x1, local copies, waits for them, and re-layouts, shards(): padded = lax.dynamic_update_slice(own, halo[:WMAX], (0, WMAX))  2.82 us
    dynamic_update_slice x1, local copies, waits for them, and re-layouts, shards(): lax.dynamic_update_slice(padded, halo[-WMAX:], (rows_here + WMAX, WMAX))  2.23 us
  transfers between devices with their start and end apart: 6, of which 3 were waited for; matrix products, arithmetic and copies ran while one was open for 7% of the time, Pallas kernels for 0%

profile of v10, /device:TPU:0, one launch (start us, length us, event | category | flops | bytes accessed | tf_op | source)
XLA Modules:
  0.0 60.6 jit_solution(9758399250735221219)
XLA Ops:
  0.0 1.1 %slice_select_fusion.1 = (f32[3,6144]{1,0:T(4,128)S(1)}, f32[3,6144]{1,0:T(4,128)S(1)}) fusion(f32[16,6144]{1,0:T(8,128)} %param.4, pred[]{:T(512)S(6)} %eq.37), kind=kLoop, calls=%fused_computation.37 | loop fusion | flops 36864 | bytes 294913 | tf_op jit(solution)/shard_map/jit(_where)/select_n | solution.py:24
  1.1 0.7 %collective-permute-start.1 = (f32[3,6144]{1,0:T(4,128)S(1)}, f32[3,6144]{1,0:T(4,128)S(1)}, u32[]{:S(2)}, u32[]{:S(2)}) collective-permute-start(f32[3,6144]{1,0:T(4,128)S(1)} %get-tuple-element.10), channel_id=1, source_target_pairs={{2,1},{4,3},{6,5},{8,7},{10,9},{12,11},{14,13},{1,2},{3,4},{5,6},{... | collective-permute-start | bytes 221192 | tf_op jit(solution)/shard_map/ppermute | solution.py:23
  1.8 4.4 %collective-permute-start = (f32[3,6144]{1,0:T(4,128)S(1)}, f32[3,6144]{1,0:T(4,128)S(1)}, u32[]{:S(2)}, u32[]{:S(2)}) collective-permute-start(f32[3,6144]{1,0:T(4,128)S(1)} %get-tuple-element.11), channel_id=1, source_target_pairs={{0,1},{1,0},{2,3},{3,2},{4,5},{5,4},{6,7},{7,6},{8,9},{9,8},{10,11... | collective-permute-start | bytes 221192 | tf_op jit(solution)/shard_map/ppermute | solution.py:20
  6.8 0.1 slice.103
  6.9 0.1 reverse
  7.0 0.1 slice.247
  7.1 0.1 fusion.12
  7.2 0.2 tile.9
  7.5 0.2 slice.137
  7.6 0.0 copy-start
  7.7 0.3 reshape.37
  7.9 0.7 %copy-done = f32[16,6144]{1,0:T(8,128)S(1)} copy-done((f32[16,6144]{1,0:T(8,128)S(1)}, f32[16,6144]{1,0:T(8,128)}, u32[]{:S(2)}) %copy-start) | copy-done | bytes 393240
  8.6 0.2 pad.12
  8.9 2.8 %dynamic_update_slice.9 = f32[22,6150]{1,0:T(8,128)S(1)} dynamic-update-slice(f32[22,6150]{1,0:T(8,128)S(1)} %pad.12, f32[3,6144]{1,0:T(4,128)S(1)} %get-tuple-element.13, s32[]{:T(128)} %constant.24.clone.1, s32[]{:T(128)} %constant.29.clone.1) | dynamic-update-slice | bytes 147460 | tf_op jit(solution)/shard_map/dynamic_update_slice | solution.py:140
  11.8 2.2 %dynamic_update_slice.10 = f32[22,6150]{1,0:T(8,128)S(1)} dynamic-update-slice(f32[22,6150]{1,0:T(8,128)S(1)} %dynamic_update_slice.9, f32[3,6144]{1,0:T(4,128)S(1)} %get-tuple-element.12, s32[]{:T(128)} %constant.30.clone.1, s32[]{:T(128)} %constant.29.clone.1) | dynamic-update-slice | bytes 147460 | tf_op jit(solution)/shard_map/dynamic_update_slice | solution.py:141
  14.0 0.2 slice_add_fusion
  14.2 1.6 %fusion.2 = f32[16,6144]{1,0:T(8,128)S(1)} fusion(f32[16,6150]{1,0:T(8,128)S(1)} %get-tuple-element.7, f32[16,6150]{1,0:T(8,128)S(1)} %get-tuple-element.8, f32[16,6150]{1,0:T(8,128)S(1)} %get-tuple-element.9, f32[22,6150]{1,0:T(8,128)S(1)} %dynamic_update_slice.10, s32[16,6158]{1,0:T(8,128)S(1)} %reshape.37), kind=kLoop, calls=%fused_computation.11 | loop fusion | flops 2555904 | bytes 7077888 | tf_op jit(solution)/shard_map/add | solution.py:54
  15.8 0.2 pad.13
  16.0 0.2 reshape.38
  16.3 0.2 reshape.39
  16.5 0.1 reduce_sum.36
  16.6 0.2 slice_dynamic-update-slice_fusion
  16.8 0.1 reverse.1
  16.9 0.1 slice.248
  17.0 0.1 slice_add_fusion.18
  17.1 0.1 collective-permute-start.2
  17.2 1.2 %collective-permute-done.2 = f32[6144]{0:T(1024)S(1)} collective-permute-done((f32[6144]{0:T(1024)S(1)}, f32[6144]{0:T(1024)S(1)}, u32[]{:S(2)}, u32[]{:S(2)}) %collective-permute-start.2) | collective-permute-done | bytes 24608 | tf_op jit(solution)/shard_map/ppermute | solution.py:114
  18.3 2.2 %collective-permute-start.3 = (f32[6144]{0:T(1024)S(1)}, f32[6144]{0:T(1024)S(1)}, u32[]{:S(2)}, u32[]{:S(2)}) collective-permute-start(f32[6144]{0:T(1024)S(1)} %add.150), channel_id=1, source_target_pairs={{0,2},{1,3},{2,0},{3,1},{4,6},{5,7},{6,4},{7,5},{8,10},{9,11},{10,... | collective-permute-start | bytes 73736 | tf_op jit(solution)/shard_map/ppermute | solution.py:114
  20.5 1.8 %collective-permute-done.3 = f32[6144]{0:T(1024)S(1)} collective-permute-done((f32[6144]{0:T(1024)S(1)}, f32[6144]{0:T(1024)S(1)}, u32[]{:S(2)}, u32[]{:S(2)}) %collective-permute-start.3) | collective-permute-done | bytes 24608 | tf_op jit(solution)/shard_map/ppermute | solution.py:114
  22.3 2.1 %collective-permute-start.4 = (f32[6144]{0:T(1024)S(1)}, f32[6144]{0:T(1024)S(1)}, u32[]{:S(2)}, u32[]{:S(2)}) collective-permute-start(f32[6144]{0:T(1024)S(1)} %add.151), channel_id=1, source_target_pairs={{0,4},{1,5},{2,6},{3,7},{4,0},{5,1},{6,2},{7,3},{8,12},{9,13},{10,... | collective-permute-start | bytes 73736 | tf_op jit(solution)/shard_map/ppermute | solution.py:114
  24.4 1.8 %collective-permute-done.4 = f32[6144]{0:T(1024)S(1)} collective-permute-done((f32[6144]{0:T(1024)S(1)}, f32[6144]{0:T(1024)S(1)}, u32[]{:S(2)}, u32[]{:S(2)}) %collective-permute-start.4) | collective-permute-done | bytes 24608 | tf_op jit(solution)/shard_map/ppermute | solution.py:114
  26.2 3.0 %collective-permute-start.5 = (f32[6144]{0:T(1024)S(1)}, f32[6144]{0:T(1024)S(1)}, u32[]{:S(2)}, u32[]{:S(2)}) collective-permute-start(f32[6144]{0:T(1024)S(1)} %add.152), channel_id=1, source_target_pairs={{0,8},{1,9},{2,10},{3,11},{4,12},{5,13},{6,14},{7,15},{8,0},{9,1},... | collective-permute-start | bytes 73736 | tf_op jit(solution)/shard_map/ppermute | solution.py:114
  29.3 2.9 %scatter_custom_fusion = f32[6144]{0:T(1024)S(1)} fusion(s32[384]{0:T(512)S(1)} %compare_select_fusion, f32[384]{0:T(512)S(1)} %broadcast.40, f32[]{:T(128)} %constant.70.clone.1), kind=kCustom, calls=%fused_computation.51 | custom fusion | bytes 24580 | tf_op jit(solution)/shard_map/scatter | solution.py:147
  32.2 0.1 dynamic_slice.11
  32.3 0.1 slice.165
  32.4 0.1 reverse.2
  32.5 0.1 slice.249
  32.6 0.1 fusion.11
  32.7 0.2 tile.21
  33.0 0.2 slice.166
  33.1 0.3 reshape.40
  33.4 0.2 multiply_reduce_fusion.1
  33.6 0.3 multiply_reduce_fusion
  33.9 0.1 multiply_convert_fusion
  34.1 13.0 %all_to_all.25 = bf16[16,16,384]{2,0,1:T(8,128)(2,1)S(1)} all-to-all(bf16[16,16,384]{2,0,1:T(8,128)(2,1)S(1)} %bitcast.21), channel_id=1, replica_groups=mesh['groups'=2,'blk'=16] {'blk'}, dimensions={1} | all-to-all | bytes 393216 | tf_op jit(solution)/shard_map/all_to_all | solution.py:122
  47.0 0.3 fusion.9
  47.3 12.6 %all_to_all.26 = f32[16,16,256]{2,1,0:T(8,128)S(1)} all-to-all(f32[16,16,256]{2,1,0:T(8,128)S(1)} %fusion.9), channel_id=1, replica_groups=mesh['groups'=2,'blk'=16] {'blk'}, dimensions={0} | all-to-all | bytes 524288 | tf_op jit(solution)/shard_map/all_to_all | solution.py:124
  59.9 0.6 %broadcast_multiply_fusion = f32[16,256]{1,0:T(8,128)} fusion(f32[16,256]{1,0:T(8,128)S(1)} %reduce_sum.39), kind=kLoop, calls=%fused_computation.53 | loop fusion | flops 4096 | bytes 32768 | tf_op jit(solution)/shard_map/div | solution.py:151
  (23 shorter events, 0.3 us)
Async XLA Ops:
  0.0 6.8 %copy-start.1 = (s32[6144]{0:T(1024)S(1)}, s32[6144]{0:T(1024)}, u32[]{:S(2)}) copy-start(s32[6144]{0:T(1024)} %param.5) | copy-start | bytes 73732
  1.1 7.8 %collective-permute-start.1 = (f32[3,6144]{1,0:T(4,128)S(1)}, f32[3,6144]{1,0:T(4,128)S(1)}, u32[]{:S(2)}, u32[]{:S(2)}) collective-permute-start(f32[3,6144]{1,0:T(4,128)S(1)} %get-tuple-element.10), channel_id=1, source_target_pairs={{2,1},{4,3},{6,5},{8,7},{10,9},{12,11},{14,13},{1,2},{3,4},{5,6},{... | collective-permute-start | bytes 221192 | tf_op jit(solution)/shard_map/ppermute | solution.py:23
  1.8 7.1 %collective-permute-start = (f32[3,6144]{1,0:T(4,128)S(1)}, f32[3,6144]{1,0:T(4,128)S(1)}, u32[]{:S(2)}, u32[]{:S(2)}) collective-permute-start(f32[3,6144]{1,0:T(4,128)S(1)} %get-tuple-element.11), channel_id=1, source_target_pairs={{0,1},{1,0},{2,3},{3,2},{4,5},{5,4},{6,7},{7,6},{8,9},{9,8},{10,11... | collective-permute-start | bytes 221192 | tf_op jit(solution)/shard_map/ppermute | solution.py:20
  7.6 1.0 %copy-start = (f32[16,6144]{1,0:T(8,128)S(1)}, f32[16,6144]{1,0:T(8,128)}, u32[]{:S(2)}) copy-start(f32[16,6144]{1,0:T(8,128)} %param.4) | copy-start | bytes 1179652
  17.1 1.3 %collective-permute-start.2 = (f32[6144]{0:T(1024)S(1)}, f32[6144]{0:T(1024)S(1)}, u32[]{:S(2)}, u32[]{:S(2)}) collective-permute-start(f32[6144]{0:T(1024)S(1)} %slice_add_fusion.18), channel_id=1, source_target_pairs={{0,1},{1,0},{2,3},{3,2},{4,5},{5,4},{6,7},{7,6},{8,9},{9,8},{10,11... | collective-permute-start | bytes 73736 | tf_op jit(solution)/shard_map/ppermute | solution.py:114
  18.3 4.0 %collective-permute-start.3 = (f32[6144]{0:T(1024)S(1)}, f32[6144]{0:T(1024)S(1)}, u32[]{:S(2)}, u32[]{:S(2)}) collective-permute-start(f32[6144]{0:T(1024)S(1)} %add.150), channel_id=1, source_target_pairs={{0,2},{1,3},{2,0},{3,1},{4,6},{5,7},{6,4},{7,5},{8,10},{9,11},{10,... | collective-permute-start | bytes 73736 | tf_op jit(solution)/shard_map/ppermute | solution.py:114
  22.3 6.9 %copy-start.2 = (s32[384]{0:T(512)S(1)}, s32[384]{0:T(512)}, u32[]{:S(2)}) copy-start(s32[384]{0:T(512)} %param.6) | copy-start | bytes 4612
  22.3 3.9 %collective-permute-start.4 = (f32[6144]{0:T(1024)S(1)}, f32[6144]{0:T(1024)S(1)}, u32[]{:S(2)}, u32[]{:S(2)}) collective-permute-start(f32[6144]{0:T(1024)S(1)} %add.151), channel_id=1, source_target_pairs={{0,4},{1,5},{2,6},{3,7},{4,0},{5,1},{6,2},{7,3},{8,12},{9,13},{10,... | collective-permute-start | bytes 73736 | tf_op jit(solution)/shard_map/ppermute | solution.py:114
  26.2 6.1 %collective-permute-start.5 = (f32[6144]{0:T(1024)S(1)}, f32[6144]{0:T(1024)S(1)}, u32[]{:S(2)}, u32[]{:S(2)}) collective-permute-start(f32[6144]{0:T(1024)S(1)} %add.152), channel_id=1, source_target_pairs={{0,8},{1,9},{2,10},{3,11},{4,12},{5,13},{6,14},{7,15},{8,0},{9,1},... | collective-permute-start | bytes 73736 | tf_op jit(solution)/shard_map/ppermute | solution.py:114

commit v11 on v7

--- a/solution.py
+++ b/solution.py
@@ -142,7 +142,8 @@
     denominator = pair_counts(first_bin, nbins, col_count)
     expected = tree_sum(local_total, "blk") / denominator
     expected_map = skewed_map(expected, window_first, rows_here, col_count)
-    kept_bins = jnp.ones((col_count,), jnp.float32).at[masked_bins].set(0.0)
+    hit = masked_bins[:, None] == jnp.arange(col_count, dtype=masked_bins.dtype)[None, :]
+    kept_bins = jnp.where(jnp.any(hit, axis=0), 0.0, 1.0).astype(jnp.float32)
     kept_rows = lax.dynamic_slice_in_dim(kept_bins, first_bin + first_row, rows_here)
     kept_total = jnp.float32(col_count - masked_bins.shape[0])
     zscores = normalize(smoothed, expected_map, kept_rows, kept_bins, kept_total)

time: 56.3 us -> 56.3 us (level)
  local copies, waits for them, and re-layouts: 6.89 us -> 4.41 us
  other arithmetic: 4.8 us -> 6.17 us
  blocking collectives: 25.6 us -> 26.8 us
    scatter x1 -> x0, local copies, waits for them, and re-layouts: 2.95 us -> none  [shards(): kept_bins = jnp.ones((col_count,), jnp.float32).at[masked_bins].set(0.0)]
    reduce_or x0 -> x1, other arithmetic: none -> 1.35 us  [shards(): kept_bins = jnp.where(jnp.any(hit, axis=0), 0.0, 1.0).astype(jnp.float32)]
    all_to_all x1, blocking collectives: 13 us -> 14.2 us  [gram_rows(): columns = lax.all_to_all(zscores, axis, 1, 0, tiled=True)]
    slice x2, local copies, waits for them, and re-layouts: 0.15 us -> 0.89 us  [mirrored_table(): return jnp.concatenate([table[1:][::-1], table])]
  transfers between devices with their start and end apart: 6 -> 6, of which waited for: 3 -> 4; matrix products, arithmetic and copies ran while one was open for 7% -> 6% of each run, Pallas kernels for 0% -> 0%
where the time goes in v11:
time: 56.3 us; the launch traced here: 56 us
  blocking collectives  26.8 us (48%)
  starting transfers between devices  12.6 us (22%)
  other arithmetic  6.17 us (11%)
  waiting for transfers between devices  4.83 us (9%)
  local copies, waits for them, and re-layouts  4.41 us (8%)
  between operations  0.9 us (2%)
    all_to_all x1, blocking collectives, gram_rows(): columns = lax.all_to_all(zscores, axis, 1, 0, tiled=True)  14.2 us
    all_to_all x1, blocking collectives, gram_rows(): pieces = lax.all_to_all(partial, axis, 0, 0, tiled=True)  12.6 us
    ppermute x4, starting transfers between devices, tree_sum(): lax.ppermute(values, axis, [(i, i ^ step) for i in range(count)])  11.4 us
    ppermute x4, waiting for transfers between devices, tree_sum(): lax.ppermute(values, axis, [(i, i ^ step) for i in range(count)])  4.82 us
    add x1, other arithmetic, smooth(): smoothed + jnp.where(radius_map == radius, box_sums / float((2 * radius +...  1.51 us
    reduce_or x1, other arithmetic, shards(): kept_bins = jnp.where(jnp.any(hit, axis=0), 0.0, 1.0).astype(jnp.float32)  1.35 us
    unnamed x12, local copies, waits for them, and re-layouts  1.14 us
  transfers between devices with their start and end apart: 6, of which 4 were waited for; matrix products, arithmetic and copies ran while one was open for 6% of the time, Pallas kernels for 0%

profile of v11, /device:TPU:0, one launch (start us, length us, event | category | flops | bytes accessed | tf_op | source)
XLA Modules:
  0.0 56.0 jit_solution(7389066024513561603)
XLA Ops:
  0.0 1.1 %slice_select_fusion.1 = (f32[3,6144]{1,0:T(4,128)S(1)}, f32[3,6144]{1,0:T(4,128)S(1)}) fusion(f32[16,6144]{1,0:T(8,128)} %param.4, pred[]{:T(512)S(6)} %eq.52), kind=kLoop, calls=%fused_computation.43 | loop fusion | flops 36864 | bytes 294913 | tf_op jit(solution)/shard_map/jit(_where)/select_n | solution.py:21
  1.1 0.6 collective-permute-start
  1.6 0.7 %collective-permute-start.1 = (f32[3,6144]{1,0:T(4,128)S(1)}, f32[3,6144]{1,0:T(4,128)S(1)}, u32[]{:S(2)}, u32[]{:S(2)}) collective-permute-start(f32[3,6144]{1,0:T(4,128)S(1)} %get-tuple-element.11), channel_id=1, source_target_pairs={{2,1},{4,3},{6,5},{8,7},{10,9},{12,11},{14,13},{1,2},{3,4},{5,6},{... | collective-permute-start | bytes 221192 | tf_op jit(solution)/shard_map/ppermute | solution.py:23
  3.0 0.8 %slice.102 = s32[6143]{0:T(1024)S(1)} slice(s32[6144]{0:T(1024)} %param.5), slice={[1:6144]} | slice | bytes 49144 | tf_op jit(solution)/shard_map/slice | solution.py:69
  3.8 0.1 reverse
  3.8 0.1 slice.241
  3.9 0.1 fusion.14
  4.1 0.2 tile.9
  4.3 0.2 slice.135
  4.5 0.0 copy-start
  4.5 0.3 reshape.40
  4.8 0.7 %copy-done = f32[16,6144]{1,0:T(8,128)S(1)} copy-done((f32[16,6144]{1,0:T(8,128)S(1)}, f32[16,6144]{1,0:T(8,128)}, u32[]{:S(2)}) %copy-start) | copy-done | bytes 393240
  5.5 0.3 select_maximum_fusion
  5.8 0.2 slice_add_fusion
  6.1 1.5 %fusion.4 = f32[16,6144]{1,0:T(8,128)S(1)} fusion(f32[16,6150]{1,0:T(8,128)S(1)} %get-tuple-element.7, f32[16,6150]{1,0:T(8,128)S(1)} %get-tuple-element.8, f32[16,6150]{1,0:T(8,128)S(1)} %get-tuple-element.9, f32[16,6144]{1,0:T(8,128)S(1)} %copy-done, s32[16,6158]{1,0:T(8,128)S(1)} %reshape.40), kind=kLoop, calls=%fused_computation.17 | loop fusion | flops 2555904 | bytes 7077888 | tf_op jit(solution)/shard_map/add | solution.py:54
  7.6 0.2 pad.13
  7.8 0.2 reshape.41
  8.0 0.2 reshape.42
  8.3 0.0 copy-start.2
  8.3 0.1 reduce_sum.36
  8.4 0.2 slice_dynamic-update-slice_fusion
  8.6 0.1 reverse.1
  8.7 0.1 slice.242
  8.8 0.1 slice_add_fusion.18
  8.8 4.0 %collective-permute-start.2 = (f32[6144]{0:T(1024)S(1)}, f32[6144]{0:T(1024)S(1)}, u32[]{:S(2)}, u32[]{:S(2)}) collective-permute-start(f32[6144]{0:T(1024)S(1)} %slice_add_fusion.18), channel_id=1, source_target_pairs={{0,1},{1,0},{2,3},{3,2},{4,5},{5,4},{6,7},{7,6},{8,9},{9,8},{10,11... | collective-permute-start | bytes 73736 | tf_op jit(solution)/shard_map/ppermute | solution.py:114
  12.8 0.8 %collective-permute-done.2 = f32[6144]{0:T(1024)S(1)} collective-permute-done((f32[6144]{0:T(1024)S(1)}, f32[6144]{0:T(1024)S(1)}, u32[]{:S(2)}, u32[]{:S(2)}) %collective-permute-start.2) | collective-permute-done | bytes 24608 | tf_op jit(solution)/shard_map/ppermute | solution.py:114
  13.7 2.1 %collective-permute-start.3 = (f32[6144]{0:T(1024)S(1)}, f32[6144]{0:T(1024)S(1)}, u32[]{:S(2)}, u32[]{:S(2)}) collective-permute-start(f32[6144]{0:T(1024)S(1)} %add.144), channel_id=1, source_target_pairs={{0,2},{1,3},{2,0},{3,1},{4,6},{5,7},{6,4},{7,5},{8,10},{9,11},{10,... | collective-permute-start | bytes 73736 | tf_op jit(solution)/shard_map/ppermute | solution.py:114
  15.8 1.8 %collective-permute-done.3 = f32[6144]{0:T(1024)S(1)} collective-permute-done((f32[6144]{0:T(1024)S(1)}, f32[6144]{0:T(1024)S(1)}, u32[]{:S(2)}, u32[]{:S(2)}) %collective-permute-start.3) | collective-permute-done | bytes 24608 | tf_op jit(solution)/shard_map/ppermute | solution.py:114
  17.6 2.2 %collective-permute-start.4 = (f32[6144]{0:T(1024)S(1)}, f32[6144]{0:T(1024)S(1)}, u32[]{:S(2)}, u32[]{:S(2)}) collective-permute-start(f32[6144]{0:T(1024)S(1)} %add.145), channel_id=1, source_target_pairs={{0,4},{1,5},{2,6},{3,7},{4,0},{5,1},{6,2},{7,3},{8,12},{9,13},{10,... | collective-permute-start | bytes 73736 | tf_op jit(solution)/shard_map/ppermute | solution.py:114
  19.8 1.4 %fusion = pred[6144]{0:T(1024)(128)(4,1)S(1)} fusion(s32[384]{0:T(512)S(1)} %copy-done.2), kind=kLoop, calls=%fused_computation.1 | loop fusion | flops 4712448 | bytes 7680 | tf_op jit(solution)/shard_map/reduce_or | solution.py:146
  21.2 0.4 collective-permute-done.4
  21.6 3.0 %collective-permute-start.5 = (f32[6144]{0:T(1024)S(1)}, f32[6144]{0:T(1024)S(1)}, u32[]{:S(2)}, u32[]{:S(2)}) collective-permute-start(f32[6144]{0:T(1024)S(1)} %add.146), channel_id=1, source_target_pairs={{0,8},{1,9},{2,10},{3,11},{4,12},{5,13},{6,14},{7,15},{8,0},{9,1},... | collective-permute-start | bytes 73736 | tf_op jit(solution)/shard_map/ppermute | solution.py:114
  24.7 0.1 dynamic_slice.11
  24.8 1.7 %collective-permute-done.5 = f32[6144]{0:T(1024)S(1)} collective-permute-done((f32[6144]{0:T(1024)S(1)}, f32[6144]{0:T(1024)S(1)}, u32[]{:S(2)}, u32[]{:S(2)}) %collective-permute-start.5) | collective-permute-done | bytes 24608 | tf_op jit(solution)/shard_map/ppermute | solution.py:114
  26.5 0.1 slice.162
  26.6 0.1 reverse.2
  26.7 0.1 slice.243
  26.7 0.1 fusion.13
  26.9 0.2 tile.21
  27.1 0.2 slice.163
  27.3 0.3 reshape.43
  27.6 0.2 multiply_reduce_fusion.1
  27.8 0.3 multiply_reduce_fusion
  28.1 0.1 multiply_convert_fusion
  28.2 14.2 %all_to_all.25 = bf16[16,16,384]{2,0,1:T(8,128)(2,1)S(1)} all-to-all(bf16[16,16,384]{2,0,1:T(8,128)(2,1)S(1)} %bitcast.20), channel_id=1, replica_groups=mesh['groups'=2,'blk'=16] {'blk'}, dimensions={1} | all-to-all | bytes 393216 | tf_op jit(solution)/shard_map/all_to_all | solution.py:122
  42.5 0.3 fusion.11
  42.7 12.6 %all_to_all.26 = f32[16,16,256]{2,1,0:T(8,128)S(1)} all-to-all(f32[16,16,256]{2,1,0:T(8,128)S(1)} %fusion.11), channel_id=1, replica_groups=mesh['groups'=2,'blk'=16] {'blk'}, dimensions={0} | all-to-all | bytes 524288 | tf_op jit(solution)/shard_map/all_to_all | solution.py:124
  55.4 0.6 %broadcast_multiply_fusion = f32[16,256]{1,0:T(8,128)} fusion(f32[16,256]{1,0:T(8,128)S(1)} %reduce_sum.39), kind=kLoop, calls=%fused_computation.57 | loop fusion | flops 4096 | bytes 32768 | tf_op jit(solution)/shard_map/div | solution.py:150
  (20 shorter events, 0.3 us)
Async XLA Ops:
  0.0 3.9 %copy-start.1 = (s32[6144]{0:T(1024)S(1)}, s32[6144]{0:T(1024)}, u32[]{:S(2)}) copy-start(s32[6144]{0:T(1024)} %param.5) | copy-start | bytes 73732
  1.1 3.7 %collective-permute-start = (f32[3,6144]{1,0:T(4,128)S(1)}, f32[3,6144]{1,0:T(4,128)S(1)}, u32[]{:S(2)}, u32[]{:S(2)}) collective-permute-start(f32[3,6144]{1,0:T(4,128)S(1)} %get-tuple-element.10), channel_id=1, source_target_pairs={{0,1},{1,0},{2,3},{3,2},{4,5},{5,4},{6,7},{7,6},{8,9},{9,8},{10,11... | collective-permute-start | bytes 221192 | tf_op jit(solution)/shard_map/ppermute | solution.py:20
  1.6 3.2 %collective-permute-start.1 = (f32[3,6144]{1,0:T(4,128)S(1)}, f32[3,6144]{1,0:T(4,128)S(1)}, u32[]{:S(2)}, u32[]{:S(2)}) collective-permute-start(f32[3,6144]{1,0:T(4,128)S(1)} %get-tuple-element.11), channel_id=1, source_target_pairs={{2,1},{4,3},{6,5},{8,7},{10,9},{12,11},{14,13},{1,2},{3,4},{5,6},{... | collective-permute-start | bytes 221192 | tf_op jit(solution)/shard_map/ppermute | solution.py:23
  4.5 1.0 %copy-start = (f32[16,6144]{1,0:T(8,128)S(1)}, f32[16,6144]{1,0:T(8,128)}, u32[]{:S(2)}) copy-start(f32[16,6144]{1,0:T(8,128)} %param.4) | copy-start | bytes 1179652
  8.3 11.6 %copy-start.2 = (s32[384]{0:T(512)S(1)}, s32[384]{0:T(512)}, u32[]{:S(2)}) copy-start(s32[384]{0:T(512)} %param.6) | copy-start | bytes 4612
  8.8 4.8 %collective-permute-start.2 = (f32[6144]{0:T(1024)S(1)}, f32[6144]{0:T(1024)S(1)}, u32[]{:S(2)}, u32[]{:S(2)}) collective-permute-start(f32[6144]{0:T(1024)S(1)} %slice_add_fusion.18), channel_id=1, source_target_pairs={{0,1},{1,0},{2,3},{3,2},{4,5},{5,4},{6,7},{7,6},{8,9},{9,8},{10,11... | collective-permute-start | bytes 73736 | tf_op jit(solution)/shard_map/ppermute | solution.py:114
  13.7 3.9 %collective-permute-start.3 = (f32[6144]{0:T(1024)S(1)}, f32[6144]{0:T(1024)S(1)}, u32[]{:S(2)}, u32[]{:S(2)}) collective-permute-start(f32[6144]{0:T(1024)S(1)} %add.144), channel_id=1, source_target_pairs={{0,2},{1,3},{2,0},{3,1},{4,6},{5,7},{6,4},{7,5},{8,10},{9,11},{10,... | collective-permute-start | bytes 73736 | tf_op jit(solution)/shard_map/ppermute | solution.py:114
  17.6 4.0 %collective-permute-start.4 = (f32[6144]{0:T(1024)S(1)}, f32[6144]{0:T(1024)S(1)}, u32[]{:S(2)}, u32[]{:S(2)}) collective-permute-start(f32[6144]{0:T(1024)S(1)} %add.145), channel_id=1, source_target_pairs={{0,4},{1,5},{2,6},{3,7},{4,0},{5,1},{6,2},{7,3},{8,12},{9,13},{10,... | collective-permute-start | bytes 73736 | tf_op jit(solution)/shard_map/ppermute | solution.py:114
  21.6 4.8 %collective-permute-start.5 = (f32[6144]{0:T(1024)S(1)}, f32[6144]{0:T(1024)S(1)}, u32[]{:S(2)}, u32[]{:S(2)}) collective-permute-start(f32[6144]{0:T(1024)S(1)} %add.146), channel_id=1, source_target_pairs={{0,8},{1,9},{2,10},{3,11},{4,12},{5,13},{6,14},{7,15},{8,0},{9,1},... | collective-permute-start | bytes 73736 | tf_op jit(solution)/shard_map/ppermute | solution.py:114

commit v12 on v7

--- a/solution.py
+++ b/solution.py
@@ -65,19 +65,22 @@
     return jnp.maximum(pair_total, 1).astype(jnp.float32)
 
 
-def mirrored_table(table):
-    return jnp.concatenate([table[1:][::-1], table])
+def mirrored_table(table, margin=0):
+    mirrored = jnp.concatenate([table[1:][::-1], table])
+    return jnp.pad(mirrored, margin, mode="edge")
 
 
-def skewed_map(table, window_first, rows_here, col_count):
+def skewed_map(table, window_first, rows_here, col_count, margin=0):
     span = col_count + rows_here - 1
-    window = lax.dynamic_slice_in_dim(mirrored_table(table), window_first, span)
+    window = lax.dynamic_slice_in_dim(
+        mirrored_table(table, margin), window_first + margin, span
+    )
     tiled = jnp.tile(window, rows_here + 1)
     flat = tiled[rows_here - 1 : rows_here - 1 + rows_here * (span - 1)]
     return flat.reshape(rows_here, span - 1)[:, :col_count]
 
 
-def diagonal_totals(smoothed, window_first):
+def diagonal_totals(smoothed, window_first, margin=0):
     rows_here = smoothed.shape[0]
     col_count = smoothed.shape[1]
     span = col_count + rows_here - 1
@@ -85,8 +88,11 @@
     flat = jnp.pad(placed.reshape(rows_here * span), (0, rows_here))
     offsets = jnp.sum(flat.reshape(rows_here, span + 1), axis=0)[:span]
     spread = lax.dynamic_update_slice_in_dim(
-        jnp.zeros((2 * col_count - 1,), jnp.float32), offsets, window_first, 0
-    )
+        jnp.zeros((2 * col_count - 1 + 2 * margin,), jnp.float32),
+        offsets,
+        window_first + margin,
+        0,
+    )[margin : margin + 2 * col_count - 1]
     lower = jnp.concatenate([jnp.zeros((1,), jnp.float32), spread[: col_count - 1][::-1]])
     return spread[col_count - 1 :] + lower
 
@@ -134,11 +140,18 @@
     first_row = position * rows_here
     first_bin = row_start[0]
     window_first = col_count - 1 - (first_bin + first_row + rows_here - 1)
+    wide_rows = rows_here + 2 * WMAX
+    wide_first = window_first - WMAX
+    wide_radius = skewed_map(widths, wide_first, wide_rows, col_count, WMAX)
+    own = jnp.pad(contacts, ((2 * WMAX, 2 * WMAX), (WMAX, WMAX)))
+    target = first_row - WMAX + jnp.arange(wide_rows, dtype=jnp.int32)
+    inside = (target >= 0) & (target < nbins)
+    own_part = jnp.where(inside[:, None], smooth(own, wide_radius), 0.0)
+    local_total = diagonal_totals(own_part, wide_first, WMAX)
     radius_map = skewed_map(widths, window_first, rows_here, col_count)
     padded_rows = with_halo(contacts, (("blk", 0),), WMAX)
     padded = jnp.pad(padded_rows, ((0, 0), (WMAX, WMAX)))
-    smoothed = smooth(padded, radius_map)
-    local_total = diagonal_totals(smoothed, window_first)
+    smoothed = lax.optimization_barrier(smooth(padded, radius_map))
     denominator = pair_counts(first_bin, nbins, col_count)
     expected = tree_sum(local_total, "blk") / denominator
     expected_map = skewed_map(expected, window_first, rows_here, col_count)

time: 56.3 us -> 60 us (1.066)
  other arithmetic: 4.8 us -> 8.04 us
  local copies, waits for them, and re-layouts: 6.89 us -> 9.44 us
  starting transfers between devices: 13.1 us -> 10.9 us
  blocking collectives: 25.6 us -> 26.7 us
  waiting for transfers between devices: 4.47 us -> 3.51 us
    select_n x0 -> x1, other arithmetic: none -> 2.2 us  [shards(): own_part = jnp.where(inside[:, None], smooth(own, wide_radius), 0.0)]
    ppermute x4, starting transfers between devices: 11.9 us -> 9.7 us  [tree_sum(): lax.ppermute(values, axis, [(i, i ^ step) for i in range(count)])]
    add x1 -> x2, other arithmetic: 0.24 us -> 1.6 us  [smooth(): row_sums + padded[WMAX - radius:WMAX - radius + rows_here]]
    all_to_all x1, blocking collectives: 13 us -> 14 us  [gram_rows(): columns = lax.all_to_all(zscores, axis, 1, 0, tiled=True)]
    ppermute x4, waiting for transfers between devices: 4.46 us -> 3.5 us  [tree_sum(): lax.ppermute(values, axis, [(i, i ^ step) for i in range(count)])]
  transfers between devices with their start and end apart: 6 -> 6, of which waited for: 3 -> 3; matrix products, arithmetic and copies ran while one was open for 7% -> 13% of each run, Pallas kernels for 0% -> 0%
where the time goes in v12:
time: 60 us; the launch traced here: 59.8 us
  blocking collectives  26.7 us (44%)
  starting transfers between devices  10.9 us (18%)
  local copies, waits for them, and re-layouts  9.44 us (16%)
  other arithmetic  8.04 us (13%)
  waiting for transfers between devices  3.51 us (6%)
  between operations  0.97 us (2%)
    all_to_all x1, blocking collectives, gram_rows(): columns = lax.all_to_all(zscores, axis, 1, 0, tiled=True)  14 us
    all_to_all x1, blocking collectives, gram_rows(): pieces = lax.all_to_all(partial, axis, 0, 0, tiled=True)  12.6 us
    ppermute x4, starting transfers between devices, tree_sum(): lax.ppermute(values, axis, [(i, i ^ step) for i in range(count)])  9.7 us
    ppermute x4, waiting for transfers between devices, tree_sum(): lax.ppermute(values, axis, [(i, i ^ step) for i in range(count)])  3.5 us
    scatter x1, local copies, waits for them, and re-layouts, shards(): kept_bins = jnp.ones((col_count,), jnp.float32).at[masked_bins].set(0.0)  2.95 us
    select_n x1, other arithmetic, shards(): own_part = jnp.where(inside[:, None], smooth(own, wide_radius), 0.0)  2.2 us
    add x2, other arithmetic, smooth(): row_sums + padded[WMAX - radius:WMAX - radius + rows_here]  1.6 us
    add x1, other arithmetic, smooth(): smoothed + jnp.where(radius_map == radius, box_sums / float((2 * radius +...  1.49 us
  transfers between devices with their start and end apart: 6, of which 3 were waited for; matrix products, arithmetic and copies ran while one was open for 13% of the time, Pallas kernels for 0%

profile of v12, /device:TPU:0, one launch (start us, length us, event | category | flops | bytes accessed | tf_op | source)
XLA Modules:
  0.0 59.8 jit_solution(5316355955265601516)
XLA Ops:
  0.0 1.1 %slice_select_fusion.1 = (f32[3,6144]{1,0:T(4,128)S(1)}, f32[3,6144]{1,0:T(4,128)S(1)}) fusion(f32[16,6144]{1,0:T(8,128)} %param.4, pred[]{:T(512)S(6)} %eq.63), kind=kLoop, calls=%fused_computation.79 | loop fusion | flops 36864 | bytes 294913 | tf_op jit(solution)/shard_map/jit(_where)/select_n | solution.py:21
  1.1 0.6 collective-permute-start
  1.6 0.7 %collective-permute-start.1 = (f32[3,6144]{1,0:T(4,128)S(1)}, f32[3,6144]{1,0:T(4,128)S(1)}, u32[]{:S(2)}, u32[]{:S(2)}) collective-permute-start(f32[3,6144]{1,0:T(4,128)S(1)} %get-tuple-element.15), channel_id=1, source_target_pairs={{2,1},{4,3},{6,5},{8,7},{10,9},{12,11},{14,13},{1,2},{3,4},{5,6},{... | collective-permute-start | bytes 221192 | tf_op jit(solution)/shard_map/ppermute | solution.py:23
  2.4 0.6 slice.221
  3.6 0.1 reverse.1
  3.7 0.1 slice.467
  3.8 0.6 reshape.57
  4.3 0.1 concatenate.20
  4.4 0.1 dynamic_slice.13
  4.6 0.3 tile.30
  4.9 0.2 slice.278
  5.1 0.4 reshape.58
  5.6 0.9 %copy-done = f32[16,6144]{1,0:T(8,128)S(1)} copy-done((f32[16,6144]{1,0:T(8,128)S(1)}, f32[16,6144]{1,0:T(8,128)}, u32[]{:S(2)}) %copy-start) | copy-done | bytes 393240
  6.5 1.4 %fusion.5 = (f32[22,6150]{1,0:T(8,128)S(1)}, f32[22,6150]{1,0:T(8,128)S(1)}, f32[22,6150]{1,0:T(8,128)S(1)}, f32[22,6150]{1,0:T(8,128)S(1)}) fusion(f32[16,6144]{1,0:T(8,128)S(1)} %copy-done, f32[3,6144]{1,0:T(4,128)S(1)} %get-tuple-element.17, f32[3,6144]{1,0:T(4,128)S(1)} %get-tuple-element.16), kind=kLoop, calls=%fused_computation.16 | loop fusion | flops 1894200 | bytes 2705472 | tf_op jit(solution)/shard_map/add | solution.py:43
  7.8 2.2 %fusion.11 = f32[22,6144]{1,0:T(8,128)S(1)} fusion(f32[16,6144]{1,0:T(8,128)S(1)} %copy-done, f32[22,6150]{1,0:T(8,128)S(1)} %get-tuple-element.7, f32[22,6150]{1,0:T(8,128)S(1)} %get-tuple-element.8, f32[22,6150]{1,0:T(8,128)S(1)} %get-tuple-element.9, s32[22,6164]{1,0:T(8,128)S(1)} %reshape.58, pred[22]{0:T(512)(128)(4,1)S(1)} %compare_and_fusion), kind=kLoop, calls=%fused_computation.24 | loop fusion | flops 3649536 | bytes 9584662 | tf_op jit(solution)/shard_map/jit(_where)/select_n | solution.py:149
  10.0 0.2 pad.18
  10.3 0.3 reshape.59
  10.6 0.4 reshape.60
  11.1 0.2 slice_dynamic-update-slice_fusion
  11.4 0.1 reverse.2
  11.5 0.1 slice_add_fusion.30
  11.6 4.0 %collective-permute-start.2 = (f32[6144]{0:T(1024)S(1)}, f32[6144]{0:T(1024)S(1)}, u32[]{:S(2)}, u32[]{:S(2)}) collective-permute-start(f32[6144]{0:T(1024)S(1)} %slice_add_fusion.30), channel_id=1, source_target_pairs={{0,1},{1,0},{2,3},{3,2},{4,5},{5,4},{6,7},{7,6},{8,9},{9,8},{10,11... | collective-permute-start | bytes 73736 | tf_op jit(solution)/shard_map/ppermute | solution.py:120
  15.6 0.8 %collective-permute-done.2 = f32[6144]{0:T(1024)S(1)} collective-permute-done((f32[6144]{0:T(1024)S(1)}, f32[6144]{0:T(1024)S(1)}, u32[]{:S(2)}, u32[]{:S(2)}) %collective-permute-start.2) | collective-permute-done | bytes 24608 | tf_op jit(solution)/shard_map/ppermute | solution.py:120
  16.4 1.5 %collective-permute-start.3 = (f32[6144]{0:T(1024)S(1)}, f32[6144]{0:T(1024)S(1)}, u32[]{:S(2)}, u32[]{:S(2)}) collective-permute-start(f32[6144]{0:T(1024)S(1)} %add.261), channel_id=1, source_target_pairs={{0,2},{1,3},{2,0},{3,1},{4,6},{5,7},{6,4},{7,5},{8,10},{9,11},{10,... | collective-permute-start | bytes 73736 | tf_op jit(solution)/shard_map/ppermute | solution.py:120
  17.9 0.1 fusion.30
  18.1 0.2 tile.13
  18.3 0.2 slice.254
  18.5 0.3 reshape.56
  18.8 3.0 %scatter_custom_fusion = f32[6144]{0:T(1024)S(1)} fusion(s32[384]{0:T(512)S(1)} %compare_select_fusion, f32[384]{0:T(512)S(1)} %broadcast.70, f32[]{:T(128)} %constant.90.clone.1), kind=kCustom, calls=%fused_computation.92 | custom fusion | bytes 24580 | tf_op jit(solution)/shard_map/scatter | solution.py:158
  21.8 0.1 dynamic_slice.15
  21.8 1.6 %collective-permute-start.4 = (f32[6144]{0:T(1024)S(1)}, f32[6144]{0:T(1024)S(1)}, u32[]{:S(2)}, u32[]{:S(2)}) collective-permute-start(f32[6144]{0:T(1024)S(1)} %add.262), channel_id=1, source_target_pairs={{0,4},{1,5},{2,6},{3,7},{4,0},{5,1},{6,2},{7,3},{8,12},{9,13},{10,... | collective-permute-start | bytes 73736 | tf_op jit(solution)/shard_map/ppermute | solution.py:120
  23.5 0.2 slice_add_fusion.12
  23.7 2.0 %collective-permute-done.4 = f32[6144]{0:T(1024)S(1)} collective-permute-done((f32[6144]{0:T(1024)S(1)}, f32[6144]{0:T(1024)S(1)}, u32[]{:S(2)}, u32[]{:S(2)}) %collective-permute-start.4) | collective-permute-done | bytes 24608 | tf_op jit(solution)/shard_map/ppermute | solution.py:120
  25.7 2.6 %collective-permute-start.5 = (f32[6144]{0:T(1024)S(1)}, f32[6144]{0:T(1024)S(1)}, u32[]{:S(2)}, u32[]{:S(2)}) collective-permute-start(f32[6144]{0:T(1024)S(1)} %add.263), channel_id=1, source_target_pairs={{0,8},{1,9},{2,10},{3,11},{4,12},{5,13},{6,14},{7,15},{8,0},{9,1},... | collective-permute-start | bytes 73736 | tf_op jit(solution)/shard_map/ppermute | solution.py:120
  28.3 1.5 %fusion.20 = f32[16,6144]{1,0:T(8,128)S(1)} fusion(f32[16,6150]{1,0:T(8,128)S(1)} %get-tuple-element.10, f32[16,6150]{1,0:T(8,128)S(1)} %get-tuple-element.11, f32[16,6150]{1,0:T(8,128)S(1)} %get-tuple-element.12, f32[16,6144]{1,0:T(8,128)S(1)} %copy-done, s32[16,6158]{1,0:T(8,128)S(1)} %reshape.56), kind=kLoop, calls=%fused_computation.53 | loop fusion | flops 2555904 | bytes 7077888 | tf_op jit(solution)/shard_map/add | solution.py:54
  29.8 0.6 %collective-permute-done.5 = f32[6144]{0:T(1024)S(1)} collective-permute-done((f32[6144]{0:T(1024)S(1)}, f32[6144]{0:T(1024)S(1)}, u32[]{:S(2)}, u32[]{:S(2)}) %collective-permute-start.5) | collective-permute-done | bytes 24608 | tf_op jit(solution)/shard_map/ppermute | solution.py:120
  30.6 0.1 reverse.3
  30.7 0.1 fusion.29
  30.9 0.2 tile.32
  31.1 0.2 slice.299
  31.3 0.3 reshape.61
  31.6 0.2 multiply_reduce_fusion.1
  31.8 0.3 multiply_reduce_fusion
  32.0 0.1 multiply_convert_fusion
  32.2 14.0 %all_to_all.25 = bf16[16,16,384]{2,0,1:T(8,128)(2,1)S(1)} all-to-all(bf16[16,16,384]{2,0,1:T(8,128)(2,1)S(1)} %bitcast.21), channel_id=1, replica_groups=mesh['groups'=2,'blk'=16] {'blk'}, dimensions={1} | all-to-all | bytes 393216 | tf_op jit(solution)/shard_map/all_to_all | solution.py:128
  46.3 0.3 fusion.27
  46.5 12.6 %all_to_all.26 = f32[16,16,256]{2,1,0:T(8,128)S(1)} all-to-all(f32[16,16,256]{2,1,0:T(8,128)S(1)} %fusion.27), channel_id=1, replica_groups=mesh['groups'=2,'blk'=16] {'blk'}, dimensions={0} | all-to-all | bytes 524288 | tf_op jit(solution)/shard_map/all_to_all | solution.py:130
  59.2 0.6 %broadcast_multiply_fusion = f32[16,256]{1,0:T(8,128)} fusion(f32[16,256]{1,0:T(8,128)S(1)} %reduce_sum.39), kind=kLoop, calls=%fused_computation.94 | loop fusion | flops 4096 | bytes 32768 | tf_op jit(solution)/shard_map/div | solution.py:162
  (31 shorter events, 0.8 us)
Async XLA Ops:
  0.0 2.3 %copy-start.1 = (s32[6144]{0:T(1024)S(1)}, s32[6144]{0:T(1024)}, u32[]{:S(2)}) copy-start(s32[6144]{0:T(1024)} %param.5) | copy-start | bytes 73732
  1.1 4.4 %collective-permute-start = (f32[3,6144]{1,0:T(4,128)S(1)}, f32[3,6144]{1,0:T(4,128)S(1)}, u32[]{:S(2)}, u32[]{:S(2)}) collective-permute-start(f32[3,6144]{1,0:T(4,128)S(1)} %get-tuple-element.14), channel_id=1, source_target_pairs={{0,1},{1,0},{2,3},{3,2},{4,5},{5,4},{6,7},{7,6},{8,9},{9,8},{10,11... | collective-permute-start | bytes 221192 | tf_op jit(solution)/shard_map/ppermute | solution.py:20
  1.6 3.9 %collective-permute-start.1 = (f32[3,6144]{1,0:T(4,128)S(1)}, f32[3,6144]{1,0:T(4,128)S(1)}, u32[]{:S(2)}, u32[]{:S(2)}) collective-permute-start(f32[3,6144]{1,0:T(4,128)S(1)} %get-tuple-element.15), channel_id=1, source_target_pairs={{2,1},{4,3},{6,5},{8,7},{10,9},{12,11},{14,13},{1,2},{3,4},{5,6},{... | collective-permute-start | bytes 221192 | tf_op jit(solution)/shard_map/ppermute | solution.py:23
  5.5 1.0 %copy-start = (f32[16,6144]{1,0:T(8,128)S(1)}, f32[16,6144]{1,0:T(8,128)}, u32[]{:S(2)}) copy-start(f32[16,6144]{1,0:T(8,128)} %param.4) | copy-start | bytes 1179652
  11.5 4.0 %copy-start.2 = (s32[384]{0:T(512)S(1)}, s32[384]{0:T(512)}, u32[]{:S(2)}) copy-start(s32[384]{0:T(512)} %param.6) | copy-start | bytes 4612
  11.6 4.8 %collective-permute-start.2 = (f32[6144]{0:T(1024)S(1)}, f32[6144]{0:T(1024)S(1)}, u32[]{:S(2)}, u32[]{:S(2)}) collective-permute-start(f32[6144]{0:T(1024)S(1)} %slice_add_fusion.30), channel_id=1, source_target_pairs={{0,1},{1,0},{2,3},{3,2},{4,5},{5,4},{6,7},{7,6},{8,9},{9,8},{10,11... | collective-permute-start | bytes 73736 | tf_op jit(solution)/shard_map/ppermute | solution.py:120
  16.4 5.4 %collective-permute-start.3 = (f32[6144]{0:T(1024)S(1)}, f32[6144]{0:T(1024)S(1)}, u32[]{:S(2)}, u32[]{:S(2)}) collective-permute-start(f32[6144]{0:T(1024)S(1)} %add.261), channel_id=1, source_target_pairs={{0,2},{1,3},{2,0},{3,1},{4,6},{5,7},{6,4},{7,5},{8,10},{9,11},{10,... | collective-permute-start | bytes 73736 | tf_op jit(solution)/shard_map/ppermute | solution.py:120
  21.8 3.9 %collective-permute-start.4 = (f32[6144]{0:T(1024)S(1)}, f32[6144]{0:T(1024)S(1)}, u32[]{:S(2)}, u32[]{:S(2)}) collective-permute-start(f32[6144]{0:T(1024)S(1)} %add.262), channel_id=1, source_target_pairs={{0,4},{1,5},{2,6},{3,7},{4,0},{5,1},{6,2},{7,3},{8,12},{9,13},{10,... | collective-permute-start | bytes 73736 | tf_op jit(solution)/shard_map/ppermute | solution.py:120
  25.7 4.7 %collective-permute-start.5 = (f32[6144]{0:T(1024)S(1)}, f32[6144]{0:T(1024)S(1)}, u32[]{:S(2)}, u32[]{:S(2)}) collective-permute-start(f32[6144]{0:T(1024)S(1)} %add.263), channel_id=1, source_target_pairs={{0,8},{1,9},{2,10},{3,11},{4,12},{5,13},{6,14},{7,15},{8,0},{9,1},... | collective-permute-start | bytes 73736 | tf_op jit(solution)/shard_map/ppermute | solution.py:120

commit v13 on v10

--- a/solution.py
+++ b/solution.py
@@ -136,9 +136,11 @@
     window_first = col_count - 1 - (first_bin + first_row + rows_here - 1)
     radius_map = skewed_map(widths, window_first, rows_here, col_count)
     own = lax.optimization_barrier(jnp.pad(contacts, WMAX))
-    halo = with_halo(contacts, (("blk", 0),), WMAX)
-    padded = lax.dynamic_update_slice(own, halo[:WMAX], (0, WMAX))
-    padded = lax.dynamic_update_slice(padded, halo[-WMAX:], (rows_here + WMAX, WMAX))
+    halo = with_halo(own[WMAX:-WMAX, WMAX:-WMAX], (("blk", 0),), WMAX)
+    top = jnp.pad(halo[:WMAX], ((0, rows_here + WMAX), (WMAX, WMAX)))
+    bottom = jnp.pad(halo[-WMAX:], ((rows_here + WMAX, 0), (WMAX, WMAX)))
+    row = lax.broadcasted_iota(jnp.int32, own.shape, 0)
+    padded = jnp.where(row < WMAX, top, jnp.where(row >= rows_here + WMAX, bottom, own))
     smoothed = smooth(padded, radius_map)
     local_total = diagonal_totals(smoothed, window_first)
     denominator = pair_counts(first_bin, nbins, col_count)

time: 60.8 us -> 56.5 us (0.929)
  local copies, waits for them, and re-layouts: 12 us -> 7.18 us
  starting transfers between devices: 12.5 us -> 14 us
  other arithmetic: 4.57 us -> 3.86 us
    ppermute x4, starting transfers between devices: 7.37 us -> 12.8 us  [tree_sum(): lax.ppermute(values, axis, [(i, i ^ step) for i in range(count)])]
    dynamic_update_slice x2 -> x0, local copies, waits for them, and re-layouts: 5.05 us -> none  [the longest x1 2.82 us: shards(): padded = lax.dynamic_update_slice(own, halo[:WMAX], (0, WMAX))]
    ppermute x1, starting transfers between devices: 4.42 us -> 0.56 us  [with_halo(): lax.ppermute(jnp.where(odd, head, tail), axis, [(i, i ^ 1) for i in range...]
    pad x1, local copies, waits for them, and re-layouts: 0.22 us -> 1.22 us  [shards(): own = lax.optimization_barrier(jnp.pad(contacts, WMAX))]
    unnamed x12 -> x10, local copies, waits for them, and re-layouts: 1.21 us -> 0.48 us
    select_n x2 -> x3, other arithmetic: 1.11 us -> 0.39 us  [the longest x1 0.18 us: shards(): jnp.where(row < WMAX, top, jnp.where(row >= rows_here + WMAX, bottom, own))]
where the time goes in v13:
time: 56.5 us; the launch traced here: 56.3 us
  blocking collectives  25.6 us (45%)
  starting transfers between devices  14 us (25%)
  local copies, waits for them, and re-layouts  7.18 us (13%)
  waiting for transfers between devices  4.47 us (8%)
  other arithmetic  3.86 us (7%)
  between operations  0.92 us (2%)
    all_to_all x1, blocking collectives, gram_rows(): columns = lax.all_to_all(zscores, axis, 1, 0, tiled=True)  13 us
    ppermute x4, starting transfers between devices, tree_sum(): lax.ppermute(values, axis, [(i, i ^ step) for i in range(count)])  12.8 us
    all_to_all x1, blocking collectives, gram_rows(): pieces = lax.all_to_all(partial, axis, 0, 0, tiled=True)  12.6 us
    ppermute x4, waiting for transfers between devices, tree_sum(): lax.ppermute(values, axis, [(i, i ^ step) for i in range(count)])  4.46 us
    scatter x1, local copies, waits for them, and re-layouts, shards(): kept_bins = jnp.ones((col_count,), jnp.float32).at[masked_bins].set(0.0)  2.95 us
    add x1, other arithmetic, smooth(): smoothed + jnp.where(radius_map == radius, box_sums / float((2 * radius +...  1.59 us
    pad x1, local copies, waits for them, and re-layouts, shards(): own = lax.optimization_barrier(jnp.pad(contacts, WMAX))  1.22 us
  transfers between devices with their start and end apart: 6, of which 3 were waited for; matrix products, arithmetic and copies ran while one was open for 7% of the time, Pallas kernels for 0%

profile of v13, /device:TPU:0, one launch (start us, length us, event | category | flops | bytes accessed | tf_op | source)
XLA Modules:
  0.0 56.3 jit_solution(11138832630922773686)
XLA Ops:
  0.0 1.2 %pad.20 = f32[22,6150]{1,0:T(8,128)S(1)} pad(f32[16,6144]{1,0:T(8,128)} %param.4, f32[]{:T(128)} %constant.29.clone.1), padding=3_3x3_3 | pad | bytes 934420 | tf_op jit(solution)/shard_map/jit(_pad)/pad | solution.py:138
  1.2 0.2 slice_select_fusion.2
  1.4 0.6 collective-permute-start
  2.0 0.7 %collective-permute-start.1 = (f32[3,6144]{1,0:T(4,128)S(1)}, f32[3,6144]{1,0:T(4,128)S(1)}, u32[]{:S(2)}, u32[]{:S(2)}) collective-permute-start(f32[3,6144]{1,0:T(4,128)S(1)} %get-tuple-element.11), channel_id=1, source_target_pairs={{2,1},{4,3},{6,5},{8,7},{10,9},{12,11},{14,13},{1,2},{3,4},{5,6},{... | collective-permute-start | bytes 221192 | tf_op jit(solution)/shard_map/ppermute | solution.py:23
  3.3 0.1 slice.106
  3.4 0.1 reverse
  3.5 0.1 slice.252
  3.5 0.1 fusion.12
  3.7 0.2 tile.9
  3.9 0.2 slice.140
  4.1 0.3 reshape.37
  4.4 0.0 collective-permute-done
  4.4 0.0 collective-permute-done.1
  4.4 0.2 select_select_fusion
  4.6 0.2 slice_add_fusion
  4.9 1.6 %fusion.2 = f32[16,6144]{1,0:T(8,128)S(1)} fusion(f32[16,6150]{1,0:T(8,128)S(1)} %get-tuple-element.7, f32[16,6150]{1,0:T(8,128)S(1)} %get-tuple-element.8, f32[16,6150]{1,0:T(8,128)S(1)} %get-tuple-element.9, f32[22,6150]{1,0:T(8,128)S(1)} %select_select_fusion, s32[16,6158]{1,0:T(8,128)S(1)} %reshape.37), kind=kLoop, calls=%fused_computation.12 | loop fusion | flops 2555904 | bytes 7077888 | tf_op jit(solution)/shard_map/add | solution.py:54
  6.5 0.2 pad.23
  6.6 0.2 reshape.38
  6.9 0.2 reshape.39
  7.2 0.1 reduce_sum.36
  7.2 0.2 slice_dynamic-update-slice_fusion
  7.5 0.1 reverse.1
  7.5 0.1 slice.253
  7.6 0.1 slice_add_fusion.18
  7.7 4.5 %collective-permute-start.2 = (f32[6144]{0:T(1024)S(1)}, f32[6144]{0:T(1024)S(1)}, u32[]{:S(2)}, u32[]{:S(2)}) collective-permute-start(f32[6144]{0:T(1024)S(1)} %slice_add_fusion.18), channel_id=1, source_target_pairs={{0,1},{1,0},{2,3},{3,2},{4,5},{5,4},{6,7},{7,6},{8,9},{9,8},{10,11... | collective-permute-start | bytes 73736 | tf_op jit(solution)/shard_map/ppermute | solution.py:114
  12.2 0.8 %collective-permute-done.2 = f32[6144]{0:T(1024)S(1)} collective-permute-done((f32[6144]{0:T(1024)S(1)}, f32[6144]{0:T(1024)S(1)}, u32[]{:S(2)}, u32[]{:S(2)}) %collective-permute-start.2) | collective-permute-done | bytes 24608 | tf_op jit(solution)/shard_map/ppermute | solution.py:114
  13.0 3.0 %collective-permute-start.3 = (f32[6144]{0:T(1024)S(1)}, f32[6144]{0:T(1024)S(1)}, u32[]{:S(2)}, u32[]{:S(2)}) collective-permute-start(f32[6144]{0:T(1024)S(1)} %add.154), channel_id=1, source_target_pairs={{0,2},{1,3},{2,0},{3,1},{4,6},{5,7},{6,4},{7,5},{8,10},{9,11},{10,... | collective-permute-start | bytes 73736 | tf_op jit(solution)/shard_map/ppermute | solution.py:114
  16.0 1.8 %collective-permute-done.3 = f32[6144]{0:T(1024)S(1)} collective-permute-done((f32[6144]{0:T(1024)S(1)}, f32[6144]{0:T(1024)S(1)}, u32[]{:S(2)}, u32[]{:S(2)}) %collective-permute-start.3) | collective-permute-done | bytes 24608 | tf_op jit(solution)/shard_map/ppermute | solution.py:114
  17.8 2.3 %collective-permute-start.4 = (f32[6144]{0:T(1024)S(1)}, f32[6144]{0:T(1024)S(1)}, u32[]{:S(2)}, u32[]{:S(2)}) collective-permute-start(f32[6144]{0:T(1024)S(1)} %add.155), channel_id=1, source_target_pairs={{0,4},{1,5},{2,6},{3,7},{4,0},{5,1},{6,2},{7,3},{8,12},{9,13},{10,... | collective-permute-start | bytes 73736 | tf_op jit(solution)/shard_map/ppermute | solution.py:114
  20.1 1.8 %collective-permute-done.4 = f32[6144]{0:T(1024)S(1)} collective-permute-done((f32[6144]{0:T(1024)S(1)}, f32[6144]{0:T(1024)S(1)}, u32[]{:S(2)}, u32[]{:S(2)}) %collective-permute-start.4) | collective-permute-done | bytes 24608 | tf_op jit(solution)/shard_map/ppermute | solution.py:114
  21.9 3.0 %collective-permute-start.5 = (f32[6144]{0:T(1024)S(1)}, f32[6144]{0:T(1024)S(1)}, u32[]{:S(2)}, u32[]{:S(2)}) collective-permute-start(f32[6144]{0:T(1024)S(1)} %add.156), channel_id=1, source_target_pairs={{0,8},{1,9},{2,10},{3,11},{4,12},{5,13},{6,14},{7,15},{8,0},{9,1},... | collective-permute-start | bytes 73736 | tf_op jit(solution)/shard_map/ppermute | solution.py:114
  25.0 2.9 %scatter_custom_fusion = f32[6144]{0:T(1024)S(1)} fusion(s32[384]{0:T(512)S(1)} %compare_select_fusion, f32[384]{0:T(512)S(1)} %broadcast.48, f32[]{:T(128)} %constant.70.clone.1), kind=kCustom, calls=%fused_computation.52 | custom fusion | bytes 24580 | tf_op jit(solution)/shard_map/scatter | solution.py:149
  27.9 0.1 dynamic_slice.11
  28.0 0.0 collective-permute-done.5
  28.1 0.1 slice.170
  28.1 0.1 reverse.2
  28.2 0.1 slice.254
  28.3 0.1 fusion.11
  28.5 0.2 tile.21
  28.7 0.2 slice.171
  28.9 0.3 reshape.40
  29.1 0.2 multiply_reduce_fusion.1
  29.3 0.3 multiply_reduce_fusion
  29.6 0.1 multiply_convert_fusion
  29.8 13.0 %all_to_all.25 = bf16[16,16,384]{2,0,1:T(8,128)(2,1)S(1)} all-to-all(bf16[16,16,384]{2,0,1:T(8,128)(2,1)S(1)} %bitcast.21), channel_id=1, replica_groups=mesh['groups'=2,'blk'=16] {'blk'}, dimensions={1} | all-to-all | bytes 393216 | tf_op jit(solution)/shard_map/all_to_all | solution.py:122
  42.8 0.2 fusion.9
  43.0 12.6 %all_to_all.26 = f32[16,16,256]{2,1,0:T(8,128)S(1)} all-to-all(f32[16,16,256]{2,1,0:T(8,128)S(1)} %fusion.9), channel_id=1, replica_groups=mesh['groups'=2,'blk'=16] {'blk'}, dimensions={0} | all-to-all | bytes 524288 | tf_op jit(solution)/shard_map/all_to_all | solution.py:124
  55.7 0.6 %broadcast_multiply_fusion = f32[16,256]{1,0:T(8,128)} fusion(f32[16,256]{1,0:T(8,128)S(1)} %reduce_sum.39), kind=kLoop, calls=%fused_computation.54 | loop fusion | flops 4096 | bytes 32768 | tf_op jit(solution)/shard_map/div | solution.py:153
  (21 shorter events, 0.3 us)
Async XLA Ops:
  1.2 2.1 %copy-start = (s32[6144]{0:T(1024)S(1)}, s32[6144]{0:T(1024)}, u32[]{:S(2)}) copy-start(s32[6144]{0:T(1024)} %param.5) | copy-start | bytes 73732
  1.4 3.0 %collective-permute-start = (f32[3,6144]{1,0:T(4,128)S(1)}, f32[3,6144]{1,0:T(4,128)S(1)}, u32[]{:S(2)}, u32[]{:S(2)}) collective-permute-start(f32[3,6144]{1,0:T(4,128)S(1)} %get-tuple-element.10), channel_id=1, source_target_pairs={{0,1},{1,0},{2,3},{3,2},{4,5},{5,4},{6,7},{7,6},{8,9},{9,8},{10,11... | collective-permute-start | bytes 221192 | tf_op jit(solution)/shard_map/ppermute | solution.py:20
  2.0 2.4 %collective-permute-start.1 = (f32[3,6144]{1,0:T(4,128)S(1)}, f32[3,6144]{1,0:T(4,128)S(1)}, u32[]{:S(2)}, u32[]{:S(2)}) collective-permute-start(f32[3,6144]{1,0:T(4,128)S(1)} %get-tuple-element.11), channel_id=1, source_target_pairs={{2,1},{4,3},{6,5},{8,7},{10,9},{12,11},{14,13},{1,2},{3,4},{5,6},{... | collective-permute-start | bytes 221192 | tf_op jit(solution)/shard_map/ppermute | solution.py:23
  7.7 5.3 %collective-permute-start.2 = (f32[6144]{0:T(1024)S(1)}, f32[6144]{0:T(1024)S(1)}, u32[]{:S(2)}, u32[]{:S(2)}) collective-permute-start(f32[6144]{0:T(1024)S(1)} %slice_add_fusion.18), channel_id=1, source_target_pairs={{0,1},{1,0},{2,3},{3,2},{4,5},{5,4},{6,7},{7,6},{8,9},{9,8},{10,11... | collective-permute-start | bytes 73736 | tf_op jit(solution)/shard_map/ppermute | solution.py:114
  13.0 4.8 %collective-permute-start.3 = (f32[6144]{0:T(1024)S(1)}, f32[6144]{0:T(1024)S(1)}, u32[]{:S(2)}, u32[]{:S(2)}) collective-permute-start(f32[6144]{0:T(1024)S(1)} %add.154), channel_id=1, source_target_pairs={{0,2},{1,3},{2,0},{3,1},{4,6},{5,7},{6,4},{7,5},{8,10},{9,11},{10,... | collective-permute-start | bytes 73736 | tf_op jit(solution)/shard_map/ppermute | solution.py:114
  17.8 7.1 %copy-start.1 = (s32[384]{0:T(512)S(1)}, s32[384]{0:T(512)}, u32[]{:S(2)}) copy-start(s32[384]{0:T(512)} %param.6) | copy-start | bytes 4612
  17.8 4.1 %collective-permute-start.4 = (f32[6144]{0:T(1024)S(1)}, f32[6144]{0:T(1024)S(1)}, u32[]{:S(2)}, u32[]{:S(2)}) collective-permute-start(f32[6144]{0:T(1024)S(1)} %add.155), channel_id=1, source_target_pairs={{0,4},{1,5},{2,6},{3,7},{4,0},{5,1},{6,2},{7,3},{8,12},{9,13},{10,... | collective-permute-start | bytes 73736 | tf_op jit(solution)/shard_map/ppermute | solution.py:114
  21.9 6.1 %collective-permute-start.5 = (f32[6144]{0:T(1024)S(1)}, f32[6144]{0:T(1024)S(1)}, u32[]{:S(2)}, u32[]{:S(2)}) collective-permute-start(f32[6144]{0:T(1024)S(1)} %add.156), channel_id=1, source_target_pairs={{0,8},{1,9},{2,10},{3,11},{4,12},{5,13},{6,14},{7,15},{8,0},{9,1},... | collective-permute-start | bytes 73736 | tf_op jit(solution)/shard_map/ppermute | solution.py:114

commit v14 on v13

--- a/solution.py
+++ b/solution.py
@@ -116,11 +116,11 @@
     return values
 
 
-def gram_rows(zscores, axis):
+def gram_rows(zscores, axis, scale):
     blocks = lax.axis_size(axis)
     rows_here = zscores.shape[0]
     columns = lax.all_to_all(zscores, axis, 1, 0, tiled=True)
-    partial = cross_block(columns, columns)
+    partial = cross_block(columns, columns) / scale
     pieces = lax.all_to_all(partial, axis, 0, 0, tiled=True)
     return jnp.sum(pieces.reshape(blocks, rows_here, pieces.shape[1]), axis=0)
 
@@ -146,11 +146,12 @@
     denominator = pair_counts(first_bin, nbins, col_count)
     expected = tree_sum(local_total, "blk") / denominator
     expected_map = skewed_map(expected, window_first, rows_here, col_count)
-    kept_bins = jnp.ones((col_count,), jnp.float32).at[masked_bins].set(0.0)
+    hit = masked_bins[:, None] == jnp.arange(col_count, dtype=masked_bins.dtype)[None, :]
+    kept_bins = jnp.where(jnp.any(hit, axis=0), 0.0, 1.0).astype(jnp.float32)
     kept_rows = lax.dynamic_slice_in_dim(kept_bins, first_bin + first_row, rows_here)
     kept_total = jnp.float32(col_count - masked_bins.shape[0])
     zscores = normalize(smoothed, expected_map, kept_rows, kept_bins, kept_total)
-    return gram_rows(zscores, "blk") / kept_total
+    return gram_rows(zscores, "blk", kept_total)
 
 
 def solution(mesh):

time: 56.5 us -> 56.4 us (level)
  local copies, waits for them, and re-layouts: 7.18 us -> 4.24 us
  other arithmetic: 3.86 us -> 5.21 us
  blocking collectives: 25.6 us -> 26.8 us
    scatter x1 -> x0, local copies, waits for them, and re-layouts: 2.95 us -> none  [shards(): kept_bins = jnp.ones((col_count,), jnp.float32).at[masked_bins].set(0.0)]
    reduce_or x0 -> x1, other arithmetic: none -> 1.35 us  [shards(): kept_bins = jnp.where(jnp.any(hit, axis=0), 0.0, 1.0).astype(jnp.float32)]
    all_to_all x1, blocking collectives: 13 us -> 14.2 us  [gram_rows(): columns = lax.all_to_all(zscores, axis, 1, 0, tiled=True)]
    div x1 -> x0, other arithmetic: 0.61 us -> none  [shards(): return gram_rows(zscores, 'blk') / kept_total]
    reduce_sum x1, other arithmetic: 0.02 us -> 0.63 us  [gram_rows(): return jnp.sum(pieces.reshape(blocks, rows_here, pieces.shape[1]), axis=0)]
  transfers between devices with their start and end apart: 6 -> 6, of which waited for: 3 -> 4; matrix products, arithmetic and copies ran while one was open for 7% -> 4% of each run, Pallas kernels for 0% -> 0%
where the time goes in v14:
time: 56.4 us; the launch traced here: 56.2 us
  blocking collectives  26.8 us (48%)
  starting transfers between devices  13.9 us (25%)
  other arithmetic  5.21 us (9%)
  waiting for transfers between devices  4.83 us (9%)
  local copies, waits for them, and re-layouts  4.24 us (8%)
  between operations  0.91 us (2%)
    all_to_all x1, blocking collectives, gram_rows(): columns = lax.all_to_all(zscores, axis, 1, 0, tiled=True)  14.2 us
    ppermute x4, starting transfers between devices, tree_sum(): lax.ppermute(values, axis, [(i, i ^ step) for i in range(count)])  12.7 us
    all_to_all x1, blocking collectives, gram_rows(): pieces = lax.all_to_all(partial, axis, 0, 0, tiled=True)  12.6 us
    ppermute x4, waiting for transfers between devices, tree_sum(): lax.ppermute(values, axis, [(i, i ^ step) for i in range(count)])  4.82 us
    add x1, other arithmetic, smooth(): smoothed + jnp.where(radius_map == radius, box_sums / float((2 * radius +...  1.59 us
    reduce_or x1, other arithmetic, shards(): kept_bins = jnp.where(jnp.any(hit, axis=0), 0.0, 1.0).astype(jnp.float32)  1.35 us
    pad x1, local copies, waits for them, and re-layouts, shards(): own = lax.optimization_barrier(jnp.pad(contacts, WMAX))  1.23 us
  transfers between devices with their start and end apart: 6, of which 4 were waited for; matrix products, arithmetic and copies ran while one was open for 4% of the time, Pallas kernels for 0%

profile of v14, /device:TPU:0, one launch (start us, length us, event | category | flops | bytes accessed | tf_op | source)
XLA Modules:
  0.0 56.2 jit_solution(9712493027896543380)
XLA Ops:
  0.0 1.2 %pad.20 = f32[22,6150]{1,0:T(8,128)S(1)} pad(f32[16,6144]{1,0:T(8,128)} %param.4, f32[]{:T(128)} %constant.30.clone.1), padding=3_3x3_3 | pad | bytes 934420 | tf_op jit(solution)/shard_map/jit(_pad)/pad | solution.py:138
  1.2 0.2 slice_select_fusion.2
  1.4 0.6 collective-permute-start
  2.0 0.7 %collective-permute-start.1 = (f32[3,6144]{1,0:T(4,128)S(1)}, f32[3,6144]{1,0:T(4,128)S(1)}, u32[]{:S(2)}, u32[]{:S(2)}) collective-permute-start(f32[3,6144]{1,0:T(4,128)S(1)} %get-tuple-element.11), channel_id=1, source_target_pairs={{2,1},{4,3},{6,5},{8,7},{10,9},{12,11},{14,13},{1,2},{3,4},{5,6},{... | collective-permute-start | bytes 221192 | tf_op jit(solution)/shard_map/ppermute | solution.py:23
  3.3 0.1 slice.106
  3.4 0.1 reverse
  3.5 0.1 slice.252
  3.5 0.1 fusion.11
  3.7 0.2 tile.9
  3.9 0.2 slice.140
  4.1 0.3 reshape.38
  4.4 0.0 collective-permute-done.1
  4.4 0.2 select_select_fusion
  4.6 0.2 slice_add_fusion
  4.9 1.6 %fusion.3 = f32[16,6144]{1,0:T(8,128)S(1)} fusion(f32[16,6150]{1,0:T(8,128)S(1)} %get-tuple-element.7, f32[16,6150]{1,0:T(8,128)S(1)} %get-tuple-element.8, f32[16,6150]{1,0:T(8,128)S(1)} %get-tuple-element.9, f32[22,6150]{1,0:T(8,128)S(1)} %select_select_fusion, s32[16,6158]{1,0:T(8,128)S(1)} %reshape.38), kind=kLoop, calls=%fused_computation.14 | loop fusion | flops 2555904 | bytes 7077888 | tf_op jit(solution)/shard_map/add | solution.py:54
  6.5 0.2 pad.23
  6.6 0.2 reshape.39
  6.9 0.2 reshape.40
  7.2 0.0 copy-start.1
  7.2 0.1 reduce_sum.36
  7.2 0.2 slice_dynamic-update-slice_fusion
  7.5 0.1 reverse.1
  7.6 0.1 slice.253
  7.6 0.1 slice_add_fusion.18
  7.7 4.5 %collective-permute-start.2 = (f32[6144]{0:T(1024)S(1)}, f32[6144]{0:T(1024)S(1)}, u32[]{:S(2)}, u32[]{:S(2)}) collective-permute-start(f32[6144]{0:T(1024)S(1)} %slice_add_fusion.18), channel_id=1, source_target_pairs={{0,1},{1,0},{2,3},{3,2},{4,5},{5,4},{6,7},{7,6},{8,9},{9,8},{10,11... | collective-permute-start | bytes 73736 | tf_op jit(solution)/shard_map/ppermute | solution.py:114
  12.2 0.8 %collective-permute-done.2 = f32[6144]{0:T(1024)S(1)} collective-permute-done((f32[6144]{0:T(1024)S(1)}, f32[6144]{0:T(1024)S(1)}, u32[]{:S(2)}, u32[]{:S(2)}) %collective-permute-start.2) | collective-permute-done | bytes 24608 | tf_op jit(solution)/shard_map/ppermute | solution.py:114
  13.0 3.0 %collective-permute-start.3 = (f32[6144]{0:T(1024)S(1)}, f32[6144]{0:T(1024)S(1)}, u32[]{:S(2)}, u32[]{:S(2)}) collective-permute-start(f32[6144]{0:T(1024)S(1)} %add.148), channel_id=1, source_target_pairs={{0,2},{1,3},{2,0},{3,1},{4,6},{5,7},{6,4},{7,5},{8,10},{9,11},{10,... | collective-permute-start | bytes 73736 | tf_op jit(solution)/shard_map/ppermute | solution.py:114
  16.0 1.8 %collective-permute-done.3 = f32[6144]{0:T(1024)S(1)} collective-permute-done((f32[6144]{0:T(1024)S(1)}, f32[6144]{0:T(1024)S(1)}, u32[]{:S(2)}, u32[]{:S(2)}) %collective-permute-start.3) | collective-permute-done | bytes 24608 | tf_op jit(solution)/shard_map/ppermute | solution.py:114
  17.9 2.2 %collective-permute-start.4 = (f32[6144]{0:T(1024)S(1)}, f32[6144]{0:T(1024)S(1)}, u32[]{:S(2)}, u32[]{:S(2)}) collective-permute-start(f32[6144]{0:T(1024)S(1)} %add.149), channel_id=1, source_target_pairs={{0,4},{1,5},{2,6},{3,7},{4,0},{5,1},{6,2},{7,3},{8,12},{9,13},{10,... | collective-permute-start | bytes 73736 | tf_op jit(solution)/shard_map/ppermute | solution.py:114
  20.1 1.4 %fusion = pred[6144]{0:T(1024)(128)(4,1)S(1)} fusion(s32[384]{0:T(512)S(1)} %copy-done.1), kind=kLoop, calls=%fused_computation.1 | loop fusion | flops 4712448 | bytes 7680 | tf_op jit(solution)/shard_map/reduce_or | solution.py:150
  21.4 0.4 collective-permute-done.4
  21.9 3.0 %collective-permute-start.5 = (f32[6144]{0:T(1024)S(1)}, f32[6144]{0:T(1024)S(1)}, u32[]{:S(2)}, u32[]{:S(2)}) collective-permute-start(f32[6144]{0:T(1024)S(1)} %add.150), channel_id=1, source_target_pairs={{0,8},{1,9},{2,10},{3,11},{4,12},{5,13},{6,14},{7,15},{8,0},{9,1},... | collective-permute-start | bytes 73736 | tf_op jit(solution)/shard_map/ppermute | solution.py:114
  24.9 0.1 dynamic_slice.11
  25.0 1.7 %collective-permute-done.5 = f32[6144]{0:T(1024)S(1)} collective-permute-done((f32[6144]{0:T(1024)S(1)}, f32[6144]{0:T(1024)S(1)}, u32[]{:S(2)}, u32[]{:S(2)}) %collective-permute-start.5) | collective-permute-done | bytes 24608 | tf_op jit(solution)/shard_map/ppermute | solution.py:114
  26.8 0.1 slice.170
  26.8 0.1 reverse.2
  26.9 0.1 slice.254
  27.0 0.1 fusion.10
  27.2 0.2 tile.21
  27.4 0.2 slice.171
  27.6 0.3 reshape.41
  27.8 0.2 multiply_reduce_fusion.1
  28.1 0.3 multiply_reduce_fusion
  28.3 0.1 multiply_convert_fusion
  28.5 14.2 %all_to_all.28 = bf16[16,16,384]{2,0,1:T(8,128)(2,1)S(1)} all-to-all(bf16[16,16,384]{2,0,1:T(8,128)(2,1)S(1)} %bitcast.19), channel_id=1, replica_groups=mesh['groups'=2,'blk'=16] {'blk'}, dimensions={1} | all-to-all | bytes 393216 | tf_op jit(solution)/shard_map/all_to_all | solution.py:122
  42.7 0.3 convolution_multiply_fusion
  43.0 12.6 %all_to_all.29 = f32[16,16,256]{2,1,0:T(8,128)S(1)} all-to-all(f32[16,16,256]{2,1,0:T(8,128)S(1)} %bitcast.18), channel_id=1, replica_groups=mesh['groups'=2,'blk'=16] {'blk'}, dimensions={0} | all-to-all | bytes 524288 | tf_op jit(solution)/shard_map/all_to_all | solution.py:124
  55.6 0.6 %reduce_sum.39 = f32[16,256]{1,0:T(8,128)} reduce(f32[16,16,256]{2,1,0:T(8,128)S(1)} %all_to_all.29, f32[]{:T(128)} %constant.30.clone.1), dimensions={0}, to_apply=%region_4.5 | reduce | flops 61440 | bytes 278532 | tf_op jit(solution)/shard_map/reduce_sum | solution.py:125
  (19 shorter events, 0.3 us)
Async XLA Ops:
  0.0 3.3 %copy-start = (s32[6144]{0:T(1024)S(1)}, s32[6144]{0:T(1024)}, u32[]{:S(2)}) copy-start(s32[6144]{0:T(1024)} %param.5) | copy-start | bytes 73732
  1.4 3.0 %collective-permute-start = (f32[3,6144]{1,0:T(4,128)S(1)}, f32[3,6144]{1,0:T(4,128)S(1)}, u32[]{:S(2)}, u32[]{:S(2)}) collective-permute-start(f32[3,6144]{1,0:T(4,128)S(1)} %get-tuple-element.10), channel_id=1, source_target_pairs={{0,1},{1,0},{2,3},{3,2},{4,5},{5,4},{6,7},{7,6},{8,9},{9,8},{10,11... | collective-permute-start | bytes 221192 | tf_op jit(solution)/shard_map/ppermute | solution.py:20
  2.0 2.4 %collective-permute-start.1 = (f32[3,6144]{1,0:T(4,128)S(1)}, f32[3,6144]{1,0:T(4,128)S(1)}, u32[]{:S(2)}, u32[]{:S(2)}) collective-permute-start(f32[3,6144]{1,0:T(4,128)S(1)} %get-tuple-element.11), channel_id=1, source_target_pairs={{2,1},{4,3},{6,5},{8,7},{10,9},{12,11},{14,13},{1,2},{3,4},{5,6},{... | collective-permute-start | bytes 221192 | tf_op jit(solution)/shard_map/ppermute | solution.py:23
  7.2 12.9 %copy-start.1 = (s32[384]{0:T(512)S(1)}, s32[384]{0:T(512)}, u32[]{:S(2)}) copy-start(s32[384]{0:T(512)} %param.6) | copy-start | bytes 4612
  7.7 5.3 %collective-permute-start.2 = (f32[6144]{0:T(1024)S(1)}, f32[6144]{0:T(1024)S(1)}, u32[]{:S(2)}, u32[]{:S(2)}) collective-permute-start(f32[6144]{0:T(1024)S(1)} %slice_add_fusion.18), channel_id=1, source_target_pairs={{0,1},{1,0},{2,3},{3,2},{4,5},{5,4},{6,7},{7,6},{8,9},{9,8},{10,11... | collective-permute-start | bytes 73736 | tf_op jit(solution)/shard_map/ppermute | solution.py:114
  13.0 4.8 %collective-permute-start.3 = (f32[6144]{0:T(1024)S(1)}, f32[6144]{0:T(1024)S(1)}, u32[]{:S(2)}, u32[]{:S(2)}) collective-permute-start(f32[6144]{0:T(1024)S(1)} %add.148), channel_id=1, source_target_pairs={{0,2},{1,3},{2,0},{3,1},{4,6},{5,7},{6,4},{7,5},{8,10},{9,11},{10,... | collective-permute-start | bytes 73736 | tf_op jit(solution)/shard_map/ppermute | solution.py:114
  17.9 4.0 %collective-permute-start.4 = (f32[6144]{0:T(1024)S(1)}, f32[6144]{0:T(1024)S(1)}, u32[]{:S(2)}, u32[]{:S(2)}) collective-permute-start(f32[6144]{0:T(1024)S(1)} %add.149), channel_id=1, source_target_pairs={{0,4},{1,5},{2,6},{3,7},{4,0},{5,1},{6,2},{7,3},{8,12},{9,13},{10,... | collective-permute-start | bytes 73736 | tf_op jit(solution)/shard_map/ppermute | solution.py:114
  21.9 4.8 %collective-permute-start.5 = (f32[6144]{0:T(1024)S(1)}, f32[6144]{0:T(1024)S(1)}, u32[]{:S(2)}, u32[]{:S(2)}) collective-permute-start(f32[6144]{0:T(1024)S(1)} %add.150), channel_id=1, source_target_pairs={{0,8},{1,9},{2,10},{3,11},{4,12},{5,13},{6,14},{7,15},{8,0},{9,1},... | collective-permute-start | bytes 73736 | tf_op jit(solution)/shard_map/ppermute | solution.py:114
